TPU v7x, 1024 devices: a whole 4x4x32 slice. The times are simulated.
1024 devices in a mesh: ctx: 64 (over z_lo, y, core), row: 4 (over x), col: 4 (over z_hi).
Axes of the slice: x: 4, y: 4, z: 32 (z_hi: 4, z_lo: 8; z = z_hi * 8 + z_lo), core: 2. Of those that a mesh axis runs over, the one named last changes fastest.
Arguments:
- tokens: bfloat16 [16384, 4096], P('ctx', 'col'), may hold values from -6 to 6
- w_xz: bfloat16 [4096, 80, 128], P('col', 'row'), may hold values from -0.09375 to 0.09375
- w_dt: bfloat16 [4096, 80], P('col', 'row'), may hold values from -0.1875 to 0.1875
- w_bc: bfloat16 [4096, 8, 256], P('col', 'row'), may hold values from -0.03125 to 0.03125
- conv_x: float32 [4, 80, 64], P(None, ('row', 'col')), may hold values from -3 to 3
- conv_x_bias: float32 [80, 64], P(('row', 'col')), may hold values from -1.5 to 1.5
- conv_bc: float32 [4, 8, 256], replicated, may hold values from -3 to 3
- conv_bc_bias: float32 [8, 256], replicated, may hold values from -1.5 to 1.5
- dt_bias: float32 [80], P(('row', 'col')), may hold values from -1 to 1
- a_log: float32 [80], P(('row', 'col')), as said below
- d_skip: float32 [80], P(('row', 'col')), may hold values from 0.5 to 1.5
- norm_gain: float32 [80, 64], P(('row', 'col')), may hold values from 0.5 to 1.5
- w_out: bfloat16 [80, 64, 4096], P(('row', 'col')), may hold values from -0.125 to 0.125
Outputs:
- mixed: float32 [16384, 4096], P('ctx', ('row', 'col'))
Inputs may be any that keep to these rules, and one draw needn't show every extreme that they name: `a_log`: one logarithm of a decay rate a head.
All inputs are finite; a program needn't handle non-finite values.
Results may differ from a plain program's by a relative error of at most 0.04.
Values may be sent and summed in bfloat16 or wider, within the bound.
No kernel may reach another device: no remote copies, remote signals or barrier semaphores. Data moves between devices by JAX's collectives and lax.ppermute only.
A program may use at most 64 MiB of HBM per device.

v0:
```python
import jax
import jax.numpy as jnp
from jax import lax
from jax.sharding import PartitionSpec as P

EPSILON = 1e-05


def shifted(block, axis, distance):
    devices = range(lax.axis_size(axis))
    route = [(i - distance, i) for i in devices if i - distance in devices]
    return lax.ppermute(block, axis, route)


def entering(array, axis, combine, identity):
    size, mine = (lax.axis_size(axis), lax.axis_index(axis))
    everything = jax.tree.map(lambda part: lax.all_gather(part, axis), array)
    start = jax.tree.map(
        lambda part, zero: jnp.broadcast_to(jnp.asarray(zero, part.dtype), part.shape),
        array,
        identity,
    )

    def hop(k, before):
        reached = k < mine
        new = combine(before, jax.tree.map(lambda part: part[k], everything))
        return jax.tree.map(lambda a, b: jnp.where(reached, a, b), new, before)

    return lax.fori_loop(0, size, hop, start)


def causal_conv(edge_rows, own_rows, weights, bias):
    width_k = weights.shape[0]
    count = own_rows.shape[0]
    joined = jnp.concatenate([edge_rows, own_rows], axis=0).astype(jnp.float32)
    total = bias + jnp.zeros(own_rows.shape, jnp.float32)
    for offset in range(width_k):
        total = total + weights[offset] * joined[offset : offset + count]
    return jax.nn.silu(total).astype(jnp.bfloat16)


def combine_states(earlier, later):
    return (earlier[0] * later[0], later[0][:, None, None] * earlier[1] + later[1])


def body(
    tokens,
    w_xz,
    w_dt,
    w_bc,
    conv_x,
    conv_x_bias,
    conv_bc,
    conv_bc_bias,
    dt_bias,
    a_log,
    d_skip,
    norm_gain,
    w_out,
):
    tok_rows = tokens.shape[0]
    row_count = lax.axis_size("row")
    col_count = lax.axis_size("col")
    heads_row = w_xz.shape[1]
    heads_dev = heads_row // col_count
    head_width = w_xz.shape[2] // 2
    groups_row = w_bc.shape[1]
    groups = groups_row * row_count
    state_width = w_bc.shape[2] // 2
    group_heads = heads_row * row_count // groups
    row_first = lax.axis_index("row") * col_count * heads_dev
    group_start = row_first // group_heads
    own_group = (row_first + lax.axis_index("col") * heads_dev) // group_heads
    xz_term = jnp.einsum("ld,dhe->lhe", tokens, w_xz, preferred_element_type=jnp.float32)
    dt_term = jnp.dot(tokens, w_dt, preferred_element_type=jnp.float32)
    bc_part = jnp.einsum("ld,dgn->lgn", tokens, w_bc, preferred_element_type=jnp.float32)
    slot_group = (
        row_first + jnp.arange(col_count, dtype=jnp.int32) * heads_dev
    ) // group_heads - group_start
    bc_slots = jnp.zeros((tok_rows, col_count, 2 * state_width), jnp.float32)
    for member in range(groups_row):
        picked = (slot_group == member).astype(jnp.float32)
        bc_slots = bc_slots + bc_part[:, member][:, None, :] * picked[None, :, None]
    xz_sum, dt_raw, bc_sum = (
        lax.psum_scatter(
            xz_term.astype(jnp.bfloat16), "col", scatter_dimension=1, tiled=True
        ).astype(jnp.float32),
        lax.psum_scatter(
            dt_term.astype(jnp.bfloat16), "col", scatter_dimension=1, tiled=True
        ).astype(jnp.float32),
        lax.psum_scatter(
            bc_slots.astype(jnp.bfloat16), "col", scatter_dimension=1, tiled=True
        ).astype(jnp.float32),
    )
    x_pre = xz_sum[:, :, :head_width].astype(jnp.bfloat16)
    gate_z = xz_sum[:, :, head_width:].astype(jnp.bfloat16)
    bc_pre = bc_sum[:, 0].astype(jnp.bfloat16)
    edge_len = conv_x.shape[0] - 1
    x_edge, bc_edge = shifted(
        (x_pre[tok_rows - edge_len :], bc_pre[tok_rows - edge_len :]), "ctx", 1
    )
    x_conv = causal_conv(x_edge, x_pre, conv_x, conv_x_bias)
    bc_kernel = lax.dynamic_index_in_dim(conv_bc, own_group, 1, keepdims=False)
    bc_offset = lax.dynamic_index_in_dim(conv_bc_bias, own_group, 0, keepdims=False)
    bc_conv = causal_conv(bc_edge, bc_pre, bc_kernel, bc_offset)
    b_input = bc_conv[:, :state_width]
    c_output = bc_conv[:, state_width:]
    step_size = jax.nn.softplus(dt_raw + dt_bias)
    cumul = jnp.cumsum(step_size * jnp.exp(a_log), axis=0)
    cum_heads = cumul.T
    diff = cum_heads[:, :, None] - cum_heads[:, None, :]
    positions = jnp.arange(tok_rows)
    causal = (positions[:, None] >= positions[None, :])[None]
    decay = jnp.where(causal, jnp.exp(-jnp.where(causal, diff, 0.0)), 0.0)
    scores = jnp.einsum("tn,sn->ts", c_output, b_input, preferred_element_type=jnp.float32)
    mixing = (scores[None] * decay * step_size.T[:, None, :]).astype(jnp.bfloat16)
    y_intra = jnp.einsum("hts,shp->thp", mixing, x_conv, preferred_element_type=jnp.float32)
    tail = jnp.exp(-(cumul[-1][None, :] - cumul))
    scaled = ((tail * step_size)[:, :, None] * x_conv.astype(jnp.float32)).astype(jnp.bfloat16)
    local = jnp.einsum("shp,sn->hpn", scaled, b_input, preferred_element_type=jnp.float32)
    fall = jnp.exp(-cumul[-1])
    identity = (jnp.ones_like(fall), jnp.zeros_like(local))
    prior_fall, state_in = entering((fall, local), "ctx", combine_states, identity)
    carried = jnp.einsum(
        "tn,hpn->thp", c_output.astype(jnp.float32), state_in, precision=lax.Precision.HIGHEST
    )
    y_total = (
        y_intra
        + jnp.exp(-cumul)[:, :, None] * carried
        + d_skip[None, :, None] * x_conv.astype(jnp.float32)
    )
    gated = y_total * jax.nn.silu(gate_z.astype(jnp.float32))
    squares = jnp.sum(gated * gated, axis=(1, 2))
    selector = (jnp.arange(groups, dtype=jnp.int32) == own_group).astype(jnp.float32)
    group_sums = lax.psum(squares[:, None] * selector[None, :], ("row", "col"))
    mean_sq = jnp.sum(group_sums * selector[None, :], axis=1) / (group_heads * head_width)
    normed = (gated * lax.rsqrt(mean_sq + EPSILON)[:, None, None] * norm_gain).astype(jnp.bfloat16)
    partial_out = jnp.einsum("lhp,hpd->ld", normed, w_out, preferred_element_type=jnp.float32)
    mixed = lax.psum_scatter(partial_out, ("row", "col"), scatter_dimension=1, tiled=True)
    return mixed


def solution(mesh):
    in_specs = (
        P("ctx", "col"),
        P("col", "row", None),
        P("col", "row"),
        P("col", "row", None),
        P(None, ("row", "col"), None),
        P(("row", "col"), None),
        P(),
        P(),
        P(("row", "col")),
        P(("row", "col")),
        P(("row", "col")),
        P(("row", "col"), None),
        P(("row", "col"), None, None),
    )
    out_specs = P("ctx", ("row", "col"))
    return jax.shard_map(body, mesh=mesh, in_specs=in_specs, out_specs=out_specs, check_vma=False)
```

profile of v0, /device:TPU:24, one launch (start us, length us, event | category | flops | bytes accessed | tf_op | source)
XLA Modules:
  0.0 808.6 jit_solution(5613178046566912650)
XLA Ops:
  6.6 2.0 fusion.5
  8.6 1.0 add_convert_fusion
  9.7 5.1 convolution_convert_fusion
  15.8 46.7 %fusion = bf16[256,8]{0,1:T(8,128)(2,1)S(1)} fusion(bf16[256,20]{0,1:T(8,128)(2,1)S(1)} %convolution_convert_fusion.1), kind=kCustom, calls=%all-reduce-scatter | all-reduce-scatter fusion | flops 8193 | bytes 18432
  62.5 6.4 collective-permute-start.2
  68.9 12.6 %collective-permute-start.3 = (bf16[256,1]{0,1:T(2,128)(2,1)S(1)}, bf16[256,1]{0,1:T(2,128)(2,1)S(1)}, u32[]{:S(2)}, u32[]{:S(2)}) collective-permute-start(bf16[256,1]{0,1:T(2,128)(2,1)S(1)} %slice.138), channel_id=1, source_target_pairs={{0,2},{1,3},{4,6},{5,7},{8,10},{9,11},{12,14},{13,15},{16,18},{17,... | collective-permute-start | bytes 1544
  83.1 1.3 dynamic-slice.8
  85.4 1.5 reduce-window.6
  87.5 12.3 %reduce-scatter.8.cloned.1.call-done = bf16[256,1,256]{2,0,1:T(8,128)(2,1)} async-done(((bf16[256,4,256]{2,0,1:T(8,128)(2,1)}), bf16[256,1,256]{2,0,1:T(8,128)(2,1)}) %reduce-scatter.8.cloned.1.call-update) | async-done | bytes 131088 | tf_op jit(solution)/shard_map/reduce_scatter | solution.py:91
  100.4 1.9 collective-permute-start.1
  103.0 2.3 collective-permute-done.1
  106.3 111.8 %reduce-scatter.6.cloned.1.call-done = bf16[256,5,128]{2,0,1:T(8,128)(2,1)} async-done(((bf16[256,20,128]{2,0,1:T(8,128)(2,1)}), bf16[256,5,128]{2,0,1:T(8,128)(2,1)}) %reduce-scatter.6.cloned.1.call-update) | async-done | bytes 327696 | tf_op jit(solution)/shard_map/reduce_scatter | solution.py:85
  218.9 1.9 collective-permute-start
  221.0 2.8 collective-permute-done
  224.4 1.1 fusion.23
  226.7 95.7 %all-gather.1 = f32[64,1,5]{2,1,0:T(1,128)S(1)} all-gather(f32[1,1,5]{2,1,0:T(1,128)S(1)} %bitcast.98), channel_id=1, replica_groups=mesh['ctx'=64,'row'=4,'col'=4] {'ctx'}, dimensions={0}, use_global_device_ids=true | all-gather | bytes 1300 | tf_op jit(solution)/shard_map/all_gather | solution.py:17
  322.6 30.5 %all-gather.4.cloned.1.call-done = f32[320,64,128]{2,1,0:T(8,128)} async-done(((f32[5,64,128]{2,1,0:T(8,128)}), f32[320,64,128]{2,1,0:T(8,128)}) %all-gather.4.cloned.1.call-update) | async-done | bytes 10485776 | tf_op jit(solution)/shard_map/all_gather | solution.py:17
  353.2 98.8 %while.14 = (s32[]{:T(128)}, f32[5,64,128]{2,1,0:T(8,128)S(1)}, s32[]{:T(128)}, f32[64,5]{1,0:T(8,128)S(1)}, f32[64,5,64,128]{3,2,1,0:T(8,128)}, /*index=5*/s32[]{:T(128)}, s32[]{:T(128)}) while((s32[]{:T(128)}, f32[5,64,128]{2,1,0:T(8,128)S(1)}, s32[]{:T(128)}, f32[64,5]{1,0:T(8,128)S(1)}, f32[64,5,64,128]{3,2,1,0:T(8,128)}, ...), condition=%wide.region_6.7_spmd.clone, body=%wide.region_5.6_spmd.clone.sunk | while | flops 163844 | bytes 491685 | solution.py:29
  353.7 1.0 fusion.51
  358.3 1.0 fusion.51
  359.8 1.0 fusion.51
  361.4 1.0 fusion.51
  366.0 1.0 fusion.51
  367.6 1.0 fusion.51
  373.7 1.0 fusion.51
  375.3 1.0 fusion.51
  381.5 1.0 fusion.51
  383.0 1.0 fusion.51
  452.4 2.7 multiply_reduce_fusion
  455.2 77.5 %psum.7 = f32[256,8]{0,1:T(8,128)S(1)} all-reduce(f32[256,8]{0,1:T(8,128)S(1)} %broadcast_multiply_fusion), channel_id=1, replica_groups=mesh['ctx'=64,'row'=4,'col'=4] {'row','col'}, use_global_device_ids=true, to_apply=%region_8.9 | all-reduce | flops 2048 | bytes 16384 | tf_op jit(solution)/shard_map/psum | solution.py:135
  532.8 4.4 convolution_bitcast_fusion
  537.3 264.8 %reduce-scatter.10.cloned.1.call-done = f32[256,256]{1,0:T(8,128)} async-done(((f32[256,4096]{1,0:T(8,128)}), f32[256,256]{1,0:T(8,128)}) %reduce-scatter.10.cloned.1.call-update) | async-done | bytes 262160 | tf_op jit(solution)/shard_map/reduce_scatter | solution.py:139
  (184 shorter events, 96.9 us)
Async XLA Ops:
  6.5 526.3 %copy-start = (bf16[5,64,4096]{2,1,0:T(8,128)(2,1)S(1)}, bf16[5,64,4096]{2,1,0:T(8,128)(2,1)}, u32[]{:S(2)}) copy-start(bf16[5,64,4096]{2,1,0:T(8,128)(2,1)} %param.27) | copy-start | bytes 7864324
  6.5 93.2 %reduce-scatter.8.cloned.1.call-start = ((), (), s32[]{:S(2)}) async-start(), calls=%async_computation.4 | async-start | bytes 655360 | tf_op jit(solution)/shard_map/reduce_scatter | solution.py:91
  8.5 1.1 copy-start.1
  9.6 208.5 %reduce-scatter.6.cloned.1.call-start = ((), (), s32[]{:S(2)}) async-start(), calls=%async_computation.3 | async-start | bytes 1638400 | tf_op jit(solution)/shard_map/reduce_scatter | solution.py:85
  14.8 0.8 copy-start.3
  14.8 67.6 %copy-start.4 = (f32[4,5,64]{2,0,1:T(4,128)S(1)}, f32[4,5,64]{2,0,1:T(4,128)}, u32[]{:S(2)}) copy-start(f32[4,5,64]{2,0,1:T(4,128)} %param.19) | copy-start | bytes 15364
  14.8 68.3 %copy-start.9 = (f32[5]{0:T(128)S(1)}, f32[5]{0:T(128)}, u32[]{:S(2)}) copy-start(f32[5]{0:T(128)} %param.24) | copy-start | bytes 64
  14.8 70.5 %copy-start.6 = (f32[5]{0:T(128)S(1)}, f32[5]{0:T(128)}, u32[]{:S(2)}) copy-start(f32[5]{0:T(128)} %param.23) | copy-start | bytes 64
  14.8 338.4 %all-gather.4.cloned.1.call-start = ((), (), s32[]{:S(2)}) async-start(), calls=%async_computation.6 | async-start | bytes 10649600 | tf_op jit(solution)/shard_map/all_gather | solution.py:17
  62.5 22.6 %collective-permute-start.2 = (bf16[256,8]{0,1:T(8,128)(2,1)S(1)}, bf16[256,8]{0,1:T(8,128)(2,1)S(1)}, u32[]{:S(2)}, u32[]{:S(2)}) collective-permute-start(bf16[256,8]{0,1:T(8,128)(2,1)S(1)} %fusion), channel_id=1, source_target_pairs={{0,1},{1,2},{2,3},{4,5},{5,6},{6,7},{8,9},{9,10},{10,11},{12,13},{... | collective-permute-start | bytes 12296
  68.9 16.1 %collective-permute-start.3 = (bf16[256,1]{0,1:T(2,128)(2,1)S(1)}, bf16[256,1]{0,1:T(2,128)(2,1)S(1)}, u32[]{:S(2)}, u32[]{:S(2)}) collective-permute-start(bf16[256,1]{0,1:T(2,128)(2,1)S(1)} %slice.138), channel_id=1, source_target_pairs={{0,2},{1,3},{4,6},{5,7},{8,10},{9,11},{12,14},{13,15},{16,18},{17,... | collective-permute-start | bytes 1544
  100.4 4.9 collective-permute-start.1
  105.3 118.6 %copy-start.5 = (f32[5,64]{1,0:T(8,128)S(1)}, f32[5,64]{1,0:T(8,128)}, u32[]{:S(2)}) copy-start(f32[5,64]{1,0:T(8,128)} %param.20) | copy-start | bytes 3844
  218.1 5.7 copy-start.2
  218.9 4.9 collective-permute-start
  225.5 576.6 %reduce-scatter.10.cloned.1.call-start = ((), (), s32[]{:S(2)}) async-start(), calls=%async_computation.5 | async-start | bytes 4456448 | tf_op jit(solution)/shard_map/reduce_scatter | solution.py:139
  452.4 2.7 copy-start.7
  452.4 80.4 %copy-start.8 = (f32[5,64]{1,0:T(8,128)S(1)}, f32[5,64]{1,0:T(8,128)}, u32[]{:S(2)}) copy-start(f32[5,64]{1,0:T(8,128)} %param.26) | copy-start | bytes 3844
Sparse Core Ops, SparseCore 0:
  10.8 88.9 reduce-scatter.7
  103.2 114.8 reduce-scatter.5
  225.6 127.5 all-gather.3
  537.4 264.6 reduce-scatter.9
where the time goes:
time: 810 us; the launch traced here: 809 us
  waiting for transfers between devices  425 us (52%)
  blocking collectives  220 us (27%)
  other arithmetic  71 us (9%)
  local copies, waits for them, and re-layouts  38.7 us (5%)
  starting transfers between devices  23 us (3%)
  matrix products  16.2 us (2%)
  between operations  14.1 us (2%)
    reduce_scatter x1, waiting for transfers between devices, body(): lax.psum_scatter(partial_out, ('row', 'col'), scatter_dimension=1, tiled=...  265 us
    reduce_scatter x1, waiting for transfers between devices, body(): lax.psum_scatter(xz_term.astype(jnp.bfloat16), 'col', scatter_dimension=1...  112 us
    all_gather x1, blocking collectives, entering(): everything = jax.tree.map(lambda part: lax.all_gather(part, axis), array)  95.7 us
    psum x1, blocking collectives, body(): group_sums = lax.psum(squares[:, None] * selector[None, :], ('row', 'col'))  77.5 us
    select_n x64, other arithmetic, hop(): return jax.tree.map(lambda a, b: jnp.where(reached, a, b), new, before)  64.4 us
    unnamed x1, blocking collectives  46.7 us
    mul x64, local copies, waits for them, and re-layouts, combine_states(): later[0][:, None, None] * earlier[1] + later[1]  33.2 us
    all_gather x1, waiting for transfers between devices, entering(): everything = jax.tree.map(lambda part: lax.all_gather(part, axis), array)  30.5 us
  transfers between devices with their start and end apart: 8, of which 6 were waited for; matrix products, arithmetic and copies ran while one was open for 8% of the time, Pallas kernels for 0%

commit v1 on v0

--- a/solution.py
+++ b/solution.py
@@ -12,23 +12,6 @@
     return lax.ppermute(block, axis, route)
 
 
-def entering(array, axis, combine, identity):
-    size, mine = (lax.axis_size(axis), lax.axis_index(axis))
-    everything = jax.tree.map(lambda part: lax.all_gather(part, axis), array)
-    start = jax.tree.map(
-        lambda part, zero: jnp.broadcast_to(jnp.asarray(zero, part.dtype), part.shape),
-        array,
-        identity,
-    )
-
-    def hop(k, before):
-        reached = k < mine
-        new = combine(before, jax.tree.map(lambda part: part[k], everything))
-        return jax.tree.map(lambda a, b: jnp.where(reached, a, b), new, before)
-
-    return lax.fori_loop(0, size, hop, start)
-
-
 def causal_conv(edge_rows, own_rows, weights, bias):
     width_k = weights.shape[0]
     count = own_rows.shape[0]
@@ -41,6 +24,30 @@
 
 def combine_states(earlier, later):
     return (earlier[0] * later[0], later[0][:, None, None] * earlier[1] + later[1])
+
+
+def entering(fall, local, axis):
+    size, mine = lax.axis_size(axis), lax.axis_index(axis)
+    rows = local.shape[1]
+    packed = jnp.concatenate(
+        [local, jnp.broadcast_to(fall[:, None, None], (local.shape[0], 1, local.shape[2]))], axis=1
+    )
+    got = shifted(packed, axis, 1)
+    first = mine < 1
+    identity = jnp.concatenate(
+        [jnp.zeros_like(local), jnp.ones((local.shape[0], 1, local.shape[2]), local.dtype)], axis=1
+    )
+    acc = jnp.where(first, identity, got)
+    distance = 1
+    while distance < size:
+        before = shifted(acc, axis, distance)
+        later_fall = acc[:, rows:rows + 1, :]
+        joined = jnp.concatenate(
+            [later_fall * before[:, :rows] + acc[:, :rows], later_fall * before[:, rows:]], axis=1
+        )
+        acc = jnp.where(mine >= distance, joined, acc)
+        distance *= 2
+    return acc[:, rows, 0], acc[:, :rows]
 
 
 def body(
@@ -68,9 +75,10 @@
     groups = groups_row * row_count
     state_width = w_bc.shape[2] // 2
     group_heads = heads_row * row_count // groups
+    col_index = lax.axis_index("col")
     row_first = lax.axis_index("row") * col_count * heads_dev
     group_start = row_first // group_heads
-    own_group = (row_first + lax.axis_index("col") * heads_dev) // group_heads
+    own_group = (row_first + col_index * heads_dev) // group_heads
     xz_term = jnp.einsum("ld,dhe->lhe", tokens, w_xz, preferred_element_type=jnp.float32)
     dt_term = jnp.dot(tokens, w_dt, preferred_element_type=jnp.float32)
     bc_part = jnp.einsum("ld,dgn->lgn", tokens, w_bc, preferred_element_type=jnp.float32)
@@ -81,24 +89,34 @@
     for member in range(groups_row):
         picked = (slot_group == member).astype(jnp.float32)
         bc_slots = bc_slots + bc_part[:, member][:, None, :] * picked[None, :, None]
-    xz_sum, dt_raw, bc_sum = (
-        lax.psum_scatter(
-            xz_term.astype(jnp.bfloat16), "col", scatter_dimension=1, tiled=True
-        ).astype(jnp.float32),
-        lax.psum_scatter(
-            dt_term.astype(jnp.bfloat16), "col", scatter_dimension=1, tiled=True
-        ).astype(jnp.float32),
-        lax.psum_scatter(
-            bc_slots.astype(jnp.bfloat16), "col", scatter_dimension=1, tiled=True
-        ).astype(jnp.float32),
+    xz_slots = xz_term.reshape(tok_rows, col_count, heads_dev * 2 * head_width)
+    main = jnp.concatenate([xz_slots, bc_slots], axis=2)
+    feat = main.shape[2]
+    dt_flat = dt_term.reshape(tok_rows, col_count, heads_dev).transpose(1, 2, 0).reshape(col_count, -1)
+    dt_rows = -(-dt_flat.shape[1] // (8 * feat)) * 8
+    dt_flat = jnp.pad(dt_flat, ((0, 0), (0, dt_rows * feat - dt_flat.shape[1])))
+    dt_block = dt_flat.reshape(col_count, dt_rows, feat).transpose(1, 0, 2)
+    packed = jnp.concatenate([main, dt_block], axis=0)
+    summed = lax.optimization_barrier(
+        lax.psum_scatter(packed.astype(jnp.bfloat16), "col", scatter_dimension=1, tiled=True)
+    )[:, 0]
+    xz_width = heads_dev * 2 * head_width
+    xz_sum = summed[:tok_rows, :xz_width].reshape(tok_rows, heads_dev, 2 * head_width)
+    bc_pre = summed[:tok_rows, xz_width:]
+    dt_raw = (
+        summed[tok_rows:].reshape(-1)[: heads_dev * tok_rows]
+        .reshape(heads_dev, tok_rows)
+        .T.astype(jnp.float32)
     )
-    x_pre = xz_sum[:, :, :head_width].astype(jnp.bfloat16)
-    gate_z = xz_sum[:, :, head_width:].astype(jnp.bfloat16)
-    bc_pre = bc_sum[:, 0].astype(jnp.bfloat16)
+    x_pre = xz_sum[:, :, :head_width]
+    gate_z = xz_sum[:, :, head_width:]
     edge_len = conv_x.shape[0] - 1
-    x_edge, bc_edge = shifted(
-        (x_pre[tok_rows - edge_len :], bc_pre[tok_rows - edge_len :]), "ctx", 1
+    edge = jnp.concatenate(
+        [x_pre[tok_rows - edge_len :].reshape(edge_len, -1), bc_pre[tok_rows - edge_len :]], axis=1
     )
+    edge = shifted(edge, "ctx", 1)
+    x_edge = edge[:, : heads_dev * head_width].reshape(edge_len, heads_dev, head_width)
+    bc_edge = edge[:, heads_dev * head_width :]
     x_conv = causal_conv(x_edge, x_pre, conv_x, conv_x_bias)
     bc_kernel = lax.dynamic_index_in_dim(conv_bc, own_group, 1, keepdims=False)
     bc_offset = lax.dynamic_index_in_dim(conv_bc_bias, own_group, 0, keepdims=False)
@@ -119,8 +137,7 @@
     scaled = ((tail * step_size)[:, :, None] * x_conv.astype(jnp.float32)).astype(jnp.bfloat16)
     local = jnp.einsum("shp,sn->hpn", scaled, b_input, preferred_element_type=jnp.float32)
     fall = jnp.exp(-cumul[-1])
-    identity = (jnp.ones_like(fall), jnp.zeros_like(local))
-    prior_fall, state_in = entering((fall, local), "ctx", combine_states, identity)
+    _, state_in = entering(fall, local, "ctx")
     carried = jnp.einsum(
         "tn,hpn->thp", c_output.astype(jnp.float32), state_in, precision=lax.Precision.HIGHEST
     )
@@ -131,13 +148,21 @@
     )
     gated = y_total * jax.nn.silu(gate_z.astype(jnp.float32))
     squares = jnp.sum(gated * gated, axis=(1, 2))
-    selector = (jnp.arange(groups, dtype=jnp.int32) == own_group).astype(jnp.float32)
-    group_sums = lax.psum(squares[:, None] * selector[None, :], ("row", "col"))
-    mean_sq = jnp.sum(group_sums * selector[None, :], axis=1) / (group_heads * head_width)
+    if group_heads == 2 * heads_dev:
+        partner = [(c, c ^ 1) for c in range(col_count)]
+        group_sum = squares + lax.ppermute(squares, "col", partner)
+    else:
+        selector = (jnp.arange(groups, dtype=jnp.int32) == own_group).astype(jnp.float32)
+        group_sums = lax.psum(squares[:, None] * selector[None, :], ("row", "col"))
+        group_sum = jnp.sum(group_sums * selector[None, :], axis=1)
+    mean_sq = group_sum / (group_heads * head_width)
     normed = (gated * lax.rsqrt(mean_sq + EPSILON)[:, None, None] * norm_gain).astype(jnp.bfloat16)
     partial_out = jnp.einsum("lhp,hpd->ld", normed, w_out, preferred_element_type=jnp.float32)
-    mixed = lax.psum_scatter(partial_out, ("row", "col"), scatter_dimension=1, tiled=True)
-    return mixed
+    by_row = lax.psum_scatter(
+        partial_out.astype(jnp.bfloat16), "row", scatter_dimension=1, tiled=True
+    )
+    mixed = lax.psum_scatter(by_row, "col", scatter_dimension=1, tiled=True)
+    return mixed.astype(jnp.float32)
 
 
 def solution(mesh):

time: 810 us -> 444 us (0.55)
  blocking collectives: 220 us -> 0 us
  waiting for transfers between devices: 425 us -> 340 us
  other arithmetic: 71 us -> 10 us
  starting transfers between devices: 23 us -> 49 us
  local copies, waits for them, and re-layouts: 38.7 us -> 18.2 us
    reduce_scatter x3 -> x2, waiting for transfers between devices: 389 us -> 137 us  [the longest x1 84.4 us: body(): mixed = lax.psum_scatter(by_row, 'col', scatter_dimension=1, tiled=True)]
    unnamed x6 -> x4, waiting for transfers between devices: 0.07 us -> 166 us
    all_gather x1 -> x0, blocking collectives: 95.7 us -> none  [entering(): everything = jax.tree.map(lambda part: lax.all_gather(part, axis), array)]
    psum x1 -> x0, blocking collectives: 77.5 us -> none  [body(): group_sums = lax.psum(squares[:, None] * selector[None, :], ('row', 'col'))]
    select_n x64 -> x6, other arithmetic: 64.4 us -> 0.16 us  [the longest x5 0.13 us: entering(): acc = jnp.where(mine >= distance, joined, acc)]
    unnamed x1 -> x0, blocking collectives: 46.7 us -> none
    ppermute x2 -> x8, starting transfers between devices: 3.82 us -> 47 us  [shifted(): return lax.ppermute(block, axis, route)]
    mul x64 -> x0, local copies, waits for them, and re-layouts: 33.2 us -> none  [combine_states(): later[0][:, None, None] * earlier[1] + later[1]]
  transfers between devices with their start and end apart: 8 -> 12, of which waited for: 6 -> 12; matrix products, arithmetic and copies ran while one was open for 8% -> 1% of each run, Pallas kernels for 0% -> 0%
where the time goes in v1:
time: 444 us; the launch traced here: 443 us
  waiting for transfers between devices  340 us (77%)
  starting transfers between devices  49 us (11%)
  local copies, waits for them, and re-layouts  18.2 us (4%)
  between operations  13.6 us (3%)
  matrix products  12.5 us (3%)
  other arithmetic  10 us (2%)
    unnamed x4, waiting for transfers between devices  166 us
    reduce_scatter x1, waiting for transfers between devices, body(): mixed = lax.psum_scatter(by_row, 'col', scatter_dimension=1, tiled=True)  84.4 us
    reduce_scatter x1, waiting for transfers between devices, body(): lax.psum_scatter(partial_out.astype(jnp.bfloat16), 'row', scatter_dimensi...  52.8 us
    ppermute x8, starting transfers between devices, shifted(): return lax.ppermute(block, axis, route)  47 us
    ppermute x8, waiting for transfers between devices, shifted(): return lax.ppermute(block, axis, route)  23.8 us
    ppermute x1, waiting for transfers between devices, body(): group_sum = squares + lax.ppermute(squares, 'col', partner)  12.2 us
    unnamed x38, local copies, waits for them, and re-layouts  9.71 us
  transfers between devices with their start and end apart: 12, of which 12 were waited for; matrix products, arithmetic and copies ran while one was open for 1% of the time, Pallas kernels for 0%

profile of v1, /device:TPU:24, one launch (start us, length us, event | category | flops | bytes accessed | tf_op | source)
XLA Modules:
  0.0 442.9 jit_solution(8767214297429853286)
XLA Ops:
  6.6 2.0 fusion.4
  8.6 7.9 %copy.77 = bf16[1024,20,128]{0,2,1:T(8,128)(2,1)} copy(bf16[1024,20,128]{2,0,1:T(8,128)(2,1)} %param.14) | data formatting | bytes 10485760 | tf_op args[1]
  16.5 4.3 fusion.59
  20.8 1.3 convert.18
  22.1 2.4 copy.79
  24.5 1.3 convolution_convert_fusion
  26.1 2.8 pad_maximum_fusion
  31.0 166.3 %reduce-scatter.10.cloned.1.call-done = bf16[264,1,896]{2,0,1:T(8,128)(2,1)} async-done(((bf16[264,4,896]{2,0,1:T(8,128)(2,1)}), bf16[264,1,896]{2,0,1:T(8,128)(2,1)}) %reduce-scatter.10.cloned.1.call-update) | async-done | bytes 473104
  199.9 1.5 reduce-window.6
  202.6 1.9 collective-permute-start
  205.5 2.1 collective-permute-done
  209.5 3.5 collective-permute-start.1
  213.0 3.4 collective-permute-done.1
  216.4 5.2 %collective-permute-start.2 = (f32[5,65,128]{2,1,0:T(8,128)S(1)}, f32[5,65,128]{2,1,0:T(8,128)S(1)}, u32[]{:S(2)}, u32[]{:S(2)}) collective-permute-start(f32[5,65,128]{2,1,0:T(8,128)S(1)} %broadcast_select_fusion), channel_id=1, source_target_pairs={{0,16},{16,32},{32,48},{48,64},{64,80},{80,96},{96,112},{112,128},... | collective-permute-start | bytes 499208 | tf_op jit(solution)/shard_map/ppermute | solution.py:12
  221.6 1.7 collective-permute-done.2
  223.3 11.7 %collective-permute-start.3 = (f32[5,65,128]{2,1,0:T(8,128)S(1)}, f32[5,65,128]{2,1,0:T(8,128)S(1)}, u32[]{:S(2)}, u32[]{:S(2)}) collective-permute-start(f32[5,65,128]{2,1,0:T(8,128)S(1)} %maximum_select_fusion), channel_id=1, source_target_pairs={{0,32},{16,48},{32,64},{48,80},{64,96},{80,112},{96,128},{112,144}... | collective-permute-start | bytes 499208 | tf_op jit(solution)/shard_map/ppermute | solution.py:12
  235.1 3.6 collective-permute-done.3
  238.8 3.4 collective-permute-start.4
  242.2 5.7 %collective-permute-done.4 = f32[5,65,128]{2,1,0:T(8,128)S(1)} collective-permute-done((f32[5,65,128]{2,1,0:T(8,128)S(1)}, f32[5,65,128]{2,1,0:T(8,128)S(1)}, u32[]{:S(2)}, u32[]{:S(2)}) %collective-permute-start.4) | collective-permute-done | bytes 166432 | tf_op jit(solution)/shard_map/ppermute | solution.py:12
  247.9 2.1 collective-permute-start.5
  250.1 3.0 collective-permute-done.5
  254.7 3.8 collective-permute-start.6
  258.6 1.1 fusion.39
  259.6 2.0 collective-permute-done.6
  261.7 15.3 %collective-permute-start.7 = (f32[5,65,128]{2,1,0:T(8,128)S(1)}, f32[5,65,128]{2,1,0:T(8,128)S(1)}, u32[]{:S(2)}, u32[]{:S(2)}) collective-permute-start(f32[5,65,128]{2,1,0:T(8,128)S(1)} %maximum_select_fusion.4), channel_id=1, source_target_pairs={{0,512},{16,528},{32,544},{48,560},{64,576},{80,592},{96,608},{112... | collective-permute-start | bytes 499208 | tf_op jit(solution)/shard_map/ppermute | solution.py:12
  277.6 2.4 collective-permute-done.7
  280.5 1.9 collective-permute-start.8
  282.4 12.2 %collective-permute-done.8 = f32[256]{0:T(256)S(1)} collective-permute-done((f32[256]{0:T(256)S(1)}, f32[256]{0:T(256)S(1)}, u32[]{:S(2)}, u32[]{:S(2)}) %collective-permute-start.8) | collective-permute-done | bytes 1056 | tf_op jit(solution)/shard_map/ppermute | solution.py:153
  294.7 2.7 fusion
  297.5 52.8 %reduce-scatter.6.cloned.1.call-done = bf16[256,1024]{1,0:T(8,128)(2,1)} async-done(((bf16[256,4096]{1,0:T(8,128)(2,1)}), bf16[256,1024]{1,0:T(8,128)(2,1)}) %reduce-scatter.6.cloned.1.call-update) | async-done | bytes 524304 | tf_op jit(solution)/shard_map/reduce_scatter | solution.py:161
  350.3 84.4 %reduce-scatter.8.cloned.1.call-done = bf16[256,256]{1,0:T(8,128)(2,1)} async-done(((bf16[256,1024]{1,0:T(8,128)(2,1)}), bf16[256,256]{1,0:T(8,128)(2,1)}) %reduce-scatter.8.cloned.1.call-update) | async-done | bytes 131088 | tf_op jit(solution)/shard_map/reduce_scatter | solution.py:164
  434.7 1.6 convert_element_type.71
  (107 shorter events, 12.0 us)
Async XLA Ops:
  6.5 288.2 %copy-start = (bf16[5,64,4096]{2,1,0:T(8,128)(2,1)S(1)}, bf16[5,64,4096]{2,1,0:T(8,128)(2,1)}, u32[]{:S(2)}) copy-start(bf16[5,64,4096]{2,1,0:T(8,128)(2,1)} %param.25) | copy-start | bytes 7864324
  6.5 190.8 %reduce-scatter.10.cloned.1.call-start = ((), (), s32[]{:S(2)}) async-start(), calls=%async_computation.5 | async-start | bytes 2365440
  22.1 2.4 copy-start.7
  28.9 0.7 copy-start.12
  28.9 2.1 copy-start.9
  28.9 170.9 %copy-start.11 = (f32[5]{0:T(128)S(1)}, f32[5]{0:T(128)}, u32[]{:S(2)}) copy-start(f32[5]{0:T(128)} %param.21) | copy-start | bytes 64
  28.9 321.4 %reduce-scatter.6.cloned.1.call-start = ((), (), s32[]{:S(2)}) async-start(), calls=%async_computation.3 | async-start | bytes 2621440 | tf_op jit(solution)/shard_map/reduce_scatter | solution.py:161
  202.1 6.1 %copy-start.10 = (f32[5,64]{1,0:T(8,128)S(1)}, f32[5,64]{1,0:T(8,128)}, u32[]{:S(2)}) copy-start(f32[5,64]{1,0:T(8,128)} %param.18) | copy-start | bytes 3844
  202.6 4.9 %collective-permute-start = (bf16[3,576]{1,0:T(4,128)(2,1)S(1)}, bf16[3,576]{1,0:T(4,128)(2,1)S(1)}, u32[]{:S(2)}, u32[]{:S(2)}) collective-permute-start(bf16[3,576]{1,0:T(4,128)(2,1)S(1)} %pad_maximum_fusion.3), channel_id=1, source_target_pairs={{0,16},{16,32},{32,48},{48,64},{64,80},{80,96},{96,112},{112,128},... | collective-permute-start | bytes 10376 | tf_op jit(solution)/shard_map/ppermute | solution.py:12
  208.0 8.4 %copy-start.5 = (f32[5,65,128]{2,1,0:T(8,128)S(1)}, f32[5,65,128]{2,1,0:T(8,128)}, u32[]{:S(2)}) copy-start(f32[5,65,128]{2,1,0:T(8,128)} %constant.79.clone.1) | copy-start | bytes 499204
  208.2 0.6 copy-start.1
  208.7 0.7 copy-start.3
  209.5 6.9 %collective-permute-start.1 = (f32[5,65,128]{2,1,0:T(8,128)S(1)}, f32[5,65,128]{2,1,0:T(8,128)S(1)}, u32[]{:S(2)}, u32[]{:S(2)}) collective-permute-start(f32[5,65,128]{2,1,0:T(8,128)S(1)} %pad_maximum_fusion.1), channel_id=1, source_target_pairs={{0,16},{16,32},{32,48},{48,64},{64,80},{80,96},{96,112},{112,128},... | collective-permute-start | bytes 499208 | tf_op jit(solution)/shard_map/ppermute | solution.py:12
  216.4 6.9 %collective-permute-start.2 = (f32[5,65,128]{2,1,0:T(8,128)S(1)}, f32[5,65,128]{2,1,0:T(8,128)S(1)}, u32[]{:S(2)}, u32[]{:S(2)}) collective-permute-start(f32[5,65,128]{2,1,0:T(8,128)S(1)} %broadcast_select_fusion), channel_id=1, source_target_pairs={{0,16},{16,32},{32,48},{48,64},{64,80},{80,96},{96,112},{112,128},... | collective-permute-start | bytes 499208 | tf_op jit(solution)/shard_map/ppermute | solution.py:12
  223.3 15.4 %collective-permute-start.3 = (f32[5,65,128]{2,1,0:T(8,128)S(1)}, f32[5,65,128]{2,1,0:T(8,128)S(1)}, u32[]{:S(2)}, u32[]{:S(2)}) collective-permute-start(f32[5,65,128]{2,1,0:T(8,128)S(1)} %maximum_select_fusion), channel_id=1, source_target_pairs={{0,32},{16,48},{32,64},{48,80},{64,96},{80,112},{96,128},{112,144}... | collective-permute-start | bytes 499208 | tf_op jit(solution)/shard_map/ppermute | solution.py:12
  238.8 38.3 %copy-start.4 = (bf16[256,5,64]{0,2,1:T(8,128)(2,1)S(1)}, bf16[256,5,64]{0,2,1:T(8,128)(2,1)}, u32[]{:S(2)}) copy-start(bf16[256,5,64]{0,2,1:T(8,128)(2,1)} %copy-done.3) | copy-start | bytes 491524
  238.8 9.1 %collective-permute-start.4 = (f32[5,65,128]{2,1,0:T(8,128)S(1)}, f32[5,65,128]{2,1,0:T(8,128)S(1)}, u32[]{:S(2)}, u32[]{:S(2)}) collective-permute-start(f32[5,65,128]{2,1,0:T(8,128)S(1)} %maximum_select_fusion.1), channel_id=1, source_target_pairs={{0,64},{16,80},{32,96},{48,112},{64,128},{80,144},{96,160},{112,17... | collective-permute-start | bytes 499208 | tf_op jit(solution)/shard_map/ppermute | solution.py:12
  247.9 5.1 %collective-permute-start.5 = (f32[5,65,128]{2,1,0:T(8,128)S(1)}, f32[5,65,128]{2,1,0:T(8,128)S(1)}, u32[]{:S(2)}, u32[]{:S(2)}) collective-permute-start(f32[5,65,128]{2,1,0:T(8,128)S(1)} %maximum_select_fusion.2), channel_id=1, source_target_pairs={{0,128},{16,144},{32,160},{48,176},{64,192},{80,208},{96,224},{112... | collective-permute-start | bytes 499208 | tf_op jit(solution)/shard_map/ppermute | solution.py:12
  253.1 0.7 copy-start.6
  254.7 6.9 %collective-permute-start.6 = (f32[5,65,128]{2,1,0:T(8,128)S(1)}, f32[5,65,128]{2,1,0:T(8,128)S(1)}, u32[]{:S(2)}, u32[]{:S(2)}) collective-permute-start(f32[5,65,128]{2,1,0:T(8,128)S(1)} %maximum_select_fusion.3), channel_id=1, source_target_pairs={{0,256},{16,272},{32,288},{48,304},{64,320},{80,336},{96,352},{112... | collective-permute-start | bytes 499208 | tf_op jit(solution)/shard_map/ppermute | solution.py:12
  261.7 18.4 %copy-start.2 = (bf16[256,256]{1,0:T(8,128)(2,1)S(1)}, bf16[256,256]{1,0:T(8,128)(2,1)}, u32[]{:S(2)}) copy-start(bf16[256,256]{1,0:T(8,128)(2,1)} %copy-done.1) | copy-start | bytes 393220
  261.7 18.4 %copy-start.13 = (f32[5]{0:T(128)S(1)}, f32[5]{0:T(128)}, u32[]{:S(2)}) copy-start(f32[5]{0:T(128)} %param.23) | copy-start | bytes 64
  261.7 18.4 %collective-permute-start.7 = (f32[5,65,128]{2,1,0:T(8,128)S(1)}, f32[5,65,128]{2,1,0:T(8,128)S(1)}, u32[]{:S(2)}, u32[]{:S(2)}) collective-permute-start(f32[5,65,128]{2,1,0:T(8,128)S(1)} %maximum_select_fusion.4), channel_id=1, source_target_pairs={{0,512},{16,528},{32,544},{48,560},{64,576},{80,592},{96,608},{112... | collective-permute-start | bytes 499208 | tf_op jit(solution)/shard_map/ppermute | solution.py:12
  277.6 17.1 %copy-start.8 = (f32[5,64]{1,0:T(8,128)S(1)}, f32[5,64]{1,0:T(8,128)}, u32[]{:S(2)}) copy-start(f32[5,64]{1,0:T(8,128)} %param.24) | copy-start | bytes 3844
  280.5 14.2 %collective-permute-start.8 = (f32[256]{0:T(256)S(1)}, f32[256]{0:T(256)S(1)}, u32[]{:S(2)}, u32[]{:S(2)}) collective-permute-start(f32[256]{0:T(256)S(1)} %get-tuple-element.33), channel_id=1, source_target_pairs={{0,1},{1,0},{2,3},{3,2},{4,5},{5,4},{6,7},{7,6},{8,9},{9,8},{10,11... | collective-permute-start | bytes 3080 | tf_op jit(solution)/shard_map/ppermute | solution.py:153
  297.4 137.3 %reduce-scatter.8.cloned.1.call-start = ((), (), s32[]{:S(2)}) async-start(), calls=%async_computation.4 | async-start | bytes 655360 | tf_op jit(solution)/shard_map/reduce_scatter | solution.py:164
Sparse Core Ops, SparseCore 0:
  29.0 168.2 reduce-scatter.9
  297.5 52.6 reduce-scatter.5
  354.1 80.6 reduce-scatter.7

commit v2 on v1

--- a/solution.py
+++ b/solution.py
@@ -26,27 +26,35 @@
     return (earlier[0] * later[0], later[0][:, None, None] * earlier[1] + later[1])
 
 
-def entering(fall, local, axis):
+def entering(fall, local, axis, radix=4):
     size, mine = lax.axis_size(axis), lax.axis_index(axis)
     rows = local.shape[1]
-    packed = jnp.concatenate(
+    own = jnp.concatenate(
         [local, jnp.broadcast_to(fall[:, None, None], (local.shape[0], 1, local.shape[2]))], axis=1
     )
-    got = shifted(packed, axis, 1)
-    first = mine < 1
     identity = jnp.concatenate(
         [jnp.zeros_like(local), jnp.ones((local.shape[0], 1, local.shape[2]), local.dtype)], axis=1
     )
-    acc = jnp.where(first, identity, got)
-    distance = 1
-    while distance < size:
-        before = shifted(acc, axis, distance)
-        later_fall = acc[:, rows:rows + 1, :]
-        joined = jnp.concatenate(
-            [later_fall * before[:, :rows] + acc[:, :rows], later_fall * before[:, rows:]], axis=1
+
+    def join(before, later):
+        later_fall = later[:, rows : rows + 1, :]
+        return jnp.concatenate(
+            [later_fall * before[:, :rows] + later[:, :rows], later_fall * before[:, rows:]], axis=1
         )
-        acc = jnp.where(mine >= distance, joined, acc)
-        distance *= 2
+
+    acc = identity
+    for distance in range(radix, 0, -1):
+        if distance < size:
+            got = shifted(own, axis, distance)
+            acc = jnp.where(mine >= distance, join(acc, got), acc)
+    span = radix
+    while span < size:
+        parts = [(step * span, shifted(acc, axis, step * span)) for step in range(1, radix) if step * span < size]
+        total = acc
+        for distance, got in parts:
+            total = jnp.where(mine >= distance, join(got, total), total)
+        acc = total
+        span *= radix
     return acc[:, rows, 0], acc[:, :rows]
 
 
@@ -79,7 +87,9 @@
     row_first = lax.axis_index("row") * col_count * heads_dev
     group_start = row_first // group_heads
     own_group = (row_first + col_index * heads_dev) // group_heads
-    xz_term = jnp.einsum("ld,dhe->lhe", tokens, w_xz, preferred_element_type=jnp.float32)
+    xz_term = jnp.dot(
+        tokens, w_xz.reshape(w_xz.shape[0], -1), preferred_element_type=jnp.float32
+    ).reshape(tok_rows, heads_row, w_xz.shape[2])
     dt_term = jnp.dot(tokens, w_dt, preferred_element_type=jnp.float32)
     bc_part = jnp.einsum("ld,dgn->lgn", tokens, w_bc, preferred_element_type=jnp.float32)
     slot_group = (
@@ -158,10 +168,9 @@
     mean_sq = group_sum / (group_heads * head_width)
     normed = (gated * lax.rsqrt(mean_sq + EPSILON)[:, None, None] * norm_gain).astype(jnp.bfloat16)
     partial_out = jnp.einsum("lhp,hpd->ld", normed, w_out, preferred_element_type=jnp.float32)
-    by_row = lax.psum_scatter(
-        partial_out.astype(jnp.bfloat16), "row", scatter_dimension=1, tiled=True
+    mixed = lax.psum_scatter(
+        partial_out.astype(jnp.bfloat16), ("row", "col"), scatter_dimension=1, tiled=True
     )
-    mixed = lax.psum_scatter(by_row, "col", scatter_dimension=1, tiled=True)
     return mixed.astype(jnp.float32)
 
 

time: 444 us -> 524 us (1.18)
  waiting for transfers between devices: 340 us -> 433 us
  starting transfers between devices: 49 us -> 39.7 us
    reduce_scatter x2 -> x1, waiting for transfers between devices: 137 us -> 236 us  [body(): lax.psum_scatter(partial_out.astype(jnp.bfloat16), ('row', 'col'), scatte...]
    ppermute x8 -> x11, starting transfers between devices: 47 us -> 34.5 us  [shifted(): return lax.ppermute(block, axis, route)]
    ppermute x8 -> x11, waiting for transfers between devices: 23.8 us -> 18.4 us  [shifted(): return lax.ppermute(block, axis, route)]
    dot_general x0 -> x1, matrix products: none -> 5.33 us  [body(): jnp.dot(tokens, w_xz.reshape(w_xz.shape[0], -1), preferred_element_type=j...]
    unnamed x4 -> x3, waiting for transfers between devices: 166 us -> 169 us
  transfers between devices with their start and end apart: 12 -> 14, of which waited for: 12 -> 11; matrix products, arithmetic and copies ran while one was open for 1% -> 1% of each run, Pallas kernels for 0% -> 0%
where the time goes in v2:
time: 524 us; the launch traced here: 523 us
  waiting for transfers between devices  433 us (83%)
  starting transfers between devices  39.7 us (8%)
  local copies, waits for them, and re-layouts  14.7 us (3%)
  between operations  13.9 us (3%)
  matrix products  11.6 us (2%)
  other arithmetic  10.4 us (2%)
    reduce_scatter x1, waiting for transfers between devices, body(): lax.psum_scatter(partial_out.astype(jnp.bfloat16), ('row', 'col'), scatte...  236 us
    unnamed x3, waiting for transfers between devices  169 us
    ppermute x11, starting transfers between devices, shifted(): return lax.ppermute(block, axis, route)  34.5 us
    ppermute x11, waiting for transfers between devices, shifted(): return lax.ppermute(block, axis, route)  18.4 us
  transfers between devices with their start and end apart: 14, of which 11 were waited for; matrix products, arithmetic and copies ran while one was open for 1% of the time, Pallas kernels for 0%

profile of v2, /device:TPU:24, one launch (start us, length us, event | category | flops | bytes accessed | tf_op | source)
XLA Modules:
  0.0 523.1 jit_solution(16065064614173815468)
XLA Ops:
  6.6 2.0 fusion.4
  8.6 7.9 %copy.72 = bf16[1024,20,128]{0,2,1:T(8,128)(2,1)} copy(bf16[1024,20,128]{2,0,1:T(8,128)(2,1)} %param.14) | data formatting | bytes 10485760 | tf_op args[1]
  16.5 5.3 %convolution_convert_fusion = bf16[256,4,640]{2,0,1:T(8,128)(2,1)} fusion(bf16[4,640,1024]{2,1,0:T(8,128)(2,1)} %bitcast.130, bf16[256,1024]{1,0:T(8,128)(2,1)} %param.13), kind=kOutput, calls=%fused_computation.3 | convolution fusion | flops 1342832640 | bytes 7077888 | tf_op jit(solution)/shard_map/dot_general | solution.py:90
  22.4 2.8 pad_maximum_fusion
  27.3 169.4 %reduce-scatter.7.cloned.1.call-done = bf16[264,1,896]{2,0,1:T(8,128)(2,1)} async-done(((bf16[264,4,896]{2,0,1:T(8,128)(2,1)}), bf16[264,1,896]{2,0,1:T(8,128)(2,1)}) %reduce-scatter.7.cloned.1.call-update) | async-done | bytes 473104
  197.5 1.0 slice.302
  199.3 1.5 reduce-window.6
  202.0 2.0 collective-permute-start
  204.1 0.9 slice.312
  205.0 2.0 collective-permute-done
  209.1 3.7 collective-permute-start.4
  212.9 1.9 collective-permute-start.3
  214.8 6.1 %collective-permute-start.2 = (f32[5,65,128]{2,1,0:T(8,128)}, f32[5,65,128]{2,1,0:T(8,128)S(1)}, u32[]{:S(2)}, u32[]{:S(2)}) collective-permute-start(f32[5,65,128]{2,1,0:T(8,128)} %pad_maximum_fusion.1), channel_id=1, source_target_pairs={{0,32},{16,48},{32,64},{48,80},{64,96},{80,112},{96,128},{112,144}... | collective-permute-start | bytes 499208 | tf_op jit(solution)/shard_map/ppermute | solution.py:12
  220.9 1.9 collective-permute-start.1
  223.6 0.9 slice_add_fusion.8
  224.7 4.0 collective-permute-done.2
  229.6 3.9 collective-permute-start.5
  233.7 1.3 collective-permute-start.6
  235.0 1.3 collective-permute-start.7
  236.3 4.1 collective-permute-done.5
  240.4 2.1 collective-permute-done.6
  242.6 2.0 collective-permute-done.7
  244.7 1.3 collective-permute-start.8
  246.6 9.7 %collective-permute-start.9 = (f32[5,65,128]{2,1,0:T(8,128)S(1)}, f32[5,65,128]{2,1,0:T(8,128)S(1)}, u32[]{:S(2)}, u32[]{:S(2)}) collective-permute-start(f32[5,65,128]{2,1,0:T(8,128)S(1)} %maximum_select_fusion.6), channel_id=1, source_target_pairs={{0,512},{16,528},{32,544},{48,560},{64,576},{80,592},{96,608},{112... | collective-permute-start | bytes 499208 | tf_op jit(solution)/shard_map/ppermute | solution.py:12
  256.3 1.3 collective-permute-start.10
  257.7 1.7 collective-permute-done.9
  259.4 1.9 collective-permute-done.10
  261.7 5.2 collective-permute-start.11
  266.9 9.0 %collective-permute-done.11 = f32[256]{0:T(256)S(1)} collective-permute-done((f32[256]{0:T(256)S(1)}, f32[256]{0:T(256)S(1)}, u32[]{:S(2)}, u32[]{:S(2)}) %collective-permute-start.11) | collective-permute-done | bytes 1056 | tf_op jit(solution)/shard_map/ppermute | solution.py:163
  275.9 2.7 fusion
  278.7 236.0 %reduce-scatter.5.cloned.1.call-done = bf16[256,256]{1,0:T(8,128)(2,1)} async-done(((bf16[256,4096]{1,0:T(8,128)(2,1)}), bf16[256,256]{1,0:T(8,128)(2,1)}) %reduce-scatter.5.cloned.1.call-update) | async-done | bytes 131088 | tf_op jit(solution)/shard_map/reduce_scatter | solution.py:171
  514.7 1.6 convert_element_type.71
  (115 shorter events, 10.7 us)
Async XLA Ops:
  6.5 269.4 %copy-start = (bf16[5,64,4096]{2,1,0:T(8,128)(2,1)S(1)}, bf16[5,64,4096]{2,1,0:T(8,128)(2,1)}, u32[]{:S(2)}) copy-start(bf16[5,64,4096]{2,1,0:T(8,128)(2,1)} %param.25) | copy-start | bytes 7864324
  6.5 190.2 %reduce-scatter.7.cloned.1.call-start = ((), (), s32[]{:S(2)}) async-start(), calls=%async_computation.3 | async-start | bytes 2365440
  16.5 5.3 %copy-start.2 = (bf16[256,1024]{1,0:T(8,128)(2,1)S(1)}, bf16[256,1024]{1,0:T(8,128)(2,1)}, u32[]{:S(2)}) copy-start(bf16[256,1024]{1,0:T(8,128)(2,1)} %param.13) | copy-start | bytes 1572868
  16.5 5.3 %copy-start.3 = (bf16[1024,20]{0,1:T(8,128)(2,1)S(1)}, bf16[1024,20]{0,1:T(8,128)(2,1)}, u32[]{:S(2)}) copy-start(bf16[1024,20]{0,1:T(8,128)(2,1)} %param.15) | copy-start | bytes 122884
  25.2 0.7 copy-start.8
  25.2 2.1 copy-start.5
  25.2 174.0 %copy-start.7 = (f32[5]{0:T(128)S(1)}, f32[5]{0:T(128)}, u32[]{:S(2)}) copy-start(f32[5]{0:T(128)} %param.21) | copy-start | bytes 64
  25.2 489.4 %reduce-scatter.5.cloned.1.call-start = ((), (), s32[]{:S(2)}) async-start(), calls=%async_computation.2 | async-start | bytes 2228224 | tf_op jit(solution)/shard_map/reduce_scatter | solution.py:171
  201.5 6.0 %copy-start.6 = (f32[5,64]{1,0:T(8,128)S(1)}, f32[5,64]{1,0:T(8,128)}, u32[]{:S(2)}) copy-start(f32[5,64]{1,0:T(8,128)} %param.18) | copy-start | bytes 3844
  202.0 4.9 collective-permute-start
  207.4 17.2 %copy-start.1 = (f32[5,65,128]{2,1,0:T(8,128)S(1)}, f32[5,65,128]{2,1,0:T(8,128)}, u32[]{:S(2)}) copy-start(f32[5,65,128]{2,1,0:T(8,128)} %constant.86.clone.1) | copy-start | bytes 499204
  209.1 13.7 %collective-permute-start.4 = (f32[5,65,128]{2,1,0:T(8,128)}, f32[5,65,128]{2,1,0:T(8,128)}, u32[]{:S(2)}, u32[]{:S(2)}) collective-permute-start(f32[5,65,128]{2,1,0:T(8,128)} %pad_maximum_fusion.1), channel_id=1, source_target_pairs={{0,64},{16,80},{32,96},{48,112},{64,128},{80,144},{96,160},{112,17... | collective-permute-start | bytes 499208 | tf_op jit(solution)/shard_map/ppermute | solution.py:12
  212.9 11.7 %collective-permute-start.3 = (f32[5,65,128]{2,1,0:T(8,128)}, f32[5,65,128]{2,1,0:T(8,128)S(1)}, u32[]{:S(2)}, u32[]{:S(2)}) collective-permute-start(f32[5,65,128]{2,1,0:T(8,128)} %pad_maximum_fusion.1), channel_id=1, source_target_pairs={{0,48},{16,64},{32,80},{48,96},{64,112},{80,128},{96,144},{112,160... | collective-permute-start | bytes 499208 | tf_op jit(solution)/shard_map/ppermute | solution.py:12
  214.8 13.9 %collective-permute-start.2 = (f32[5,65,128]{2,1,0:T(8,128)}, f32[5,65,128]{2,1,0:T(8,128)S(1)}, u32[]{:S(2)}, u32[]{:S(2)}) collective-permute-start(f32[5,65,128]{2,1,0:T(8,128)} %pad_maximum_fusion.1), channel_id=1, source_target_pairs={{0,32},{16,48},{32,64},{48,80},{64,96},{80,112},{96,128},{112,144}... | collective-permute-start | bytes 499208 | tf_op jit(solution)/shard_map/ppermute | solution.py:12
  220.9 8.6 %collective-permute-start.1 = (f32[5,65,128]{2,1,0:T(8,128)}, f32[5,65,128]{2,1,0:T(8,128)S(1)}, u32[]{:S(2)}, u32[]{:S(2)}) collective-permute-start(f32[5,65,128]{2,1,0:T(8,128)} %pad_maximum_fusion.1), channel_id=1, source_target_pairs={{0,16},{16,32},{32,48},{48,64},{64,80},{80,96},{96,112},{112,128},... | collective-permute-start | bytes 499208 | tf_op jit(solution)/shard_map/ppermute | solution.py:12
  229.6 10.8 %collective-permute-start.5 = (f32[5,65,128]{2,1,0:T(8,128)S(1)}, f32[5,65,128]{2,1,0:T(8,128)S(1)}, u32[]{:S(2)}, u32[]{:S(2)}) collective-permute-start(f32[5,65,128]{2,1,0:T(8,128)S(1)} %maximum_select_fusion.3), channel_id=1, source_target_pairs={{0,64},{16,80},{32,96},{48,112},{64,128},{80,144},{96,160},{112,17... | collective-permute-start | bytes 499208 | tf_op jit(solution)/shard_map/ppermute | solution.py:12
  233.7 8.8 %collective-permute-start.6 = (f32[5,65,128]{2,1,0:T(8,128)S(1)}, f32[5,65,128]{2,1,0:T(8,128)S(1)}, u32[]{:S(2)}, u32[]{:S(2)}) collective-permute-start(f32[5,65,128]{2,1,0:T(8,128)S(1)} %maximum_select_fusion.3), channel_id=1, source_target_pairs={{0,128},{16,144},{32,160},{48,176},{64,192},{80,208},{96,224},{112... | collective-permute-start | bytes 499208 | tf_op jit(solution)/shard_map/ppermute | solution.py:12
  235.0 9.6 %collective-permute-start.7 = (f32[5,65,128]{2,1,0:T(8,128)S(1)}, f32[5,65,128]{2,1,0:T(8,128)S(1)}, u32[]{:S(2)}, u32[]{:S(2)}) collective-permute-start(f32[5,65,128]{2,1,0:T(8,128)S(1)} %maximum_select_fusion.3), channel_id=1, source_target_pairs={{0,192},{16,208},{32,224},{48,240},{64,256},{80,272},{96,288},{112... | collective-permute-start | bytes 499208 | tf_op jit(solution)/shard_map/ppermute | solution.py:12
  244.7 12.9 %collective-permute-start.8 = (f32[5,65,128]{2,1,0:T(8,128)S(1)}, f32[5,65,128]{2,1,0:T(8,128)S(1)}, u32[]{:S(2)}, u32[]{:S(2)}) collective-permute-start(f32[5,65,128]{2,1,0:T(8,128)S(1)} %maximum_select_fusion.6), channel_id=1, source_target_pairs={{0,256},{16,272},{32,288},{48,304},{64,320},{80,336},{96,352},{112... | collective-permute-start | bytes 499208 | tf_op jit(solution)/shard_map/ppermute | solution.py:12
  246.6 14.8 %copy-start.9 = (f32[5]{0:T(128)S(1)}, f32[5]{0:T(128)}, u32[]{:S(2)}) copy-start(f32[5]{0:T(128)} %param.23) | copy-start | bytes 64
  246.6 12.8 %collective-permute-start.9 = (f32[5,65,128]{2,1,0:T(8,128)S(1)}, f32[5,65,128]{2,1,0:T(8,128)S(1)}, u32[]{:S(2)}, u32[]{:S(2)}) collective-permute-start(f32[5,65,128]{2,1,0:T(8,128)S(1)} %maximum_select_fusion.6), channel_id=1, source_target_pairs={{0,512},{16,528},{32,544},{48,560},{64,576},{80,592},{96,608},{112... | collective-permute-start | bytes 499208 | tf_op jit(solution)/shard_map/ppermute | solution.py:12
  256.3 5.0 collective-permute-start.10
  259.3 16.6 %copy-start.4 = (f32[5,64]{1,0:T(8,128)S(1)}, f32[5,64]{1,0:T(8,128)}, u32[]{:S(2)}) copy-start(f32[5,64]{1,0:T(8,128)} %param.24) | copy-start | bytes 3844
  261.7 14.2 %collective-permute-start.11 = (f32[256]{0:T(256)S(1)}, f32[256]{0:T(256)S(1)}, u32[]{:S(2)}, u32[]{:S(2)}) collective-permute-start(f32[256]{0:T(256)S(1)} %get-tuple-element.41), channel_id=1, source_target_pairs={{0,1},{1,0},{2,3},{3,2},{4,5},{5,4},{6,7},{7,6},{8,9},{9,8},{10,11... | collective-permute-start | bytes 3080 | tf_op jit(solution)/shard_map/ppermute | solution.py:163
Sparse Core Ops, SparseCore 0:
  25.3 171.4 reduce-scatter.6
  278.8 235.8 reduce-scatter.4

commit v3 on v2

--- a/solution.py
+++ b/solution.py
@@ -95,10 +95,14 @@
     slot_group = (
         row_first + jnp.arange(col_count, dtype=jnp.int32) * heads_dev
     ) // group_heads - group_start
-    bc_slots = jnp.zeros((tok_rows, col_count, 2 * state_width), jnp.float32)
-    for member in range(groups_row):
-        picked = (slot_group == member).astype(jnp.float32)
-        bc_slots = bc_slots + bc_part[:, member][:, None, :] * picked[None, :, None]
+    paired = group_heads == 2 * heads_dev and col_count == 2 * groups_row
+    if paired:
+        bc_slots = bc_part.reshape(tok_rows, col_count, state_width)
+    else:
+        bc_slots = jnp.zeros((tok_rows, col_count, 2 * state_width), jnp.float32)
+        for member in range(groups_row):
+            picked = (slot_group == member).astype(jnp.float32)
+            bc_slots = bc_slots + bc_part[:, member][:, None, :] * picked[None, :, None]
     xz_slots = xz_term.reshape(tok_rows, col_count, heads_dev * 2 * head_width)
     main = jnp.concatenate([xz_slots, bc_slots], axis=2)
     feat = main.shape[2]
@@ -113,6 +117,14 @@
     xz_width = heads_dev * 2 * head_width
     xz_sum = summed[:tok_rows, :xz_width].reshape(tok_rows, heads_dev, 2 * head_width)
     bc_pre = summed[:tok_rows, xz_width:]
+    if paired:
+        partner = [(c, c ^ 1) for c in range(col_count)]
+        other = lax.ppermute(bc_pre, "col", partner)
+        bc_pre = jnp.where(
+            col_index % 2 == 0,
+            jnp.concatenate([bc_pre, other], axis=1),
+            jnp.concatenate([other, bc_pre], axis=1),
+        )
     dt_raw = (
         summed[tok_rows:].reshape(-1)[: heads_dev * tok_rows]
         .reshape(heads_dev, tok_rows)
@@ -168,9 +180,10 @@
     mean_sq = group_sum / (group_heads * head_width)
     normed = (gated * lax.rsqrt(mean_sq + EPSILON)[:, None, None] * norm_gain).astype(jnp.bfloat16)
     partial_out = jnp.einsum("lhp,hpd->ld", normed, w_out, preferred_element_type=jnp.float32)
-    mixed = lax.psum_scatter(
-        partial_out.astype(jnp.bfloat16), ("row", "col"), scatter_dimension=1, tiled=True
-    )
+    by_row = lax.psum_scatter(
+        partial_out.astype(jnp.bfloat16), "row", scatter_dimension=1, tiled=True
+    )
+    mixed = lax.psum_scatter(by_row, "col", scatter_dimension=1, tiled=True)
     return mixed.astype(jnp.float32)
 
 

time: 524 us -> 432 us (0.82)
  waiting for transfers between devices: 433 us -> 318 us
  starting transfers between devices: 39.7 us -> 59.2 us
    unnamed x3, waiting for transfers between devices: 169 us -> 0.05 us
    reduce_scatter x1 -> x3, waiting for transfers between devices: 236 us -> 297 us  [the longest x1 147 us: body(): lax.psum_scatter(packed.astype(jnp.bfloat16), 'col', scatter_dimension=1,...]
    ppermute x0 -> x1, starting transfers between devices: none -> 11.6 us  [body(): other = lax.ppermute(bc_pre, 'col', partner)]
    ppermute x1, starting transfers between devices: 5.17 us -> 11 us  [body(): group_sum = squares + lax.ppermute(squares, 'col', partner)]
    ppermute x1, waiting for transfers between devices: 8.99 us -> 3.12 us  [body(): group_sum = squares + lax.ppermute(squares, 'col', partner)]
  transfers between devices with their start and end apart: 14 -> 16, of which waited for: 11 -> 12; matrix products, arithmetic and copies ran while one was open for 1% -> 2% of each run, Pallas kernels for 0% -> 0%
where the time goes in v3:
time: 432 us; the launch traced here: 430 us
  waiting for transfers between devices  318 us (74%)
  starting transfers between devices  59.2 us (14%)
  local copies, waits for them, and re-layouts  16.9 us (4%)
  between operations  13.7 us (3%)
  other arithmetic  11.9 us (3%)
  matrix products  10.7 us (2%)
    reduce_scatter x1, waiting for transfers between devices, body(): lax.psum_scatter(packed.astype(jnp.bfloat16), 'col', scatter_dimension=1,...  147 us
    reduce_scatter x1, waiting for transfers between devices, body(): mixed = lax.psum_scatter(by_row, 'col', scatter_dimension=1, tiled=True)  84 us
    reduce_scatter x1, waiting for transfers between devices, body(): lax.psum_scatter(partial_out.astype(jnp.bfloat16), 'row', scatter_dimensi...  66.4 us
    ppermute x11, starting transfers between devices, shifted(): return lax.ppermute(block, axis, route)  36.5 us
    ppermute x11, waiting for transfers between devices, shifted(): return lax.ppermute(block, axis, route)  17.4 us
    ppermute x1, starting transfers between devices, body(): other = lax.ppermute(bc_pre, 'col', partner)  11.6 us
    ppermute x1, starting transfers between devices, body(): group_sum = squares + lax.ppermute(squares, 'col', partner)  11 us
    unnamed x42, local copies, waits for them, and re-layouts  9.4 us
  transfers between devices with their start and end apart: 16, of which 12 were waited for; matrix products, arithmetic and copies ran while one was open for 2% of the time, Pallas kernels for 0%

profile of v3, /device:TPU:24, one launch (start us, length us, event | category | flops | bytes accessed | tf_op | source)
XLA Modules:
  0.0 430.5 jit_solution(17183265143311735966)
XLA Ops:
  6.5 8.1 %copy.57 = bf16[1024,20,128]{0,2,1:T(8,128)(2,1)} copy(bf16[1024,20,128]{2,0,1:T(8,128)(2,1)} %param.14) | data formatting | bytes 10485760 | tf_op args[1]
  14.6 5.2 %convolution_convert_fusion = bf16[256,4,640]{2,0,1:T(8,128)(2,1)} fusion(bf16[4,640,1024]{2,1,0:T(8,128)(2,1)} %bitcast.126, bf16[256,1024]{1,0:T(8,128)(2,1)S(1)} %copy-done.4), kind=kOutput, calls=%fused_computation.3 | convolution fusion | flops 1342832640 | bytes 7077888 | tf_op jit(solution)/shard_map/dot_general | solution.py:90
  22.6 2.6 pad_maximum_fusion
  27.1 1.3 constant_dynamic-slice_fusion.2
  28.5 147.0 %reduce-scatter.4.cloned.1.call-done = bf16[264,1,768]{2,0,1:T(8,128)(2,1)} async-done(((bf16[264,4,768]{2,0,1:T(8,128)(2,1)}), bf16[264,1,768]{2,0,1:T(8,128)(2,1)}) %reduce-scatter.4.cloned.1.call-update) | async-done | bytes 405520 | tf_op jit(solution)/shard_map/reduce_scatter | solution.py:115
  177.1 11.6 %collective-permute-start = (bf16[256,128]{1,0:T(8,128)(2,1)S(1)}, bf16[256,128]{1,0:T(8,128)(2,1)S(1)}, u32[]{:S(2)}, u32[]{:S(2)}) collective-permute-start(bf16[256,128]{1,0:T(8,128)(2,1)S(1)} %slice.293), channel_id=1, source_target_pairs={{0,1},{1,0},{2,3},{3,2},{4,5},{5,4},{6,7},{7,6},{8,9},{9,8},{10,11... | collective-permute-start | bytes 196616 | tf_op jit(solution)/shard_map/ppermute | solution.py:122
  189.4 1.5 reduce-window.6
  193.1 1.9 collective-permute-start.1
  195.6 2.5 collective-permute-done.1
  199.4 1.3 multiply_convert_fusion.3
  201.7 8.6 %collective-permute-start.5 = (f32[5,65,128]{2,1,0:T(8,128)S(1)}, f32[5,65,128]{2,1,0:T(8,128)}, u32[]{:S(2)}, u32[]{:S(2)}) collective-permute-start(f32[5,65,128]{2,1,0:T(8,128)S(1)} %pad_maximum_fusion.1), channel_id=1, source_target_pairs={{0,64},{16,80},{32,96},{48,112},{64,128},{80,144},{96,160},{112,17... | collective-permute-start | bytes 499208 | tf_op jit(solution)/shard_map/ppermute | solution.py:12
  210.4 2.4 collective-permute-start.4
  212.8 3.2 collective-permute-start.3
  216.0 2.4 collective-permute-start.2
  220.2 1.6 collective-permute-done.3
  221.9 2.3 collective-permute-done.2
  224.2 5.1 %collective-permute-start.6 = (f32[5,65,128]{2,1,0:T(8,128)S(1)}, f32[5,65,128]{2,1,0:T(8,128)S(1)}, u32[]{:S(2)}, u32[]{:S(2)}) collective-permute-start(f32[5,65,128]{2,1,0:T(8,128)S(1)} %maximum_select_fusion.3), channel_id=1, source_target_pairs={{0,64},{16,80},{32,96},{48,112},{64,128},{80,144},{96,160},{112,17... | collective-permute-start | bytes 499208 | tf_op jit(solution)/shard_map/ppermute | solution.py:12
  229.5 1.4 collective-permute-start.7
  231.0 4.1 collective-permute-start.8
  235.1 3.2 collective-permute-done.7
  238.4 2.1 collective-permute-done.8
  240.5 3.9 collective-permute-start.9
  245.0 2.2 collective-permute-start.10
  247.2 1.3 collective-permute-start.11
  249.5 3.0 collective-permute-done.10
  252.6 1.9 collective-permute-done.11
  254.9 11.0 %collective-permute-start.12 = (f32[256]{0:T(256)S(1)}, f32[256]{0:T(256)S(1)}, u32[]{:S(2)}, u32[]{:S(2)}) collective-permute-start(f32[256]{0:T(256)S(1)} %get-tuple-element.39), channel_id=1, source_target_pairs={{0,1},{1,0},{2,3},{3,2},{4,5},{5,4},{6,7},{7,6},{8,9},{9,8},{10,11... | collective-permute-start | bytes 3080 | tf_op jit(solution)/shard_map/ppermute | solution.py:175
  266.0 3.1 collective-permute-done.12
  269.1 2.7 fusion
  271.9 66.4 %reduce-scatter.6.cloned.1.call-done = bf16[256,1024]{1,0:T(8,128)(2,1)} async-done(((bf16[256,4096]{1,0:T(8,128)(2,1)}), bf16[256,1024]{1,0:T(8,128)(2,1)}) %reduce-scatter.6.cloned.1.call-update) | async-done | bytes 524304 | tf_op jit(solution)/shard_map/reduce_scatter | solution.py:183
  338.3 84.0 %reduce-scatter.8.cloned.1.call-done = bf16[256,256]{1,0:T(8,128)(2,1)} async-done(((bf16[256,1024]{1,0:T(8,128)(2,1)}), bf16[256,256]{1,0:T(8,128)(2,1)}) %reduce-scatter.8.cloned.1.call-update) | async-done | bytes 131088 | tf_op jit(solution)/shard_map/reduce_scatter | solution.py:186
  422.3 1.6 convert_element_type.55
  (127 shorter events, 16.2 us)
Async XLA Ops:
  6.5 262.6 %copy-start = (bf16[5,64,4096]{2,1,0:T(8,128)(2,1)S(1)}, bf16[5,64,4096]{2,1,0:T(8,128)(2,1)}, u32[]{:S(2)}) copy-start(bf16[5,64,4096]{2,1,0:T(8,128)(2,1)} %param.25) | copy-start | bytes 7864324
  6.5 8.1 %copy-start.4 = (bf16[256,1024]{1,0:T(8,128)(2,1)S(1)}, bf16[256,1024]{1,0:T(8,128)(2,1)}, u32[]{:S(2)}) copy-start(bf16[256,1024]{1,0:T(8,128)(2,1)} %param.13) | copy-start | bytes 1572868
  6.5 169.0 %reduce-scatter.4.cloned.1.call-start = ((), (), s32[]{:S(2)}) async-start(), calls=%async_computation.3 | async-start | bytes 2027520 | tf_op jit(solution)/shard_map/reduce_scatter | solution.py:115
  14.6 5.2 %copy-start.11 = (bf16[1024,2,256]{2,1,0:T(2,128)(2,1)S(1)}, bf16[1024,2,256]{2,1,0:T(2,128)(2,1)}, u32[]{:S(2)}) copy-start(bf16[1024,2,256]{2,1,0:T(2,128)(2,1)} %param.16) | copy-start | bytes 3145732
  19.8 2.4 copy-start.5
  25.2 0.7 copy-start.12
  25.2 3.3 copy-start.7
  25.2 163.5 %copy-start.9 = (f32[5]{0:T(128)S(1)}, f32[5]{0:T(128)}, u32[]{:S(2)}) copy-start(f32[5]{0:T(128)} %param.21) | copy-start | bytes 64
  25.2 313.0 %reduce-scatter.6.cloned.1.call-start = ((), (), s32[]{:S(2)}) async-start(), calls=%async_computation.4 | async-start | bytes 2621440 | tf_op jit(solution)/shard_map/reduce_scatter | solution.py:183
  177.1 15.9 %collective-permute-start = (bf16[256,128]{1,0:T(8,128)(2,1)S(1)}, bf16[256,128]{1,0:T(8,128)(2,1)S(1)}, u32[]{:S(2)}, u32[]{:S(2)}) collective-permute-start(bf16[256,128]{1,0:T(8,128)(2,1)S(1)} %slice.293), channel_id=1, source_target_pairs={{0,1},{1,0},{2,3},{3,2},{4,5},{5,4},{6,7},{7,6},{8,9},{9,8},{10,11... | collective-permute-start | bytes 196616 | tf_op jit(solution)/shard_map/ppermute | solution.py:122
  193.1 4.9 %collective-permute-start.1 = (bf16[3,576]{1,0:T(4,128)(2,1)S(1)}, bf16[3,576]{1,0:T(4,128)(2,1)S(1)}, u32[]{:S(2)}, u32[]{:S(2)}) collective-permute-start(bf16[3,576]{1,0:T(4,128)(2,1)S(1)} %pad_maximum_fusion.3), channel_id=1, source_target_pairs={{0,16},{16,32},{32,48},{48,64},{64,80},{80,96},{96,112},{112,128},... | collective-permute-start | bytes 10376 | tf_op jit(solution)/shard_map/ppermute | solution.py:12
  198.5 3.1 copy-start.10
  199.4 20.7 %copy-start.1 = (f32[5,65,128]{2,1,0:T(8,128)S(1)}, f32[5,65,128]{2,1,0:T(8,128)}, u32[]{:S(2)}) copy-start(f32[5,65,128]{2,1,0:T(8,128)} %constant.84.clone.1) | copy-start | bytes 499204
  200.7 0.7 copy-start.2
  201.7 16.7 %collective-permute-start.5 = (f32[5,65,128]{2,1,0:T(8,128)S(1)}, f32[5,65,128]{2,1,0:T(8,128)}, u32[]{:S(2)}, u32[]{:S(2)}) collective-permute-start(f32[5,65,128]{2,1,0:T(8,128)S(1)} %pad_maximum_fusion.1), channel_id=1, source_target_pairs={{0,64},{16,80},{32,96},{48,112},{64,128},{80,144},{96,160},{112,17... | collective-permute-start | bytes 499208 | tf_op jit(solution)/shard_map/ppermute | solution.py:12
  210.4 9.7 %collective-permute-start.4 = (f32[5,65,128]{2,1,0:T(8,128)S(1)}, f32[5,65,128]{2,1,0:T(8,128)S(1)}, u32[]{:S(2)}, u32[]{:S(2)}) collective-permute-start(f32[5,65,128]{2,1,0:T(8,128)S(1)} %pad_maximum_fusion.1), channel_id=1, source_target_pairs={{0,48},{16,64},{32,80},{48,96},{64,112},{80,128},{96,144},{112,160... | collective-permute-start | bytes 499208 | tf_op jit(solution)/shard_map/ppermute | solution.py:12
  212.8 9.0 %collective-permute-start.3 = (f32[5,65,128]{2,1,0:T(8,128)S(1)}, f32[5,65,128]{2,1,0:T(8,128)S(1)}, u32[]{:S(2)}, u32[]{:S(2)}) collective-permute-start(f32[5,65,128]{2,1,0:T(8,128)S(1)} %pad_maximum_fusion.1), channel_id=1, source_target_pairs={{0,32},{16,48},{32,64},{48,80},{64,96},{80,112},{96,128},{112,144}... | collective-permute-start | bytes 499208 | tf_op jit(solution)/shard_map/ppermute | solution.py:12
  216.0 8.1 %collective-permute-start.2 = (f32[5,65,128]{2,1,0:T(8,128)S(1)}, f32[5,65,128]{2,1,0:T(8,128)S(1)}, u32[]{:S(2)}, u32[]{:S(2)}) collective-permute-start(f32[5,65,128]{2,1,0:T(8,128)S(1)} %pad_maximum_fusion.1), channel_id=1, source_target_pairs={{0,16},{16,32},{32,48},{48,64},{64,80},{80,96},{96,112},{112,128},... | collective-permute-start | bytes 499208 | tf_op jit(solution)/shard_map/ppermute | solution.py:12
  224.2 10.8 %collective-permute-start.6 = (f32[5,65,128]{2,1,0:T(8,128)S(1)}, f32[5,65,128]{2,1,0:T(8,128)S(1)}, u32[]{:S(2)}, u32[]{:S(2)}) collective-permute-start(f32[5,65,128]{2,1,0:T(8,128)S(1)} %maximum_select_fusion.3), channel_id=1, source_target_pairs={{0,64},{16,80},{32,96},{48,112},{64,128},{80,144},{96,160},{112,17... | collective-permute-start | bytes 499208 | tf_op jit(solution)/shard_map/ppermute | solution.py:12
  229.5 14.9 %copy-start.3 = (bf16[256,5,64]{0,2,1:T(8,128)(2,1)S(1)}, bf16[256,5,64]{0,2,1:T(8,128)(2,1)}, u32[]{:S(2)}) copy-start(bf16[256,5,64]{0,2,1:T(8,128)(2,1)} %copy-done.2) | copy-start | bytes 491524
  229.5 14.9 %copy-start.8 = (f32[5,256]{1,0:T(8,128)S(1)}, f32[5,256]{1,0:T(8,128)}, u32[]{:S(2)}) copy-start(f32[5,256]{1,0:T(8,128)} %get-tuple-element.30) | copy-start | bytes 15364
  229.5 8.8 %collective-permute-start.7 = (f32[5,65,128]{2,1,0:T(8,128)S(1)}, f32[5,65,128]{2,1,0:T(8,128)S(1)}, u32[]{:S(2)}, u32[]{:S(2)}) collective-permute-start(f32[5,65,128]{2,1,0:T(8,128)S(1)} %maximum_select_fusion.3), channel_id=1, source_target_pairs={{0,128},{16,144},{32,160},{48,176},{64,192},{80,208},{96,224},{112... | collective-permute-start | bytes 499208 | tf_op jit(solution)/shard_map/ppermute | solution.py:12
  231.0 9.5 %collective-permute-start.8 = (f32[5,65,128]{2,1,0:T(8,128)S(1)}, f32[5,65,128]{2,1,0:T(8,128)S(1)}, u32[]{:S(2)}, u32[]{:S(2)}) collective-permute-start(f32[5,65,128]{2,1,0:T(8,128)S(1)} %maximum_select_fusion.3), channel_id=1, source_target_pairs={{0,192},{16,208},{32,224},{48,240},{64,256},{80,272},{96,288},{112... | collective-permute-start | bytes 499208 | tf_op jit(solution)/shard_map/ppermute | solution.py:12
  240.5 8.9 %collective-permute-start.9 = (f32[5,65,128]{2,1,0:T(8,128)S(1)}, f32[5,65,128]{2,1,0:T(8,128)S(1)}, u32[]{:S(2)}, u32[]{:S(2)}) collective-permute-start(f32[5,65,128]{2,1,0:T(8,128)S(1)} %maximum_select_fusion.6), channel_id=1, source_target_pairs={{0,256},{16,272},{32,288},{48,304},{64,320},{80,336},{96,352},{112... | collective-permute-start | bytes 499208 | tf_op jit(solution)/shard_map/ppermute | solution.py:12
  245.0 9.5 %copy-start.13 = (f32[5]{0:T(128)S(1)}, f32[5]{0:T(128)}, u32[]{:S(2)}) copy-start(f32[5]{0:T(128)} %param.23) | copy-start | bytes 64
  245.0 7.5 %collective-permute-start.10 = (f32[5,65,128]{2,1,0:T(8,128)S(1)}, f32[5,65,128]{2,1,0:T(8,128)S(1)}, u32[]{:S(2)}, u32[]{:S(2)}) collective-permute-start(f32[5,65,128]{2,1,0:T(8,128)S(1)} %maximum_select_fusion.6), channel_id=1, source_target_pairs={{0,512},{16,528},{32,544},{48,560},{64,576},{80,592},{96,608},{112... | collective-permute-start | bytes 499208 | tf_op jit(solution)/shard_map/ppermute | solution.py:12
  247.2 7.2 %collective-permute-start.11 = (f32[5,65,128]{2,1,0:T(8,128)S(1)}, f32[5,65,128]{2,1,0:T(8,128)S(1)}, u32[]{:S(2)}, u32[]{:S(2)}) collective-permute-start(f32[5,65,128]{2,1,0:T(8,128)S(1)} %maximum_select_fusion.6), channel_id=1, source_target_pairs={{0,768},{16,784},{32,800},{48,816},{64,832},{80,848},{96,864},{112... | collective-permute-start | bytes 499208 | tf_op jit(solution)/shard_map/ppermute | solution.py:12
  252.6 16.5 %copy-start.6 = (f32[5,64]{1,0:T(8,128)S(1)}, f32[5,64]{1,0:T(8,128)}, u32[]{:S(2)}) copy-start(f32[5,64]{1,0:T(8,128)} %param.24) | copy-start | bytes 3844
  254.9 14.2 %collective-permute-start.12 = (f32[256]{0:T(256)S(1)}, f32[256]{0:T(256)S(1)}, u32[]{:S(2)}, u32[]{:S(2)}) collective-permute-start(f32[256]{0:T(256)S(1)} %get-tuple-element.39), channel_id=1, source_target_pairs={{0,1},{1,0},{2,3},{3,2},{4,5},{5,4},{6,7},{7,6},{8,9},{9,8},{10,11... | collective-permute-start | bytes 3080 | tf_op jit(solution)/shard_map/ppermute | solution.py:175
  271.9 150.5 %reduce-scatter.8.cloned.1.call-start = ((), (), s32[]{:S(2)}) async-start(), calls=%async_computation.5 | async-start | bytes 655360 | tf_op jit(solution)/shard_map/reduce_scatter | solution.py:186
Sparse Core Ops, SparseCore 0:
  25.4 150.1 reduce-scatter.3
  272.0 66.2 reduce-scatter.5
  341.7 80.6 reduce-scatter.7

commit v4 on v2

--- a/solution.py
+++ b/solution.py
@@ -99,40 +99,46 @@
     for member in range(groups_row):
         picked = (slot_group == member).astype(jnp.float32)
         bc_slots = bc_slots + bc_part[:, member][:, None, :] * picked[None, :, None]
-    xz_slots = xz_term.reshape(tok_rows, col_count, heads_dev * 2 * head_width)
-    main = jnp.concatenate([xz_slots, bc_slots], axis=2)
-    feat = main.shape[2]
+    xz_slots = xz_term.reshape(tok_rows, col_count, heads_dev, 2 * head_width)
+    x_width = heads_dev * head_width
+    first = jnp.concatenate(
+        [xz_slots[..., :head_width].reshape(tok_rows, col_count, x_width), bc_slots[..., :state_width]],
+        axis=2,
+    )
+    feat = first.shape[2]
     dt_flat = dt_term.reshape(tok_rows, col_count, heads_dev).transpose(1, 2, 0).reshape(col_count, -1)
     dt_rows = -(-dt_flat.shape[1] // (8 * feat)) * 8
     dt_flat = jnp.pad(dt_flat, ((0, 0), (0, dt_rows * feat - dt_flat.shape[1])))
     dt_block = dt_flat.reshape(col_count, dt_rows, feat).transpose(1, 0, 2)
-    packed = jnp.concatenate([main, dt_block], axis=0)
+    first = jnp.concatenate([first, dt_block], axis=0)
+    second = jnp.concatenate(
+        [xz_slots[..., head_width:].reshape(tok_rows, col_count, x_width), bc_slots[..., state_width:]],
+        axis=2,
+    )
     summed = lax.optimization_barrier(
-        lax.psum_scatter(packed.astype(jnp.bfloat16), "col", scatter_dimension=1, tiled=True)
+        lax.psum_scatter(first.astype(jnp.bfloat16), "col", scatter_dimension=1, tiled=True)
     )[:, 0]
-    xz_width = heads_dev * 2 * head_width
-    xz_sum = summed[:tok_rows, :xz_width].reshape(tok_rows, heads_dev, 2 * head_width)
-    bc_pre = summed[:tok_rows, xz_width:]
+    summed_late = lax.optimization_barrier(
+        lax.psum_scatter(second.astype(jnp.bfloat16), "col", scatter_dimension=1, tiled=True)
+    )[:, 0]
+    x_pre = summed[:tok_rows, :x_width].reshape(tok_rows, heads_dev, head_width)
+    b_pre = summed[:tok_rows, x_width:]
     dt_raw = (
         summed[tok_rows:].reshape(-1)[: heads_dev * tok_rows]
         .reshape(heads_dev, tok_rows)
         .T.astype(jnp.float32)
     )
-    x_pre = xz_sum[:, :, :head_width]
-    gate_z = xz_sum[:, :, head_width:]
     edge_len = conv_x.shape[0] - 1
     edge = jnp.concatenate(
-        [x_pre[tok_rows - edge_len :].reshape(edge_len, -1), bc_pre[tok_rows - edge_len :]], axis=1
+        [x_pre[tok_rows - edge_len :].reshape(edge_len, -1), b_pre[tok_rows - edge_len :]], axis=1
     )
     edge = shifted(edge, "ctx", 1)
-    x_edge = edge[:, : heads_dev * head_width].reshape(edge_len, heads_dev, head_width)
-    bc_edge = edge[:, heads_dev * head_width :]
+    x_edge = edge[:, :x_width].reshape(edge_len, heads_dev, head_width)
+    b_edge = edge[:, x_width:]
     x_conv = causal_conv(x_edge, x_pre, conv_x, conv_x_bias)
     bc_kernel = lax.dynamic_index_in_dim(conv_bc, own_group, 1, keepdims=False)
     bc_offset = lax.dynamic_index_in_dim(conv_bc_bias, own_group, 0, keepdims=False)
-    bc_conv = causal_conv(bc_edge, bc_pre, bc_kernel, bc_offset)
-    b_input = bc_conv[:, :state_width]
-    c_output = bc_conv[:, state_width:]
+    b_input = causal_conv(b_edge, b_pre, bc_kernel[:, :state_width], bc_offset[:state_width])
     step_size = jax.nn.softplus(dt_raw + dt_bias)
     cumul = jnp.cumsum(step_size * jnp.exp(a_log), axis=0)
     cum_heads = cumul.T
@@ -140,14 +146,19 @@
     positions = jnp.arange(tok_rows)
     causal = (positions[:, None] >= positions[None, :])[None]
     decay = jnp.where(causal, jnp.exp(-jnp.where(causal, diff, 0.0)), 0.0)
-    scores = jnp.einsum("tn,sn->ts", c_output, b_input, preferred_element_type=jnp.float32)
-    mixing = (scores[None] * decay * step_size.T[:, None, :]).astype(jnp.bfloat16)
-    y_intra = jnp.einsum("hts,shp->thp", mixing, x_conv, preferred_element_type=jnp.float32)
     tail = jnp.exp(-(cumul[-1][None, :] - cumul))
     scaled = ((tail * step_size)[:, :, None] * x_conv.astype(jnp.float32)).astype(jnp.bfloat16)
     local = jnp.einsum("shp,sn->hpn", scaled, b_input, preferred_element_type=jnp.float32)
     fall = jnp.exp(-cumul[-1])
     _, state_in = entering(fall, local, "ctx")
+    state_in, summed_late = lax.optimization_barrier((state_in, summed_late))
+    gate_z = summed_late[:, :x_width].reshape(tok_rows, heads_dev, head_width)
+    c_pre = summed_late[:, x_width:]
+    c_edge = shifted(c_pre[tok_rows - edge_len :], "ctx", 1)
+    c_output = causal_conv(c_edge, c_pre, bc_kernel[:, state_width:], bc_offset[state_width:])
+    scores = jnp.einsum("tn,sn->ts", c_output, b_input, preferred_element_type=jnp.float32)
+    mixing = (scores[None] * decay * step_size.T[:, None, :]).astype(jnp.bfloat16)
+    y_intra = jnp.einsum("hts,shp->thp", mixing, x_conv, preferred_element_type=jnp.float32)
     carried = jnp.einsum(
         "tn,hpn->thp", c_output.astype(jnp.float32), state_in, precision=lax.Precision.HIGHEST
     )
@@ -168,9 +179,10 @@
     mean_sq = group_sum / (group_heads * head_width)
     normed = (gated * lax.rsqrt(mean_sq + EPSILON)[:, None, None] * norm_gain).astype(jnp.bfloat16)
     partial_out = jnp.einsum("lhp,hpd->ld", normed, w_out, preferred_element_type=jnp.float32)
-    mixed = lax.psum_scatter(
-        partial_out.astype(jnp.bfloat16), ("row", "col"), scatter_dimension=1, tiled=True
-    )
+    by_row = lax.psum_scatter(
+        partial_out.astype(jnp.bfloat16), "row", scatter_dimension=1, tiled=True
+    )
+    mixed = lax.psum_scatter(by_row, "col", scatter_dimension=1, tiled=True)
     return mixed.astype(jnp.float32)
 
 

time: 524 us -> 486 us (0.927)
  waiting for transfers between devices: 433 us -> 374 us
  local copies, waits for them, and re-layouts: 14.7 us -> 24.4 us
  other arithmetic: 10.4 us -> 16.6 us
    unnamed x3 -> x4, waiting for transfers between devices: 169 us -> 0.07 us
    reduce_scatter x1 -> x4, waiting for transfers between devices: 236 us -> 353 us  [the longest x1 136 us: body(): lax.psum_scatter(first.astype(jnp.bfloat16), 'col', scatter_dimension=1,...]
    ppermute x11 -> x12, waiting for transfers between devices: 18.4 us -> 12.7 us  [shifted(): return lax.ppermute(block, axis, route)]
    ppermute x11 -> x12, starting transfers between devices: 34.5 us -> 37.9 us  [shifted(): return lax.ppermute(block, axis, route)]
  transfers between devices with their start and end apart: 14 -> 17, of which waited for: 11 -> 13; matrix products, arithmetic and copies ran while one was open for 1% -> 3% of each run, Pallas kernels for 0% -> 0%
where the time goes in v4:
time: 486 us; the launch traced here: 484 us
  waiting for transfers between devices  374 us (77%)
  starting transfers between devices  44 us (9%)
  local copies, waits for them, and re-layouts  24.4 us (5%)
  other arithmetic  16.6 us (3%)
  between operations  13.8 us (3%)
  matrix products  10.9 us (2%)
    reduce_scatter x1, waiting for transfers between devices, body(): lax.psum_scatter(first.astype(jnp.bfloat16), 'col', scatter_dimension=1,...  136 us
    reduce_scatter x1, waiting for transfers between devices, body(): mixed = lax.psum_scatter(by_row, 'col', scatter_dimension=1, tiled=True)  83.8 us
    reduce_scatter x1, waiting for transfers between devices, body(): lax.psum_scatter(second.astype(jnp.bfloat16), 'col', scatter_dimension=1,...  80 us
    reduce_scatter x1, waiting for transfers between devices, body(): lax.psum_scatter(partial_out.astype(jnp.bfloat16), 'row', scatter_dimensi...  53.2 us
    ppermute x12, starting transfers between devices, shifted(): return lax.ppermute(block, axis, route)  37.9 us
    ppermute x12, waiting for transfers between devices, shifted(): return lax.ppermute(block, axis, route)  12.7 us
  transfers between devices with their start and end apart: 17, of which 13 were waited for; matrix products, arithmetic and copies ran while one was open for 3% of the time, Pallas kernels for 0%

profile of v4, /device:TPU:24, one launch (start us, length us, event | category | flops | bytes accessed | tf_op | source)
XLA Modules:
  0.0 483.8 jit_solution(812488691600306242)
XLA Ops:
  6.6 2.0 fusion.4
  9.8 8.0 %copy.67 = bf16[1024,20,128]{0,2,1:T(8,128)(2,1)} copy(bf16[1024,20,128]{2,0,1:T(8,128)(2,1)} %param.14) | data formatting | bytes 10485760 | tf_op args[1]
  17.8 4.0 convolution_convert_fusion
  25.2 1.4 reshape.134
  26.6 1.8 copy.71
  28.4 2.5 pad_maximum_fusion
  32.4 1.3 slice_bitcast_fusion.10
  33.8 136.2 %reduce-scatter.5.cloned.1.call-done = bf16[264,1,448]{0,2,1:T(8,128)(2,1)} async-done(((bf16[264,4,448]{0,2,1:T(8,128)(2,1)}), bf16[264,1,448]{0,2,1:T(8,128)(2,1)}) %reduce-scatter.5.cloned.1.call-update) | async-done | bytes 236560 | tf_op jit(solution)/shard_map/reduce_scatter | solution.py:119
  171.9 1.9 collective-permute-start
  174.7 1.5 reduce-window.6
  184.3 1.9 collective-permute-start.4
  186.2 2.5 collective-permute-start.3
  188.7 3.5 collective-permute-start.2
  192.2 1.9 collective-permute-start.1
  197.4 2.4 collective-permute-done.2
  200.8 4.7 collective-permute-start.5
  206.6 3.0 collective-permute-start.6
  209.6 5.2 %collective-permute-start.7 = (f32[5,65,128]{2,1,0:T(8,128)S(1)}, f32[5,65,128]{2,1,0:T(8,128)S(1)}, u32[]{:S(2)}, u32[]{:S(2)}) collective-permute-start(f32[5,65,128]{2,1,0:T(8,128)S(1)} %maximum_select_fusion.3), channel_id=1, source_target_pairs={{0,192},{16,208},{32,224},{48,240},{64,256},{80,272},{96,288},{112... | collective-permute-start | bytes 499208 | tf_op jit(solution)/shard_map/ppermute | solution.py:12
  216.7 1.3 collective-permute-done.7
  218.0 7.6 %collective-permute-start.8 = (f32[5,65,128]{2,1,0:T(8,128)S(1)}, f32[5,65,128]{2,1,0:T(8,128)}, u32[]{:S(2)}, u32[]{:S(2)}) collective-permute-start(f32[5,65,128]{2,1,0:T(8,128)S(1)} %maximum_select_fusion.6), channel_id=1, source_target_pairs={{0,256},{16,272},{32,288},{48,304},{64,320},{80,336},{96,352},{112... | collective-permute-start | bytes 499208 | tf_op jit(solution)/shard_map/ppermute | solution.py:12
  225.6 80.0 %reduce-scatter.7.cloned.1.call-done = bf16[256,1,448]{0,2,1:T(8,128)(2,1)} async-done(((bf16[256,4,448]{0,2,1:T(8,128)(2,1)}), bf16[256,1,448]{0,2,1:T(8,128)(2,1)}) %reduce-scatter.7.cloned.1.call-update) | async-done | bytes 229392 | tf_op jit(solution)/shard_map/reduce_scatter | solution.py:122
  305.6 1.4 collective-permute-start.9
  307.0 2.3 collective-permute-start.10
  311.8 2.8 collective-permute-done.10
  314.7 1.9 collective-permute-start.11
  316.7 3.2 collective-permute-done.11
  321.6 6.0 %collective-permute-start.12 = (f32[256]{0:T(256)S(1)}, f32[256]{0:T(256)S(1)}, u32[]{:S(2)}, u32[]{:S(2)}) collective-permute-start(f32[256]{0:T(256)S(1)} %get-tuple-element.55), channel_id=1, source_target_pairs={{0,1},{1,0},{2,3},{3,2},{4,5},{5,4},{6,7},{7,6},{8,9},{9,8},{10,11... | collective-permute-start | bytes 3080 | tf_op jit(solution)/shard_map/ppermute | solution.py:174
  327.6 8.2 %collective-permute-done.12 = f32[256]{0:T(256)S(1)} collective-permute-done((f32[256]{0:T(256)S(1)}, f32[256]{0:T(256)S(1)}, u32[]{:S(2)}, u32[]{:S(2)}) %collective-permute-start.12) | collective-permute-done | bytes 1056 | tf_op jit(solution)/shard_map/ppermute | solution.py:174
  335.8 2.7 fusion
  338.6 53.2 %reduce-scatter.9.cloned.1.call-done = bf16[256,1024]{1,0:T(8,128)(2,1)} async-done(((bf16[256,4096]{1,0:T(8,128)(2,1)}), bf16[256,1024]{1,0:T(8,128)(2,1)}) %reduce-scatter.9.cloned.1.call-update) | async-done | bytes 524304 | tf_op jit(solution)/shard_map/reduce_scatter | solution.py:182
  391.9 83.8 %reduce-scatter.11.cloned.1.call-done = bf16[256,256]{1,0:T(8,128)(2,1)} async-done(((bf16[256,1024]{1,0:T(8,128)(2,1)}), bf16[256,256]{1,0:T(8,128)(2,1)}) %reduce-scatter.11.cloned.1.call-update) | async-done | bytes 131088 | tf_op jit(solution)/shard_map/reduce_scatter | solution.py:185
  475.7 1.6 convert_element_type.84
  (153 shorter events, 28.2 us)
Async XLA Ops:
  6.5 329.3 %copy-start = (bf16[5,64,4096]{2,1,0:T(8,128)(2,1)S(1)}, bf16[5,64,4096]{2,1,0:T(8,128)(2,1)}, u32[]{:S(2)}) copy-start(bf16[5,64,4096]{2,1,0:T(8,128)(2,1)} %param.25) | copy-start | bytes 7864324
  6.5 163.4 %reduce-scatter.5.cloned.1.call-start = ((), (), s32[]{:S(2)}) async-start(), calls=%async_computation.4 | async-start | bytes 1720320 | tf_op jit(solution)/shard_map/reduce_scatter | solution.py:119
  9.8 8.0 %copy-start.5 = (bf16[256,1024]{1,0:T(8,128)(2,1)S(1)}, bf16[256,1024]{1,0:T(8,128)(2,1)}, u32[]{:S(2)}) copy-start(bf16[256,1024]{1,0:T(8,128)(2,1)} %param.13) | copy-start | bytes 1572868
  30.9 143.1 %copy-start.14 = (f32[5]{0:T(128)S(1)}, f32[5]{0:T(128)}, u32[]{:S(2)}) copy-start(f32[5]{0:T(128)} %param.21) | copy-start | bytes 64
  30.9 151.1 %copy-start.13 = (f32[5,64]{1,0:T(8,128)S(1)}, f32[5,64]{1,0:T(8,128)}, u32[]{:S(2)}) copy-start(f32[5,64]{1,0:T(8,128)} %param.18) | copy-start | bytes 3844
  30.9 274.6 %reduce-scatter.7.cloned.1.call-start = ((), (), s32[]{:S(2)}) async-start(), calls=%async_computation.5 | async-start | bytes 1146880 | tf_op jit(solution)/shard_map/reduce_scatter | solution.py:122
  171.9 7.3 %collective-permute-start = (bf16[3,448]{0,1:T(8,128)(2,1)S(1)}, bf16[3,448]{0,1:T(8,128)(2,1)}, u32[]{:S(2)}, u32[]{:S(2)}) collective-permute-start(bf16[3,448]{0,1:T(8,128)(2,1)S(1)} %slice_bitcast_fusion.2), channel_id=1, source_target_pairs={{0,16},{16,32},{32,48},{48,64},{64,80},{80,96},{96,112},{112,128},... | collective-permute-start | bytes 8072 | tf_op jit(solution)/shard_map/ppermute | solution.py:12
  180.9 16.0 %copy-start.2 = (f32[5,65,128]{2,1,0:T(8,128)S(1)}, f32[5,65,128]{2,1,0:T(8,128)}, u32[]{:S(2)}) copy-start(f32[5,65,128]{2,1,0:T(8,128)} %constant.87.clone.1) | copy-start | bytes 499204
  184.3 11.0 %collective-permute-start.4 = (f32[5,65,128]{2,1,0:T(8,128)}, f32[5,65,128]{2,1,0:T(8,128)}, u32[]{:S(2)}, u32[]{:S(2)}) collective-permute-start(f32[5,65,128]{2,1,0:T(8,128)} %pad_maximum_fusion.2), channel_id=1, source_target_pairs={{0,64},{16,80},{32,96},{48,112},{64,128},{80,144},{96,160},{112,17... | collective-permute-start | bytes 499208 | tf_op jit(solution)/shard_map/ppermute | solution.py:12
  186.2 11.2 %collective-permute-start.3 = (f32[5,65,128]{2,1,0:T(8,128)}, f32[5,65,128]{2,1,0:T(8,128)S(1)}, u32[]{:S(2)}, u32[]{:S(2)}) collective-permute-start(f32[5,65,128]{2,1,0:T(8,128)} %pad_maximum_fusion.2), channel_id=1, source_target_pairs={{0,48},{16,64},{32,80},{48,96},{64,112},{80,128},{96,144},{112,160... | collective-permute-start | bytes 499208 | tf_op jit(solution)/shard_map/ppermute | solution.py:12
  188.7 11.2 %collective-permute-start.2 = (f32[5,65,128]{2,1,0:T(8,128)}, f32[5,65,128]{2,1,0:T(8,128)S(1)}, u32[]{:S(2)}, u32[]{:S(2)}) collective-permute-start(f32[5,65,128]{2,1,0:T(8,128)} %pad_maximum_fusion.2), channel_id=1, source_target_pairs={{0,32},{16,48},{32,64},{48,80},{64,96},{80,112},{96,128},{112,144}... | collective-permute-start | bytes 499208 | tf_op jit(solution)/shard_map/ppermute | solution.py:12
  192.2 8.6 %collective-permute-start.1 = (f32[5,65,128]{2,1,0:T(8,128)}, f32[5,65,128]{2,1,0:T(8,128)S(1)}, u32[]{:S(2)}, u32[]{:S(2)}) collective-permute-start(f32[5,65,128]{2,1,0:T(8,128)} %pad_maximum_fusion.2), channel_id=1, source_target_pairs={{0,16},{16,32},{32,48},{48,64},{64,80},{80,96},{96,112},{112,128},... | collective-permute-start | bytes 499208 | tf_op jit(solution)/shard_map/ppermute | solution.py:12
  196.9 8.6 %copy-start.1 = (bf16[256,4,128]{0,2,1:T(8,128)(2,1)S(1)}, bf16[256,4,128]{0,2,1:T(8,128)(2,1)}, u32[]{:S(2)}) copy-start(bf16[256,4,128]{0,2,1:T(8,128)(2,1)} %get-tuple-element.11) | copy-start | bytes 786436
  200.8 14.1 %collective-permute-start.5 = (f32[5,65,128]{2,1,0:T(8,128)S(1)}, f32[5,65,128]{2,1,0:T(8,128)}, u32[]{:S(2)}, u32[]{:S(2)}) collective-permute-start(f32[5,65,128]{2,1,0:T(8,128)S(1)} %maximum_select_fusion.3), channel_id=1, source_target_pairs={{0,64},{16,80},{32,96},{48,112},{64,128},{80,144},{96,160},{112,17... | collective-permute-start | bytes 499208 | tf_op jit(solution)/shard_map/ppermute | solution.py:12
  206.5 185.3 %reduce-scatter.9.cloned.1.call-start = ((), (), s32[]{:S(2)}) async-start(), calls=%async_computation.6 | async-start | bytes 2621440 | tf_op jit(solution)/shard_map/reduce_scatter | solution.py:182
  206.6 10.0 %collective-permute-start.6 = (f32[5,65,128]{2,1,0:T(8,128)S(1)}, f32[5,65,128]{2,1,0:T(8,128)S(1)}, u32[]{:S(2)}, u32[]{:S(2)}) collective-permute-start(f32[5,65,128]{2,1,0:T(8,128)S(1)} %maximum_select_fusion.3), channel_id=1, source_target_pairs={{0,128},{16,144},{32,160},{48,176},{64,192},{80,208},{96,224},{112... | collective-permute-start | bytes 499208 | tf_op jit(solution)/shard_map/ppermute | solution.py:12
  209.6 8.3 %collective-permute-start.7 = (f32[5,65,128]{2,1,0:T(8,128)S(1)}, f32[5,65,128]{2,1,0:T(8,128)S(1)}, u32[]{:S(2)}, u32[]{:S(2)}) collective-permute-start(f32[5,65,128]{2,1,0:T(8,128)S(1)} %maximum_select_fusion.3), channel_id=1, source_target_pairs={{0,192},{16,208},{32,224},{48,240},{64,256},{80,272},{96,288},{112... | collective-permute-start | bytes 499208 | tf_op jit(solution)/shard_map/ppermute | solution.py:12
  218.0 91.3 %collective-permute-start.8 = (f32[5,65,128]{2,1,0:T(8,128)S(1)}, f32[5,65,128]{2,1,0:T(8,128)}, u32[]{:S(2)}, u32[]{:S(2)}) collective-permute-start(f32[5,65,128]{2,1,0:T(8,128)S(1)} %maximum_select_fusion.6), channel_id=1, source_target_pairs={{0,256},{16,272},{32,288},{48,304},{64,320},{80,336},{96,352},{112... | collective-permute-start | bytes 499208 | tf_op jit(solution)/shard_map/ppermute | solution.py:12
  305.6 9.1 %copy-start.7 = (bf16[256,1,448]{0,2,1:T(8,128)(2,1)S(1)}, bf16[256,1,448]{0,2,1:T(8,128)(2,1)}, u32[]{:S(2)}) copy-start(bf16[256,1,448]{0,2,1:T(8,128)(2,1)} %reduce-scatter.7.cloned.1.call-done) | copy-start | bytes 688132
  305.6 6.2 %collective-permute-start.9 = (f32[5,65,128]{2,1,0:T(8,128)S(1)}, f32[5,65,128]{2,1,0:T(8,128)S(1)}, u32[]{:S(2)}, u32[]{:S(2)}) collective-permute-start(f32[5,65,128]{2,1,0:T(8,128)S(1)} %maximum_select_fusion.6), channel_id=1, source_target_pairs={{0,512},{16,528},{32,544},{48,560},{64,576},{80,592},{96,608},{112... | collective-permute-start | bytes 499208 | tf_op jit(solution)/shard_map/ppermute | solution.py:12
  307.0 7.6 %collective-permute-start.10 = (f32[5,65,128]{2,1,0:T(8,128)S(1)}, f32[5,65,128]{2,1,0:T(8,128)S(1)}, u32[]{:S(2)}, u32[]{:S(2)}) collective-permute-start(f32[5,65,128]{2,1,0:T(8,128)S(1)} %maximum_select_fusion.6), channel_id=1, source_target_pairs={{0,768},{16,784},{32,800},{48,816},{64,832},{80,848},{96,864},{112... | collective-permute-start | bytes 499208 | tf_op jit(solution)/shard_map/ppermute | solution.py:12
  311.0 9.1 %copy-start.15 = (f32[128]{0:T(128)S(1)}, f32[128]{0:T(128)}, u32[]{:S(2)}) copy-start(f32[128]{0:T(128)} %get-tuple-element.47) | copy-start | bytes 1540
  311.0 9.1 %copy-start.16 = (f32[128]{0:T(128)S(1)}, f32[128]{0:T(128)}, u32[]{:S(2)}) copy-start(f32[128]{0:T(128)} %get-tuple-element.48) | copy-start | bytes 1540
  311.0 9.1 %copy-start.17 = (f32[128]{0:T(128)S(1)}, f32[128]{0:T(128)}, u32[]{:S(2)}) copy-start(f32[128]{0:T(128)} %get-tuple-element.49) | copy-start | bytes 1540
  311.0 9.1 %copy-start.18 = (f32[128]{0:T(128)S(1)}, f32[128]{0:T(128)}, u32[]{:S(2)}) copy-start(f32[128]{0:T(128)} %get-tuple-element.50) | copy-start | bytes 1540
  311.0 9.1 %copy-start.19 = (f32[128]{0:T(128)S(1)}, f32[128]{0:T(128)}, u32[]{:S(2)}) copy-start(f32[128]{0:T(128)} %get-tuple-element.64) | copy-start | bytes 1540
  311.8 8.9 %copy-start.4 = (bf16[256,5,64]{0,2,1:T(8,128)(2,1)S(1)}, bf16[256,5,64]{0,2,1:T(8,128)(2,1)}, u32[]{:S(2)}) copy-start(bf16[256,5,64]{0,2,1:T(8,128)(2,1)} %copy-done.3) | copy-start | bytes 491524
  311.8 8.9 %copy-start.11 = (f32[5,256]{1,0:T(8,128)S(1)}, f32[5,256]{1,0:T(8,128)}, u32[]{:S(2)}) copy-start(f32[5,256]{1,0:T(8,128)} %get-tuple-element.40) | copy-start | bytes 15364
  314.7 5.2 %collective-permute-start.11 = (bf16[3,128]{0,1:T(8,128)(2,1)S(1)}, bf16[3,128]{0,1:T(8,128)(2,1)S(1)}, u32[]{:S(2)}, u32[]{:S(2)}) collective-permute-start(bf16[3,128]{0,1:T(8,128)(2,1)S(1)} %slice.352), channel_id=1, source_target_pairs={{0,16},{16,32},{32,48},{48,64},{64,80},{80,96},{96,112},{112,128},... | collective-permute-start | bytes 2312 | tf_op jit(solution)/shard_map/ppermute | solution.py:12
  321.2 14.6 %copy-start.9 = (f32[5,64]{1,0:T(8,128)S(1)}, f32[5,64]{1,0:T(8,128)}, u32[]{:S(2)}) copy-start(f32[5,64]{1,0:T(8,128)} %param.24) | copy-start | bytes 3844
  321.6 14.2 %collective-permute-start.12 = (f32[256]{0:T(256)S(1)}, f32[256]{0:T(256)S(1)}, u32[]{:S(2)}, u32[]{:S(2)}) collective-permute-start(f32[256]{0:T(256)S(1)} %get-tuple-element.55), channel_id=1, source_target_pairs={{0,1},{1,0},{2,3},{3,2},{4,5},{5,4},{6,7},{7,6},{8,9},{9,8},{10,11... | collective-permute-start | bytes 3080 | tf_op jit(solution)/shard_map/ppermute | solution.py:174
  338.6 137.1 %reduce-scatter.11.cloned.1.call-start = ((), (), s32[]{:S(2)}) async-start(), calls=%async_computation.7 | async-start | bytes 655360 | tf_op jit(solution)/shard_map/reduce_scatter | solution.py:185
  (6 other events, 10.0 us)
Sparse Core Ops, SparseCore 0:
  31.0 138.8 reduce-scatter.4
  206.7 98.8 reduce-scatter.6
  338.7 53.1 reduce-scatter.8
  395.1 80.5 reduce-scatter.10

commit v5 on v3

--- a/solution.py
+++ b/solution.py
@@ -10,6 +10,10 @@
     devices = range(lax.axis_size(axis))
     route = [(i - distance, i) for i in devices if i - distance in devices]
     return lax.ppermute(block, axis, route)
+
+
+def shifted_narrow(block, axis, distance):
+    return shifted(block.astype(jnp.bfloat16), axis, distance).astype(block.dtype)
 
 
 def causal_conv(edge_rows, own_rows, weights, bias):
@@ -45,11 +49,11 @@
     acc = identity
     for distance in range(radix, 0, -1):
         if distance < size:
-            got = shifted(own, axis, distance)
+            got = shifted_narrow(own, axis, distance)
             acc = jnp.where(mine >= distance, join(acc, got), acc)
     span = radix
     while span < size:
-        parts = [(step * span, shifted(acc, axis, step * span)) for step in range(1, radix) if step * span < size]
+        parts = [(step * span, shifted_narrow(acc, axis, step * span)) for step in range(1, radix) if step * span < size]
         total = acc
         for distance, got in parts:
             total = jnp.where(mine >= distance, join(got, total), total)
@@ -180,9 +184,14 @@
     mean_sq = group_sum / (group_heads * head_width)
     normed = (gated * lax.rsqrt(mean_sq + EPSILON)[:, None, None] * norm_gain).astype(jnp.bfloat16)
     partial_out = jnp.einsum("lhp,hpd->ld", normed, w_out, preferred_element_type=jnp.float32)
-    by_row = lax.psum_scatter(
-        partial_out.astype(jnp.bfloat16), "row", scatter_dimension=1, tiled=True
-    )
+    row_index = lax.axis_index("row")
+    shares = partial_out.astype(jnp.bfloat16).reshape(tok_rows, row_count, -1)
+    by_row = lax.dynamic_index_in_dim(shares, row_index, 1, keepdims=False).astype(jnp.float32)
+    for step in range(1, row_count):
+        sent = lax.dynamic_index_in_dim(shares, (row_index + step) % row_count, 1, keepdims=False)
+        route = [(j, (j + step) % row_count) for j in range(row_count)]
+        by_row = by_row + lax.ppermute(sent, "row", route).astype(jnp.float32)
+    by_row = by_row.astype(jnp.bfloat16)
     mixed = lax.psum_scatter(by_row, "col", scatter_dimension=1, tiled=True)
     return mixed.astype(jnp.float32)
 

time: 432 us -> 399 us (0.924)
  waiting for transfers between devices: 318 us -> 264 us
  local copies, waits for them, and re-layouts: 16.9 us -> 28.9 us
  starting transfers between devices: 59.2 us -> 69.2 us
    reduce_scatter x1 -> x0, waiting for transfers between devices: 66.4 us -> none  [body(): lax.psum_scatter(partial_out.astype(jnp.bfloat16), 'row', scatter_dimensi...]
    ppermute x0 -> x3, waiting for transfers between devices: none -> 15.4 us  [body(): by_row = by_row + lax.ppermute(sent, 'row', route).astype(jnp.float32)]
    ppermute x0 -> x3, starting transfers between devices: none -> 11.2 us  [body(): by_row = by_row + lax.ppermute(sent, 'row', route).astype(jnp.float32)]
    dynamic_slice x0 -> x1, local copies, waits for them, and re-layouts: none -> 8.1 us  [body(): lax.dynamic_index_in_dim(shares, row_index, 1, keepdims=False)]
    ppermute x11, waiting for transfers between devices: 17.4 us -> 10.8 us  [shifted(): return lax.ppermute(block, axis, route)]
    reshape x1 -> x2, local copies, waits for them, and re-layouts: 0.01 us -> 4.52 us  [the longest x1 4.51 us: body(): shares = partial_out.astype(jnp.bfloat16).reshape(tok_rows, row_count, -1)]
    unnamed x42 -> x53, local copies, waits for them, and re-layouts: 9.4 us -> 8.73 us
  transfers between devices with their start and end apart: 16 -> 18, of which waited for: 12 -> 14; matrix products, arithmetic and copies ran while one was open for 2% -> 2% of each run, Pallas kernels for 0% -> 0%
where the time goes in v5:
time: 399 us; the launch traced here: 398 us
  waiting for transfers between devices  264 us (66%)
  starting transfers between devices  69.2 us (17%)
  local copies, waits for them, and re-layouts  28.9 us (7%)
  between operations  14.4 us (4%)
  matrix products  10.8 us (3%)
  other arithmetic  10.4 us (3%)
    reduce_scatter x1, waiting for transfers between devices, body(): lax.psum_scatter(packed.astype(jnp.bfloat16), 'col', scatter_dimension=1,...  148 us
    reduce_scatter x1, waiting for transfers between devices, body(): mixed = lax.psum_scatter(by_row, 'col', scatter_dimension=1, tiled=True)  85.9 us
    ppermute x11, starting transfers between devices, shifted(): return lax.ppermute(block, axis, route)  33.8 us
    ppermute x3, waiting for transfers between devices, body(): by_row = by_row + lax.ppermute(sent, 'row', route).astype(jnp.float32)  15.4 us
    ppermute x1, starting transfers between devices, body(): other = lax.ppermute(bc_pre, 'col', partner)  13.6 us
    ppermute x3, starting transfers between devices, body(): by_row = by_row + lax.ppermute(sent, 'row', route).astype(jnp.float32)  11.2 us
    ppermute x11, waiting for transfers between devices, shifted(): return lax.ppermute(block, axis, route)  10.8 us
    ppermute x1, starting transfers between devices, body(): group_sum = squares + lax.ppermute(squares, 'col', partner)  10.6 us
  transfers between devices with their start and end apart: 18, of which 14 were waited for; matrix products, arithmetic and copies ran while one was open for 2% of the time, Pallas kernels for 0%

profile of v5, /device:TPU:24, one launch (start us, length us, event | category | flops | bytes accessed | tf_op | source)
XLA Modules:
  0.0 397.7 jit_solution(7429883450807047708)
XLA Ops:
  6.5 8.1 %copy.66 = bf16[1024,20,128]{0,2,1:T(8,128)(2,1)} copy(bf16[1024,20,128]{2,0,1:T(8,128)(2,1)} %param.14) | data formatting | bytes 10485760 | tf_op args[1]
  14.6 5.2 %convolution_convert_fusion = bf16[256,4,640]{2,0,1:T(8,128)(2,1)} fusion(bf16[4,640,1024]{2,1,0:T(8,128)(2,1)} %bitcast.140, bf16[256,1024]{1,0:T(8,128)(2,1)S(1)} %copy-done.2), kind=kOutput, calls=%fused_computation.3 | convolution fusion | flops 1342832640 | bytes 7077888 | tf_op jit(solution)/shard_map/dot_general | solution.py:94
  22.6 2.7 pad_maximum_fusion
  28.1 148.3 %reduce-scatter.3.cloned.1.call-done = bf16[264,1,768]{2,0,1:T(8,128)(2,1)} async-done(((bf16[264,4,768]{2,0,1:T(8,128)(2,1)}), bf16[264,1,768]{2,0,1:T(8,128)(2,1)}) %reduce-scatter.3.cloned.1.call-update) | async-done | bytes 405520 | tf_op jit(solution)/shard_map/reduce_scatter | solution.py:119
  178.0 13.6 %collective-permute-start = (bf16[256,128]{1,0:T(8,128)(2,1)S(1)}, bf16[256,128]{1,0:T(8,128)(2,1)S(1)}, u32[]{:S(2)}, u32[]{:S(2)}) collective-permute-start(bf16[256,128]{1,0:T(8,128)(2,1)S(1)} %slice.293), channel_id=1, source_target_pairs={{0,1},{1,0},{2,3},{3,2},{4,5},{5,4},{6,7},{7,6},{8,9},{9,8},{10,11... | collective-permute-start | bytes 196616 | tf_op jit(solution)/shard_map/ppermute | solution.py:126
  192.3 1.5 reduce-window.6
  196.7 1.9 collective-permute-start.1
  198.7 3.8 collective-permute-done.1
  204.1 4.3 %collective-permute-start.5 = (bf16[5,65,128]{2,1,0:T(8,128)(2,1)S(1)}, bf16[5,65,128]{2,1,0:T(8,128)(2,1)S(1)}, u32[]{:S(2)}, u32[]{:S(2)}) collective-permute-start(bf16[5,65,128]{2,1,0:T(8,128)(2,1)S(1)} %pad_maximum_fusion.2), channel_id=1, source_target_pairs={{0,64},{16,80},{32,96},{48,112},{64,128},{80,144},{96,160},{112,17... | collective-permute-start | bytes 249608 | tf_op jit(solution)/shard_map/ppermute | solution.py:12
  208.4 2.6 collective-permute-start.4
  211.0 3.3 collective-permute-start.3
  214.4 2.3 collective-permute-start.2
  217.8 2.4 collective-permute-done.2
  220.4 2.2 collective-permute-start.6
  222.8 3.7 collective-permute-start.7
  226.5 2.4 collective-permute-start.8
  229.5 1.6 collective-permute-done.8
  231.2 4.7 %collective-permute-start.9 = (bf16[5,65,128]{2,1,0:T(8,128)(2,1)S(1)}, bf16[5,65,128]{2,1,0:T(8,128)(2,1)S(1)}, u32[]{:S(2)}, u32[]{:S(2)}) collective-permute-start(bf16[5,65,128]{2,1,0:T(8,128)(2,1)S(1)} %get-tuple-element.5), channel_id=1, source_target_pairs={{0,256},{16,272},{32,288},{48,304},{64,320},{80,336},{96,352},{112... | collective-permute-start | bytes 249608 | tf_op jit(solution)/shard_map/ppermute | solution.py:12
  236.5 5.0 %collective-permute-start.10 = (bf16[5,65,128]{2,1,0:T(8,128)(2,1)S(1)}, bf16[5,65,128]{2,1,0:T(8,128)(2,1)S(1)}, u32[]{:S(2)}, u32[]{:S(2)}) collective-permute-start(bf16[5,65,128]{2,1,0:T(8,128)(2,1)S(1)} %get-tuple-element.5), channel_id=1, source_target_pairs={{0,512},{16,528},{32,544},{48,560},{64,576},{80,592},{96,608},{112... | collective-permute-start | bytes 249608 | tf_op jit(solution)/shard_map/ppermute | solution.py:12
  245.4 10.6 %collective-permute-start.12 = (f32[256]{0:T(256)S(1)}, f32[256]{0:T(256)S(1)}, u32[]{:S(2)}, u32[]{:S(2)}) collective-permute-start(f32[256]{0:T(256)S(1)} %get-tuple-element.39), channel_id=1, source_target_pairs={{0,1},{1,0},{2,3},{3,2},{4,5},{5,4},{6,7},{7,6},{8,9},{9,8},{10,11... | collective-permute-start | bytes 3080 | tf_op jit(solution)/shard_map/ppermute | solution.py:179
  256.1 3.6 collective-permute-done.12
  259.6 2.7 fusion
  262.4 4.5 %reshape.121 = bf16[256,4,1024]{2,1,0:T(4,128)(2,1)} reshape(bf16[256,4096]{1,0:T(8,128)(2,1)} %fusion) | data formatting | bytes 4194304 | tf_op jit(solution)/shard_map/reshape | solution.py:188
  266.9 8.1 %constant_dynamic-slice_fusion.6 = (bf16[256,1,1024]{2,1,0:T(2,128)(2,1)S(1)}, bf16[256,1,1024]{2,1,0:T(2,128)(2,1)S(1)}, bf16[256,1,1024]{2,1,0:T(2,128)(2,1)S(1)}, bf16[256,1,1024]{2,1,0:T(2,128)(2,1)S(1)}) fusion(bf16[256,4,1024]{2,1,0:T(4,128)(2,1)} %reshape.121, s32[]{:T(128)S(6)} %select_n.153, s32[]{:T(128)S(6)} %select_n.157, s32[]{:T(128)S(6)} %select_n.155, ...), kind=kLoop, calls=%fused_computation.152 | loop fusion | bytes 4194320 | tf_op jit(solution)/shard_map/jit(dynamic_index_in_dim)/dynamic_slice | solution.py:189
  275.2 3.2 collective-permute-start.13
  278.6 4.6 %collective-permute-start.14 = (bf16[256,1024]{1,0:T(8,128)(2,1)S(1)}, bf16[256,1024]{1,0:T(8,128)(2,1)S(1)}, u32[]{:S(2)}, u32[]{:S(2)}) collective-permute-start(bf16[256,1024]{1,0:T(8,128)(2,1)S(1)} %bitcast.145), channel_id=1, source_target_pairs={{0,8},{4,12},{8,0},{12,4},{1,9},{5,13},{9,1},{13,5},{2,10},{6,14},... | collective-permute-start | bytes 1572872 | tf_op jit(solution)/shard_map/ppermute | solution.py:193
  283.3 3.4 collective-permute-start.15
  286.7 6.7 %collective-permute-done.13 = bf16[256,1024]{1,0:T(8,128)(2,1)S(1)} collective-permute-done((bf16[256,1024]{1,0:T(8,128)(2,1)S(1)}, bf16[256,1024]{1,0:T(8,128)(2,1)S(1)}, u32[]{:S(2)}, u32[]{:S(2)}) %collective-permute-start.13) | collective-permute-done | bytes 524320 | tf_op jit(solution)/shard_map/ppermute | solution.py:193
  293.4 6.2 %collective-permute-done.14 = bf16[256,1024]{1,0:T(8,128)(2,1)S(1)} collective-permute-done((bf16[256,1024]{1,0:T(8,128)(2,1)S(1)}, bf16[256,1024]{1,0:T(8,128)(2,1)S(1)}, u32[]{:S(2)}, u32[]{:S(2)}) %collective-permute-start.14) | collective-permute-done | bytes 524320 | tf_op jit(solution)/shard_map/ppermute | solution.py:193
  299.6 2.5 collective-permute-done.15
  303.4 85.9 %reduce-scatter.5.cloned.1.call-done = bf16[256,256]{1,0:T(8,128)(2,1)} async-done(((bf16[256,1024]{1,0:T(8,128)(2,1)}), bf16[256,256]{1,0:T(8,128)(2,1)}) %reduce-scatter.5.cloned.1.call-update) | async-done | bytes 131088 | tf_op jit(solution)/shard_map/reduce_scatter | solution.py:195
  389.3 1.6 convert_element_type.135
  (158 shorter events, 20.1 us)
Async XLA Ops:
  6.5 253.1 %copy-start = (bf16[5,64,4096]{2,1,0:T(8,128)(2,1)S(1)}, bf16[5,64,4096]{2,1,0:T(8,128)(2,1)}, u32[]{:S(2)}) copy-start(bf16[5,64,4096]{2,1,0:T(8,128)(2,1)} %param.25) | copy-start | bytes 7864324
  6.5 8.1 %copy-start.2 = (bf16[256,1024]{1,0:T(8,128)(2,1)S(1)}, bf16[256,1024]{1,0:T(8,128)(2,1)}, u32[]{:S(2)}) copy-start(bf16[256,1024]{1,0:T(8,128)(2,1)} %param.13) | copy-start | bytes 1572868
  6.5 169.9 %reduce-scatter.3.cloned.1.call-start = ((), (), s32[]{:S(2)}) async-start(), calls=%async_computation.2 | async-start | bytes 2027520 | tf_op jit(solution)/shard_map/reduce_scatter | solution.py:119
  22.6 169.0 %copy-start.14 = (f32[5]{0:T(128)S(1)}, f32[5]{0:T(128)}, u32[]{:S(2)}) copy-start(f32[5]{0:T(128)} %param.21) | copy-start | bytes 64
  25.3 364.0 %reduce-scatter.5.cloned.1.call-start = ((), (), s32[]{:S(2)}) async-start(), calls=%async_computation.3 | async-start | bytes 655360 | tf_op jit(solution)/shard_map/reduce_scatter | solution.py:195
  178.0 18.6 %collective-permute-start = (bf16[256,128]{1,0:T(8,128)(2,1)S(1)}, bf16[256,128]{1,0:T(8,128)(2,1)S(1)}, u32[]{:S(2)}, u32[]{:S(2)}) collective-permute-start(bf16[256,128]{1,0:T(8,128)(2,1)S(1)} %slice.293), channel_id=1, source_target_pairs={{0,1},{1,0},{2,3},{3,2},{4,5},{5,4},{6,7},{7,6},{8,9},{9,8},{10,11... | collective-permute-start | bytes 196616 | tf_op jit(solution)/shard_map/ppermute | solution.py:126
  196.2 6.7 %copy-start.9 = (f32[1,1,256]{2,1,0:T(1,128)S(1)}, f32[1,1,256]{2,1,0:T(1,128)}, u32[]{:S(2)}) copy-start(f32[1,1,256]{2,1,0:T(1,128)} %get-tuple-element.25) | copy-start | bytes 3076
  196.2 6.7 %copy-start.10 = (f32[1,1,256]{2,1,0:T(1,128)S(1)}, f32[1,1,256]{2,1,0:T(1,128)}, u32[]{:S(2)}) copy-start(f32[1,1,256]{2,1,0:T(1,128)} %get-tuple-element.26) | copy-start | bytes 3076
  196.2 6.7 %copy-start.11 = (f32[1,1,256]{2,1,0:T(1,128)S(1)}, f32[1,1,256]{2,1,0:T(1,128)}, u32[]{:S(2)}) copy-start(f32[1,1,256]{2,1,0:T(1,128)} %get-tuple-element.27) | copy-start | bytes 3076
  196.2 6.7 %copy-start.12 = (f32[1,1,256]{2,1,0:T(1,128)S(1)}, f32[1,1,256]{2,1,0:T(1,128)}, u32[]{:S(2)}) copy-start(f32[1,1,256]{2,1,0:T(1,128)} %get-tuple-element.28) | copy-start | bytes 3076
  196.2 6.7 %copy-start.13 = (f32[1,256]{1,0:T(1,128)S(1)}, f32[1,256]{1,0:T(1,128)}, u32[]{:S(2)}) copy-start(f32[1,256]{1,0:T(1,128)} %constant_dynamic-slice_fusion.8) | copy-start | bytes 3076
  196.3 6.9 %copy-start.8 = (f32[5,64]{1,0:T(8,128)S(1)}, f32[5,64]{1,0:T(8,128)}, u32[]{:S(2)}) copy-start(f32[5,64]{1,0:T(8,128)} %param.18) | copy-start | bytes 3844
  196.7 5.8 %collective-permute-start.1 = (bf16[3,576]{1,0:T(4,128)(2,1)S(1)}, bf16[3,576]{1,0:T(4,128)(2,1)S(1)}, u32[]{:S(2)}, u32[]{:S(2)}) collective-permute-start(bf16[3,576]{1,0:T(4,128)(2,1)S(1)} %pad_maximum_fusion.3), channel_id=1, source_target_pairs={{0,16},{16,32},{32,48},{48,64},{64,80},{80,96},{96,112},{112,128},... | collective-permute-start | bytes 10376 | tf_op jit(solution)/shard_map/ppermute | solution.py:12
  202.9 13.9 %copy-start.1 = (f32[5,65,128]{2,1,0:T(8,128)S(1)}, f32[5,65,128]{2,1,0:T(8,128)}, u32[]{:S(2)}) copy-start(f32[5,65,128]{2,1,0:T(8,128)} %constant.109.clone.1) | copy-start | bytes 499204
  204.1 12.6 %collective-permute-start.5 = (bf16[5,65,128]{2,1,0:T(8,128)(2,1)S(1)}, bf16[5,65,128]{2,1,0:T(8,128)(2,1)S(1)}, u32[]{:S(2)}, u32[]{:S(2)}) collective-permute-start(bf16[5,65,128]{2,1,0:T(8,128)(2,1)S(1)} %pad_maximum_fusion.2), channel_id=1, source_target_pairs={{0,64},{16,80},{32,96},{48,112},{64,128},{80,144},{96,160},{112,17... | collective-permute-start | bytes 249608 | tf_op jit(solution)/shard_map/ppermute | solution.py:12
  208.4 8.4 %collective-permute-start.4 = (bf16[5,65,128]{2,1,0:T(8,128)(2,1)S(1)}, bf16[5,65,128]{2,1,0:T(8,128)(2,1)S(1)}, u32[]{:S(2)}, u32[]{:S(2)}) collective-permute-start(bf16[5,65,128]{2,1,0:T(8,128)(2,1)S(1)} %pad_maximum_fusion.2), channel_id=1, source_target_pairs={{0,48},{16,64},{32,80},{48,96},{64,112},{80,128},{96,144},{112,160... | collective-permute-start | bytes 249608 | tf_op jit(solution)/shard_map/ppermute | solution.py:12
  211.0 6.6 %collective-permute-start.3 = (bf16[5,65,128]{2,1,0:T(8,128)(2,1)S(1)}, bf16[5,65,128]{2,1,0:T(8,128)(2,1)S(1)}, u32[]{:S(2)}, u32[]{:S(2)}) collective-permute-start(bf16[5,65,128]{2,1,0:T(8,128)(2,1)S(1)} %pad_maximum_fusion.2), channel_id=1, source_target_pairs={{0,32},{16,48},{32,64},{48,80},{64,96},{80,112},{96,128},{112,144}... | collective-permute-start | bytes 249608 | tf_op jit(solution)/shard_map/ppermute | solution.py:12
  214.4 5.9 %collective-permute-start.2 = (bf16[5,65,128]{2,1,0:T(8,128)(2,1)S(1)}, bf16[5,65,128]{2,1,0:T(8,128)(2,1)S(1)}, u32[]{:S(2)}, u32[]{:S(2)}) collective-permute-start(bf16[5,65,128]{2,1,0:T(8,128)(2,1)S(1)} %pad_maximum_fusion.2), channel_id=1, source_target_pairs={{0,16},{16,32},{32,48},{48,64},{64,80},{80,96},{96,112},{112,128},... | collective-permute-start | bytes 249608 | tf_op jit(solution)/shard_map/ppermute | solution.py:12
  220.4 8.6 %collective-permute-start.6 = (bf16[5,65,128]{2,1,0:T(8,128)(2,1)S(1)}, bf16[5,65,128]{2,1,0:T(8,128)(2,1)S(1)}, u32[]{:S(2)}, u32[]{:S(2)}) collective-permute-start(bf16[5,65,128]{2,1,0:T(8,128)(2,1)S(1)} %get-tuple-element.7), channel_id=1, source_target_pairs={{0,64},{16,80},{32,96},{48,112},{64,128},{80,144},{96,160},{112,17... | collective-permute-start | bytes 249608 | tf_op jit(solution)/shard_map/ppermute | solution.py:12
  222.8 13.2 %copy-start.7 = (f32[5,256]{1,0:T(8,128)S(1)}, f32[5,256]{1,0:T(8,128)}, u32[]{:S(2)}) copy-start(f32[5,256]{1,0:T(8,128)} %get-tuple-element.30) | copy-start | bytes 15364
  222.8 6.6 %collective-permute-start.7 = (bf16[5,65,128]{2,1,0:T(8,128)(2,1)S(1)}, bf16[5,65,128]{2,1,0:T(8,128)(2,1)S(1)}, u32[]{:S(2)}, u32[]{:S(2)}) collective-permute-start(bf16[5,65,128]{2,1,0:T(8,128)(2,1)S(1)} %get-tuple-element.7), channel_id=1, source_target_pairs={{0,128},{16,144},{32,160},{48,176},{64,192},{80,208},{96,224},{112... | collective-permute-start | bytes 249608 | tf_op jit(solution)/shard_map/ppermute | solution.py:12
  226.5 4.6 %collective-permute-start.8 = (bf16[5,65,128]{2,1,0:T(8,128)(2,1)S(1)}, bf16[5,65,128]{2,1,0:T(8,128)(2,1)S(1)}, u32[]{:S(2)}, u32[]{:S(2)}) collective-permute-start(bf16[5,65,128]{2,1,0:T(8,128)(2,1)S(1)} %get-tuple-element.7), channel_id=1, source_target_pairs={{0,192},{16,208},{32,224},{48,240},{64,256},{80,272},{96,288},{112... | collective-permute-start | bytes 249608 | tf_op jit(solution)/shard_map/ppermute | solution.py:12
  231.2 11.6 %collective-permute-start.9 = (bf16[5,65,128]{2,1,0:T(8,128)(2,1)S(1)}, bf16[5,65,128]{2,1,0:T(8,128)(2,1)S(1)}, u32[]{:S(2)}, u32[]{:S(2)}) collective-permute-start(bf16[5,65,128]{2,1,0:T(8,128)(2,1)S(1)} %get-tuple-element.5), channel_id=1, source_target_pairs={{0,256},{16,272},{32,288},{48,304},{64,320},{80,336},{96,352},{112... | collective-permute-start | bytes 249608 | tf_op jit(solution)/shard_map/ppermute | solution.py:12
  236.5 8.5 %copy-start.6 = (f32[256,5]{0,1:T(8,128)S(1)}, f32[256,5]{0,1:T(8,128)}, u32[]{:S(2)}) copy-start(f32[256,5]{0,1:T(8,128)} %get-tuple-element.35) | copy-start | bytes 15364
  236.5 8.5 %copy-start.17 = (f32[5]{0:T(128)S(1)}, f32[5]{0:T(128)}, u32[]{:S(2)}) copy-start(f32[5]{0:T(128)} %param.23) | copy-start | bytes 64
  236.5 7.1 %collective-permute-start.10 = (bf16[5,65,128]{2,1,0:T(8,128)(2,1)S(1)}, bf16[5,65,128]{2,1,0:T(8,128)(2,1)S(1)}, u32[]{:S(2)}, u32[]{:S(2)}) collective-permute-start(bf16[5,65,128]{2,1,0:T(8,128)(2,1)S(1)} %get-tuple-element.5), channel_id=1, source_target_pairs={{0,512},{16,528},{32,544},{48,560},{64,576},{80,592},{96,608},{112... | collective-permute-start | bytes 249608 | tf_op jit(solution)/shard_map/ppermute | solution.py:12
  241.5 3.4 collective-permute-start.11
  243.7 15.9 %copy-start.4 = (f32[5,64]{1,0:T(8,128)S(1)}, f32[5,64]{1,0:T(8,128)}, u32[]{:S(2)}) copy-start(f32[5,64]{1,0:T(8,128)} %param.24) | copy-start | bytes 3844
  245.4 14.2 %collective-permute-start.12 = (f32[256]{0:T(256)S(1)}, f32[256]{0:T(256)S(1)}, u32[]{:S(2)}, u32[]{:S(2)}) collective-permute-start(f32[256]{0:T(256)S(1)} %get-tuple-element.39), channel_id=1, source_target_pairs={{0,1},{1,0},{2,3},{3,2},{4,5},{5,4},{6,7},{7,6},{8,9},{9,8},{10,11... | collective-permute-start | bytes 3080 | tf_op jit(solution)/shard_map/ppermute | solution.py:179
  275.2 18.2 %collective-permute-start.13 = (bf16[256,1024]{1,0:T(8,128)(2,1)S(1)}, bf16[256,1024]{1,0:T(8,128)(2,1)S(1)}, u32[]{:S(2)}, u32[]{:S(2)}) collective-permute-start(bf16[256,1024]{1,0:T(8,128)(2,1)S(1)} %bitcast.144), channel_id=1, source_target_pairs={{0,4},{4,8},{8,12},{12,0},{1,5},{5,9},{9,13},{13,1},{2,6},{6,10},{... | collective-permute-start | bytes 1572872 | tf_op jit(solution)/shard_map/ppermute | solution.py:193
  278.6 21.0 %collective-permute-start.14 = (bf16[256,1024]{1,0:T(8,128)(2,1)S(1)}, bf16[256,1024]{1,0:T(8,128)(2,1)S(1)}, u32[]{:S(2)}, u32[]{:S(2)}) collective-permute-start(bf16[256,1024]{1,0:T(8,128)(2,1)S(1)} %bitcast.145), channel_id=1, source_target_pairs={{0,8},{4,12},{8,0},{12,4},{1,9},{5,13},{9,1},{13,5},{2,10},{6,14},... | collective-permute-start | bytes 1572872 | tf_op jit(solution)/shard_map/ppermute | solution.py:193
  283.3 18.7 %collective-permute-start.15 = (bf16[256,1024]{1,0:T(8,128)(2,1)S(1)}, bf16[256,1024]{1,0:T(8,128)(2,1)S(1)}, u32[]{:S(2)}, u32[]{:S(2)}) collective-permute-start(bf16[256,1024]{1,0:T(8,128)(2,1)S(1)} %bitcast.146), channel_id=1, source_target_pairs={{0,12},{4,0},{8,4},{12,8},{1,13},{5,1},{9,5},{13,9},{2,14},{6,2},{... | collective-permute-start | bytes 1572872 | tf_op jit(solution)/shard_map/ppermute | solution.py:193
  (4 other events, 16.0 us)
Sparse Core Ops, SparseCore 0:
  25.4 150.9 reduce-scatter.2
  303.5 85.6 reduce-scatter.4

commit v6 on v3

--- a/solution.py
+++ b/solution.py
@@ -117,14 +117,6 @@
     xz_width = heads_dev * 2 * head_width
     xz_sum = summed[:tok_rows, :xz_width].reshape(tok_rows, heads_dev, 2 * head_width)
     bc_pre = summed[:tok_rows, xz_width:]
-    if paired:
-        partner = [(c, c ^ 1) for c in range(col_count)]
-        other = lax.ppermute(bc_pre, "col", partner)
-        bc_pre = jnp.where(
-            col_index % 2 == 0,
-            jnp.concatenate([bc_pre, other], axis=1),
-            jnp.concatenate([other, bc_pre], axis=1),
-        )
     dt_raw = (
         summed[tok_rows:].reshape(-1)[: heads_dev * tok_rows]
         .reshape(heads_dev, tok_rows)
@@ -139,6 +131,25 @@
     edge = shifted(edge, "ctx", 1)
     x_edge = edge[:, : heads_dev * head_width].reshape(edge_len, heads_dev, head_width)
     bc_edge = edge[:, heads_dev * head_width :]
+    if paired:
+        partner = [(c, c ^ 1) for c in range(col_count)]
+        other = lax.ppermute(bc_pre, "col", partner)
+        ctx_count = lax.axis_size("ctx")
+        diagonal = [
+            ((i - 1) * col_count + (c ^ 1), i * col_count + c)
+            for i in range(1, ctx_count)
+            for c in range(col_count)
+        ]
+        other_edge = lax.ppermute(bc_pre[tok_rows - edge_len :], ("ctx", "col"), diagonal)
+        low = col_index % 2 == 0
+        bc_pre = jnp.where(
+            low, jnp.concatenate([bc_pre, other], axis=1), jnp.concatenate([other, bc_pre], axis=1)
+        )
+        bc_edge = jnp.where(
+            low,
+            jnp.concatenate([bc_edge, other_edge], axis=1),
+            jnp.concatenate([other_edge, bc_edge], axis=1),
+        )
     x_conv = causal_conv(x_edge, x_pre, conv_x, conv_x_bias)
     bc_kernel = lax.dynamic_index_in_dim(conv_bc, own_group, 1, keepdims=False)
     bc_offset = lax.dynamic_index_in_dim(conv_bc_bias, own_group, 0, keepdims=False)
@@ -180,9 +191,12 @@
     mean_sq = group_sum / (group_heads * head_width)
     normed = (gated * lax.rsqrt(mean_sq + EPSILON)[:, None, None] * norm_gain).astype(jnp.bfloat16)
     partial_out = jnp.einsum("lhp,hpd->ld", normed, w_out, preferred_element_type=jnp.float32)
-    by_row = lax.psum_scatter(
-        partial_out.astype(jnp.bfloat16), "row", scatter_dimension=1, tiled=True
-    )
+    swapped = lax.all_to_all(
+        partial_out.astype(jnp.bfloat16), "row", split_axis=1, concat_axis=0, tiled=True
+    )
+    by_row = jnp.sum(
+        swapped.reshape(row_count, tok_rows, -1).astype(jnp.float32), axis=0
+    ).astype(jnp.bfloat16)
     mixed = lax.psum_scatter(by_row, "col", scatter_dimension=1, tiled=True)
     return mixed.astype(jnp.float32)
 

time: 432 us -> 418 us (0.968)
  waiting for transfers between devices: 318 us -> 277 us
  blocking collectives: 0 us -> 26.7 us
  other arithmetic: 11.9 us -> 16.6 us
    reduce_scatter x1 -> x0, waiting for transfers between devices: 66.4 us -> none  [body(): lax.psum_scatter(partial_out.astype(jnp.bfloat16), 'row', scatter_dimensi...]
    all_to_all x0 -> x1, blocking collectives: none -> 26.7 us  [body(): lax.all_to_all(partial_out.astype(jnp.bfloat16), 'row', split_axis=1, con...]
    ppermute x0 -> x1, starting transfers between devices: none -> 11.1 us  [body(): lax.ppermute(bc_pre[tok_rows - edge_len:], ('ctx', 'col'), diagonal)]
    reduce_scatter x1, waiting for transfers between devices: 84 us -> 94.8 us  [body(): mixed = lax.psum_scatter(by_row, 'col', scatter_dimension=1, tiled=True)]
    ppermute x1, waiting for transfers between devices: 0.01 us -> 9.17 us  [body(): other = lax.ppermute(bc_pre, 'col', partner)]
    ppermute x1, starting transfers between devices: 11.6 us -> 5.19 us  [body(): other = lax.ppermute(bc_pre, 'col', partner)]
    ppermute x1, starting transfers between devices: 11 us -> 5.86 us  [body(): group_sum = squares + lax.ppermute(squares, 'col', partner)]
    ppermute x1, waiting for transfers between devices: 3.12 us -> 8.3 us  [body(): group_sum = squares + lax.ppermute(squares, 'col', partner)]
  transfers between devices with their start and end apart: 16 -> 16, of which waited for: 12 -> 12; matrix products, arithmetic and copies ran while one was open for 2% -> 3% of each run, Pallas kernels for 0% -> 0%
where the time goes in v6:
time: 418 us; the launch traced here: 417 us
  waiting for transfers between devices  277 us (66%)
  starting transfers between devices  55.6 us (13%)
  blocking collectives  26.7 us (6%)
  local copies, waits for them, and re-layouts  17.2 us (4%)
  other arithmetic  16.6 us (4%)
  between operations  14 us (3%)
  matrix products  9.4 us (2%)
    reduce_scatter x1, waiting for transfers between devices, body(): lax.psum_scatter(packed.astype(jnp.bfloat16), 'col', scatter_dimension=1,...  148 us
    reduce_scatter x1, waiting for transfers between devices, body(): mixed = lax.psum_scatter(by_row, 'col', scatter_dimension=1, tiled=True)  94.8 us
    ppermute x11, starting transfers between devices, shifted(): return lax.ppermute(block, axis, route)  33.4 us
    all_to_all x1, blocking collectives, body(): lax.all_to_all(partial_out.astype(jnp.bfloat16), 'row', split_axis=1, con...  26.7 us
    ppermute x11, waiting for transfers between devices, shifted(): return lax.ppermute(block, axis, route)  17.1 us
    ppermute x1, starting transfers between devices, body(): lax.ppermute(bc_pre[tok_rows - edge_len:], ('ctx', 'col'), diagonal)  11.1 us
    ppermute x1, waiting for transfers between devices, body(): other = lax.ppermute(bc_pre, 'col', partner)  9.17 us
  transfers between devices with their start and end apart: 16, of which 12 were waited for; matrix products, arithmetic and copies ran while one was open for 3% of the time, Pallas kernels for 0%

profile of v6, /device:TPU:24, one launch (start us, length us, event | category | flops | bytes accessed | tf_op | source)
XLA Modules:
  0.0 416.5 jit_solution(14834634435360732587)
XLA Ops:
  6.5 8.1 %copy.77 = bf16[1024,20,128]{0,2,1:T(8,128)(2,1)} copy(bf16[1024,20,128]{2,0,1:T(8,128)(2,1)} %param.14) | data formatting | bytes 10485760 | tf_op args[1]
  14.6 5.2 %convolution_convert_fusion = bf16[256,4,640]{2,0,1:T(8,128)(2,1)} fusion(bf16[4,640,1024]{2,1,0:T(8,128)(2,1)} %bitcast.132, bf16[256,1024]{1,0:T(8,128)(2,1)S(1)} %copy-done.2), kind=kOutput, calls=%fused_computation.4 | convolution fusion | flops 1342832640 | bytes 7077888 | tf_op jit(solution)/shard_map/dot_general | solution.py:90
  22.6 2.7 pad_maximum_fusion
  26.7 1.4 constant_dynamic-slice_fusion.2
  28.1 147.5 %reduce-scatter.3.cloned.1.call-done = bf16[264,1,768]{2,0,1:T(8,128)(2,1)} async-done(((bf16[264,4,768]{2,0,1:T(8,128)(2,1)}), bf16[264,1,768]{2,0,1:T(8,128)(2,1)}) %reduce-scatter.3.cloned.1.call-update) | async-done | bytes 405520 | tf_op jit(solution)/shard_map/reduce_scatter | solution.py:115
  178.9 11.1 %collective-permute-start.1 = (bf16[3,128]{1,0:T(4,128)(2,1)}, bf16[3,128]{1,0:T(4,128)(2,1)}, u32[]{:S(2)}, u32[]{:S(2)}) collective-permute-start(bf16[3,128]{1,0:T(4,128)(2,1)} %slice.295), channel_id=1, source_target_pairs={{1,16},{0,17},{3,18},{2,19},{17,32},{16,33},{19,34},{18,35},{33,48... | collective-permute-start | bytes 2312 | tf_op jit(solution)/shard_map/ppermute | solution.py:143
  190.8 5.4 %collective-permute-start = (bf16[3,448]{1,0:T(4,128)(2,1)S(1)}, bf16[3,448]{1,0:T(4,128)(2,1)S(1)}, u32[]{:S(2)}, u32[]{:S(2)}) collective-permute-start(bf16[3,448]{1,0:T(4,128)(2,1)S(1)} %pad_maximum_fusion.3), channel_id=1, source_target_pairs={{0,16},{16,32},{32,48},{48,64},{64,80},{80,96},{96,112},{112,128},... | collective-permute-start | bytes 8072 | tf_op jit(solution)/shard_map/ppermute | solution.py:12
  196.4 1.5 reduce-window.6
  200.0 5.2 %collective-permute-start.2 = (bf16[256,128]{1,0:T(8,128)(2,1)S(1)}, bf16[256,128]{1,0:T(8,128)(2,1)}, u32[]{:S(2)}, u32[]{:S(2)}) collective-permute-start(bf16[256,128]{1,0:T(8,128)(2,1)S(1)} %slice.303), channel_id=1, source_target_pairs={{0,1},{1,0},{2,3},{3,2},{4,5},{5,4},{6,7},{7,6},{8,9},{9,8},{10,11... | collective-permute-start | bytes 196616 | tf_op jit(solution)/shard_map/ppermute | solution.py:136
  207.0 9.2 %collective-permute-done.2 = bf16[256,128]{1,0:T(8,128)(2,1)} collective-permute-done((bf16[256,128]{1,0:T(8,128)(2,1)S(1)}, bf16[256,128]{1,0:T(8,128)(2,1)}, u32[]{:S(2)}, u32[]{:S(2)}) %collective-permute-start.2) | collective-permute-done | bytes 65568 | tf_op jit(solution)/shard_map/ppermute | solution.py:136
  218.9 3.5 collective-permute-start.6
  222.5 3.7 collective-permute-start.5
  226.3 2.6 collective-permute-start.4
  228.9 1.9 collective-permute-start.3
  232.6 3.5 collective-permute-done.4
  236.9 6.2 %collective-permute-start.7 = (f32[5,65,128]{2,1,0:T(8,128)S(1)}, f32[5,65,128]{2,1,0:T(8,128)S(1)}, u32[]{:S(2)}, u32[]{:S(2)}) collective-permute-start(f32[5,65,128]{2,1,0:T(8,128)S(1)} %maximum_select_fusion.3), channel_id=1, source_target_pairs={{0,64},{16,80},{32,96},{48,112},{64,128},{80,144},{96,160},{112,17... | collective-permute-start | bytes 499208 | tf_op jit(solution)/shard_map/ppermute | solution.py:12
  243.3 1.3 collective-permute-start.8
  244.6 2.5 collective-permute-start.9
  248.2 3.9 collective-permute-done.8
  252.2 2.0 collective-permute-done.9
  254.3 2.4 collective-permute-start.10
  257.3 2.5 collective-permute-start.11
  259.8 1.3 collective-permute-start.12
  261.7 3.6 collective-permute-done.11
  265.4 1.9 collective-permute-done.12
  267.7 5.9 %collective-permute-start.13 = (f32[256]{0:T(256)S(1)}, f32[256]{0:T(256)S(1)}, u32[]{:S(2)}, u32[]{:S(2)}) collective-permute-start(f32[256]{0:T(256)S(1)} %get-tuple-element.39), channel_id=1, source_target_pairs={{0,1},{1,0},{2,3},{3,2},{4,5},{5,4},{6,7},{7,6},{8,9},{9,8},{10,11... | collective-permute-start | bytes 3080 | tf_op jit(solution)/shard_map/ppermute | solution.py:186
  273.6 8.3 %collective-permute-done.13 = f32[256]{0:T(256)S(1)} collective-permute-done((f32[256]{0:T(256)S(1)}, f32[256]{0:T(256)S(1)}, u32[]{:S(2)}, u32[]{:S(2)}) %collective-permute-start.13) | collective-permute-done | bytes 1056 | tf_op jit(solution)/shard_map/ppermute | solution.py:186
  281.9 1.4 fusion
  283.5 26.7 %all_to_all.13 = bf16[256,4,1024]{2,0,1:T(8,128)(2,1)} all-to-all(bf16[256,4,1024]{2,0,1:T(8,128)(2,1)S(1)} %bitcast.131), channel_id=1, replica_groups=mesh['ctx'=64,'row'=4,'col'=4] {'row'}, dimensions={1} | all-to-all | bytes 4194304 | tf_op jit(solution)/shard_map/all_to_all | solution.py:194
  310.2 2.9 reduce_sum.22
  313.2 94.8 %reduce-scatter.5.cloned.1.call-done = bf16[256,256]{1,0:T(8,128)(2,1)} async-done(((bf16[256,1024]{1,0:T(8,128)(2,1)}), bf16[256,256]{1,0:T(8,128)(2,1)}) %reduce-scatter.5.cloned.1.call-update) | async-done | bytes 131088 | tf_op jit(solution)/shard_map/reduce_scatter | solution.py:200
  408.0 1.6 convert_element_type.57
  (126 shorter events, 20.7 us)
Async XLA Ops:
  6.5 275.4 %copy-start = (bf16[5,64,4096]{2,1,0:T(8,128)(2,1)S(1)}, bf16[5,64,4096]{2,1,0:T(8,128)(2,1)}, u32[]{:S(2)}) copy-start(bf16[5,64,4096]{2,1,0:T(8,128)(2,1)} %param.25) | copy-start | bytes 7864324
  6.5 8.1 %copy-start.2 = (bf16[256,1024]{1,0:T(8,128)(2,1)S(1)}, bf16[256,1024]{1,0:T(8,128)(2,1)}, u32[]{:S(2)}) copy-start(bf16[256,1024]{1,0:T(8,128)(2,1)} %param.13) | copy-start | bytes 1572868
  6.5 169.1 %reduce-scatter.3.cloned.1.call-start = ((), (), s32[]{:S(2)}) async-start(), calls=%async_computation.3 | async-start | bytes 2027520 | tf_op jit(solution)/shard_map/reduce_scatter | solution.py:115
  14.6 5.2 %copy-start.9 = (bf16[1024,2,256]{2,1,0:T(2,128)(2,1)S(1)}, bf16[1024,2,256]{2,1,0:T(2,128)(2,1)}, u32[]{:S(2)}) copy-start(bf16[1024,2,256]{2,1,0:T(2,128)(2,1)} %param.16) | copy-start | bytes 3145732
  19.9 2.4 copy-start.3
  22.6 2.8 copy-start.10
  22.6 5.5 %copy-start.5 = (f32[4,5,64]{2,0,1:T(4,128)S(1)}, f32[4,5,64]{2,0,1:T(4,128)}, u32[]{:S(2)}) copy-start(f32[4,5,64]{2,0,1:T(4,128)} %param.17) | copy-start | bytes 15364
  25.3 171.0 %copy-start.7 = (f32[5]{0:T(128)S(1)}, f32[5]{0:T(128)}, u32[]{:S(2)}) copy-start(f32[5]{0:T(128)} %param.21) | copy-start | bytes 64
  25.3 180.3 %copy-start.6 = (f32[5,64]{1,0:T(8,128)S(1)}, f32[5,64]{1,0:T(8,128)}, u32[]{:S(2)}) copy-start(f32[5,64]{1,0:T(8,128)} %param.18) | copy-start | bytes 3844
  25.3 382.8 %reduce-scatter.5.cloned.1.call-start = ((), (), s32[]{:S(2)}) async-start(), calls=%async_computation.4 | async-start | bytes 655360 | tf_op jit(solution)/shard_map/reduce_scatter | solution.py:200
  178.9 27.3 %collective-permute-start.1 = (bf16[3,128]{1,0:T(4,128)(2,1)}, bf16[3,128]{1,0:T(4,128)(2,1)}, u32[]{:S(2)}, u32[]{:S(2)}) collective-permute-start(bf16[3,128]{1,0:T(4,128)(2,1)} %slice.295), channel_id=1, source_target_pairs={{1,16},{0,17},{3,18},{2,19},{17,32},{16,33},{19,34},{18,35},{33,48... | collective-permute-start | bytes 2312 | tf_op jit(solution)/shard_map/ppermute | solution.py:143
  190.8 14.4 %collective-permute-start = (bf16[3,448]{1,0:T(4,128)(2,1)S(1)}, bf16[3,448]{1,0:T(4,128)(2,1)S(1)}, u32[]{:S(2)}, u32[]{:S(2)}) collective-permute-start(bf16[3,448]{1,0:T(4,128)(2,1)S(1)} %pad_maximum_fusion.3), channel_id=1, source_target_pairs={{0,16},{16,32},{32,48},{48,64},{64,80},{80,96},{96,112},{112,128},... | collective-permute-start | bytes 8072 | tf_op jit(solution)/shard_map/ppermute | solution.py:12
  200.0 16.1 %collective-permute-start.2 = (bf16[256,128]{1,0:T(8,128)(2,1)S(1)}, bf16[256,128]{1,0:T(8,128)(2,1)}, u32[]{:S(2)}, u32[]{:S(2)}) collective-permute-start(bf16[256,128]{1,0:T(8,128)(2,1)S(1)} %slice.303), channel_id=1, source_target_pairs={{0,1},{1,0},{2,3},{3,2},{4,5},{5,4},{6,7},{7,6},{8,9},{9,8},{10,11... | collective-permute-start | bytes 196616 | tf_op jit(solution)/shard_map/ppermute | solution.py:136
  205.4 12.8 %copy-start.8 = (f32[5]{0:T(128)S(1)}, f32[5]{0:T(128)}, u32[]{:S(2)}) copy-start(f32[5]{0:T(128)} %negate_exponential_fusion.1) | copy-start | bytes 64
  205.6 26.9 %copy-start.1 = (f32[5,65,128]{2,1,0:T(8,128)S(1)}, f32[5,65,128]{2,1,0:T(8,128)}, u32[]{:S(2)}) copy-start(f32[5,65,128]{2,1,0:T(8,128)} %constant.85.clone.1) | copy-start | bytes 499204
  218.9 11.9 %collective-permute-start.6 = (f32[5,65,128]{2,1,0:T(8,128)}, f32[5,65,128]{2,1,0:T(8,128)}, u32[]{:S(2)}, u32[]{:S(2)}) collective-permute-start(f32[5,65,128]{2,1,0:T(8,128)} %pad_maximum_fusion.1), channel_id=1, source_target_pairs={{0,64},{16,80},{32,96},{48,112},{64,128},{80,144},{96,160},{112,17... | collective-permute-start | bytes 499208 | tf_op jit(solution)/shard_map/ppermute | solution.py:12
  222.5 10.0 %collective-permute-start.5 = (f32[5,65,128]{2,1,0:T(8,128)}, f32[5,65,128]{2,1,0:T(8,128)S(1)}, u32[]{:S(2)}, u32[]{:S(2)}) collective-permute-start(f32[5,65,128]{2,1,0:T(8,128)} %pad_maximum_fusion.1), channel_id=1, source_target_pairs={{0,48},{16,64},{32,80},{48,96},{64,112},{80,128},{96,144},{112,160... | collective-permute-start | bytes 499208 | tf_op jit(solution)/shard_map/ppermute | solution.py:12
  226.3 9.9 %collective-permute-start.4 = (f32[5,65,128]{2,1,0:T(8,128)}, f32[5,65,128]{2,1,0:T(8,128)S(1)}, u32[]{:S(2)}, u32[]{:S(2)}) collective-permute-start(f32[5,65,128]{2,1,0:T(8,128)} %pad_maximum_fusion.1), channel_id=1, source_target_pairs={{0,32},{16,48},{32,64},{48,80},{64,96},{80,112},{96,128},{112,144}... | collective-permute-start | bytes 499208 | tf_op jit(solution)/shard_map/ppermute | solution.py:12
  228.9 7.9 %collective-permute-start.3 = (f32[5,65,128]{2,1,0:T(8,128)}, f32[5,65,128]{2,1,0:T(8,128)S(1)}, u32[]{:S(2)}, u32[]{:S(2)}) collective-permute-start(f32[5,65,128]{2,1,0:T(8,128)} %pad_maximum_fusion.1), channel_id=1, source_target_pairs={{0,16},{16,32},{32,48},{48,64},{64,80},{80,96},{96,112},{112,128},... | collective-permute-start | bytes 499208 | tf_op jit(solution)/shard_map/ppermute | solution.py:12
  236.9 11.3 %collective-permute-start.7 = (f32[5,65,128]{2,1,0:T(8,128)S(1)}, f32[5,65,128]{2,1,0:T(8,128)S(1)}, u32[]{:S(2)}, u32[]{:S(2)}) collective-permute-start(f32[5,65,128]{2,1,0:T(8,128)S(1)} %maximum_select_fusion.3), channel_id=1, source_target_pairs={{0,64},{16,80},{32,96},{48,112},{64,128},{80,144},{96,160},{112,17... | collective-permute-start | bytes 499208 | tf_op jit(solution)/shard_map/ppermute | solution.py:12
  243.3 8.8 %collective-permute-start.8 = (f32[5,65,128]{2,1,0:T(8,128)S(1)}, f32[5,65,128]{2,1,0:T(8,128)S(1)}, u32[]{:S(2)}, u32[]{:S(2)}) collective-permute-start(f32[5,65,128]{2,1,0:T(8,128)S(1)} %maximum_select_fusion.3), channel_id=1, source_target_pairs={{0,128},{16,144},{32,160},{48,176},{64,192},{80,208},{96,224},{112... | collective-permute-start | bytes 499208 | tf_op jit(solution)/shard_map/ppermute | solution.py:12
  244.6 9.6 %collective-permute-start.9 = (f32[5,65,128]{2,1,0:T(8,128)S(1)}, f32[5,65,128]{2,1,0:T(8,128)S(1)}, u32[]{:S(2)}, u32[]{:S(2)}) collective-permute-start(f32[5,65,128]{2,1,0:T(8,128)S(1)} %maximum_select_fusion.3), channel_id=1, source_target_pairs={{0,192},{16,208},{32,224},{48,240},{64,256},{80,272},{96,288},{112... | collective-permute-start | bytes 499208 | tf_op jit(solution)/shard_map/ppermute | solution.py:12
  254.3 7.4 %collective-permute-start.10 = (f32[5,65,128]{2,1,0:T(8,128)S(1)}, f32[5,65,128]{2,1,0:T(8,128)S(1)}, u32[]{:S(2)}, u32[]{:S(2)}) collective-permute-start(f32[5,65,128]{2,1,0:T(8,128)S(1)} %maximum_select_fusion.6), channel_id=1, source_target_pairs={{0,256},{16,272},{32,288},{48,304},{64,320},{80,336},{96,352},{112... | collective-permute-start | bytes 499208 | tf_op jit(solution)/shard_map/ppermute | solution.py:12
  257.3 10.0 %copy-start.11 = (f32[5]{0:T(128)S(1)}, f32[5]{0:T(128)}, u32[]{:S(2)}) copy-start(f32[5]{0:T(128)} %param.23) | copy-start | bytes 64
  257.3 8.0 %collective-permute-start.11 = (f32[5,65,128]{2,1,0:T(8,128)S(1)}, f32[5,65,128]{2,1,0:T(8,128)S(1)}, u32[]{:S(2)}, u32[]{:S(2)}) collective-permute-start(f32[5,65,128]{2,1,0:T(8,128)S(1)} %maximum_select_fusion.6), channel_id=1, source_target_pairs={{0,512},{16,528},{32,544},{48,560},{64,576},{80,592},{96,608},{112... | collective-permute-start | bytes 499208 | tf_op jit(solution)/shard_map/ppermute | solution.py:12
  259.8 7.5 %collective-permute-start.12 = (f32[5,65,128]{2,1,0:T(8,128)S(1)}, f32[5,65,128]{2,1,0:T(8,128)S(1)}, u32[]{:S(2)}, u32[]{:S(2)}) collective-permute-start(f32[5,65,128]{2,1,0:T(8,128)S(1)} %maximum_select_fusion.6), channel_id=1, source_target_pairs={{0,768},{16,784},{32,800},{48,816},{64,832},{80,848},{96,864},{112... | collective-permute-start | bytes 499208 | tf_op jit(solution)/shard_map/ppermute | solution.py:12
  261.7 20.2 %copy-start.4 = (f32[5,64]{1,0:T(8,128)S(1)}, f32[5,64]{1,0:T(8,128)}, u32[]{:S(2)}) copy-start(f32[5,64]{1,0:T(8,128)} %param.24) | copy-start | bytes 3844
  267.7 14.2 %collective-permute-start.13 = (f32[256]{0:T(256)S(1)}, f32[256]{0:T(256)S(1)}, u32[]{:S(2)}, u32[]{:S(2)}) collective-permute-start(f32[256]{0:T(256)S(1)} %get-tuple-element.39), channel_id=1, source_target_pairs={{0,1},{1,0},{2,3},{3,2},{4,5},{5,4},{6,7},{7,6},{8,9},{9,8},{10,11... | collective-permute-start | bytes 3080 | tf_op jit(solution)/shard_map/ppermute | solution.py:186
Sparse Core Ops, SparseCore 0:
  25.4 150.1 reduce-scatter.2
  313.3 94.6 reduce-scatter.4

commit v7 on v3

--- a/solution.py
+++ b/solution.py
@@ -10,6 +10,10 @@
     devices = range(lax.axis_size(axis))
     route = [(i - distance, i) for i in devices if i - distance in devices]
     return lax.ppermute(block, axis, route)
+
+
+def shifted_narrow(block, axis, distance):
+    return shifted(block.astype(jnp.bfloat16), axis, distance).astype(block.dtype)
 
 
 def causal_conv(edge_rows, own_rows, weights, bias):
@@ -45,11 +49,11 @@
     acc = identity
     for distance in range(radix, 0, -1):
         if distance < size:
-            got = shifted(own, axis, distance)
+            got = shifted_narrow(own, axis, distance)
             acc = jnp.where(mine >= distance, join(acc, got), acc)
     span = radix
     while span < size:
-        parts = [(step * span, shifted(acc, axis, step * span)) for step in range(1, radix) if step * span < size]
+        parts = [(step * span, shifted_narrow(acc, axis, step * span)) for step in range(1, radix) if step * span < size]
         total = acc
         for distance, got in parts:
             total = jnp.where(mine >= distance, join(got, total), total)
@@ -180,9 +184,12 @@
     mean_sq = group_sum / (group_heads * head_width)
     normed = (gated * lax.rsqrt(mean_sq + EPSILON)[:, None, None] * norm_gain).astype(jnp.bfloat16)
     partial_out = jnp.einsum("lhp,hpd->ld", normed, w_out, preferred_element_type=jnp.float32)
-    by_row = lax.psum_scatter(
-        partial_out.astype(jnp.bfloat16), "row", scatter_dimension=1, tiled=True
-    )
+    swapped = lax.all_to_all(
+        partial_out.astype(jnp.bfloat16), "row", split_axis=1, concat_axis=0, tiled=True
+    )
+    by_row = jnp.sum(
+        swapped.reshape(row_count, tok_rows, -1).astype(jnp.float32), axis=0
+    ).astype(jnp.bfloat16)
     mixed = lax.psum_scatter(by_row, "col", scatter_dimension=1, tiled=True)
     return mixed.astype(jnp.float32)
 

time: 432 us -> 385 us (0.89)
  waiting for transfers between devices: 318 us -> 242 us
  blocking collectives: 0 us -> 28.1 us
    reduce_scatter x1 -> x0, waiting for transfers between devices: 66.4 us -> none  [body(): lax.psum_scatter(partial_out.astype(jnp.bfloat16), 'row', scatter_dimensi...]
    all_to_all x0 -> x1, blocking collectives: none -> 28.1 us  [body(): lax.all_to_all(partial_out.astype(jnp.bfloat16), 'row', split_axis=1, con...]
    ppermute x11, waiting for transfers between devices: 17.4 us -> 10 us  [shifted(): return lax.ppermute(block, axis, route)]
    unnamed x42 -> x50, local copies, waits for them, and re-layouts: 9.4 us -> 8.24 us
  transfers between devices with their start and end apart: 16 -> 15, of which waited for: 12 -> 9; matrix products, arithmetic and copies ran while one was open for 2% -> 2% of each run, Pallas kernels for 0% -> 0%
where the time goes in v7:
time: 385 us; the launch traced here: 383 us
  waiting for transfers between devices  242 us (63%)
  starting transfers between devices  61.4 us (16%)
  blocking collectives  28.1 us (7%)
  local copies, waits for them, and re-layouts  16 us (4%)
  between operations  14.3 us (4%)
  other arithmetic  12 us (3%)
  matrix products  9.4 us (2%)
    reduce_scatter x1, waiting for transfers between devices, body(): lax.psum_scatter(packed.astype(jnp.bfloat16), 'col', scatter_dimension=1,...  147 us
    reduce_scatter x1, waiting for transfers between devices, body(): mixed = lax.psum_scatter(by_row, 'col', scatter_dimension=1, tiled=True)  82.7 us
    ppermute x11, starting transfers between devices, shifted(): return lax.ppermute(block, axis, route)  37.4 us
    all_to_all x1, blocking collectives, body(): lax.all_to_all(partial_out.astype(jnp.bfloat16), 'row', split_axis=1, con...  28.1 us
    ppermute x1, starting transfers between devices, body(): group_sum = squares + lax.ppermute(squares, 'col', partner)  12.2 us
    ppermute x1, starting transfers between devices, body(): other = lax.ppermute(bc_pre, 'col', partner)  11.7 us
    ppermute x11, waiting for transfers between devices, shifted(): return lax.ppermute(block, axis, route)  10 us
    unnamed x50, local copies, waits for them, and re-layouts  8.24 us
  transfers between devices with their start and end apart: 15, of which 9 were waited for; matrix products, arithmetic and copies ran while one was open for 2% of the time, Pallas kernels for 0%

profile of v7, /device:TPU:24, one launch (start us, length us, event | category | flops | bytes accessed | tf_op | source)
XLA Modules:
  0.0 383.3 jit_solution(12041199525469599665)
XLA Ops:
  6.5 8.1 %copy.77 = bf16[1024,20,128]{0,2,1:T(8,128)(2,1)} copy(bf16[1024,20,128]{2,0,1:T(8,128)(2,1)} %param.14) | data formatting | bytes 10485760 | tf_op args[1]
  14.6 5.2 %convolution_convert_fusion = bf16[256,4,640]{2,0,1:T(8,128)(2,1)} fusion(bf16[4,640,1024]{2,1,0:T(8,128)(2,1)} %bitcast.132, bf16[256,1024]{1,0:T(8,128)(2,1)S(1)} %copy-done.2), kind=kOutput, calls=%fused_computation.4 | convolution fusion | flops 1342832640 | bytes 7077888 | tf_op jit(solution)/shard_map/dot_general | solution.py:94
  19.8 1.3 convolution_convert_fusion.1
  21.1 1.1 copy.79
  22.6 2.7 pad_maximum_fusion
  25.4 1.2 constant_dynamic-slice_fusion.4
  26.7 1.3 constant_dynamic-slice_fusion.2
  28.1 147.3 %reduce-scatter.3.cloned.1.call-done = bf16[264,1,768]{2,0,1:T(8,128)(2,1)} async-done(((bf16[264,4,768]{2,0,1:T(8,128)(2,1)}), bf16[264,1,768]{2,0,1:T(8,128)(2,1)}) %reduce-scatter.3.cloned.1.call-update) | async-done | bytes 405520 | tf_op jit(solution)/shard_map/reduce_scatter | solution.py:119
  176.9 11.7 %collective-permute-start = (bf16[256,128]{1,0:T(8,128)(2,1)S(1)}, bf16[256,128]{1,0:T(8,128)(2,1)S(1)}, u32[]{:S(2)}, u32[]{:S(2)}) collective-permute-start(bf16[256,128]{1,0:T(8,128)(2,1)S(1)} %slice.293), channel_id=1, source_target_pairs={{0,1},{1,0},{2,3},{3,2},{4,5},{5,4},{6,7},{7,6},{8,9},{9,8},{10,11... | collective-permute-start | bytes 196616 | tf_op jit(solution)/shard_map/ppermute | solution.py:126
  189.4 1.5 reduce-window.6
  193.7 1.9 collective-permute-start.1
  195.6 3.0 collective-permute-done.1
  200.2 8.2 %collective-permute-start.5 = (bf16[5,65,128]{2,1,0:T(8,128)(2,1)S(1)}, bf16[5,65,128]{2,1,0:T(8,128)(2,1)S(1)}, u32[]{:S(2)}, u32[]{:S(2)}) collective-permute-start(bf16[5,65,128]{2,1,0:T(8,128)(2,1)S(1)} %pad_maximum_fusion.2), channel_id=1, source_target_pairs={{0,64},{16,80},{32,96},{48,112},{64,128},{80,144},{96,160},{112,17... | collective-permute-start | bytes 249608 | tf_op jit(solution)/shard_map/ppermute | solution.py:12
  208.4 2.3 collective-permute-start.4
  210.7 3.4 collective-permute-start.3
  214.1 2.2 collective-permute-start.2
  217.5 2.5 collective-permute-done.2
  220.1 2.1 collective-permute-start.6
  222.4 2.8 collective-permute-start.7
  225.2 3.7 collective-permute-start.8
  229.2 1.9 collective-permute-done.8
  231.2 3.9 %collective-permute-start.9 = (bf16[5,65,128]{2,1,0:T(8,128)(2,1)S(1)}, bf16[5,65,128]{2,1,0:T(8,128)(2,1)S(1)}, u32[]{:S(2)}, u32[]{:S(2)}) collective-permute-start(bf16[5,65,128]{2,1,0:T(8,128)(2,1)S(1)} %get-tuple-element.5), channel_id=1, source_target_pairs={{0,256},{16,272},{32,288},{48,304},{64,320},{80,336},{96,352},{112... | collective-permute-start | bytes 249608 | tf_op jit(solution)/shard_map/ppermute | solution.py:12
  235.7 5.6 %collective-permute-start.10 = (bf16[5,65,128]{2,1,0:T(8,128)(2,1)S(1)}, bf16[5,65,128]{2,1,0:T(8,128)(2,1)S(1)}, u32[]{:S(2)}, u32[]{:S(2)}) collective-permute-start(bf16[5,65,128]{2,1,0:T(8,128)(2,1)S(1)} %get-tuple-element.5), channel_id=1, source_target_pairs={{0,512},{16,528},{32,544},{48,560},{64,576},{80,592},{96,608},{112... | collective-permute-start | bytes 249608 | tf_op jit(solution)/shard_map/ppermute | solution.py:12
  241.3 1.3 collective-permute-start.11
  243.6 1.2 collective-permute-done.11
  245.2 12.2 %collective-permute-start.12 = (f32[256]{0:T(256)S(1)}, f32[256]{0:T(256)S(1)}, u32[]{:S(2)}, u32[]{:S(2)}) collective-permute-start(f32[256]{0:T(256)S(1)} %get-tuple-element.35), channel_id=1, source_target_pairs={{0,1},{1,0},{2,3},{3,2},{4,5},{5,4},{6,7},{7,6},{8,9},{9,8},{10,11... | collective-permute-start | bytes 3080 | tf_op jit(solution)/shard_map/ppermute | solution.py:179
  257.4 2.0 collective-permute-done.12
  259.4 1.4 fusion
  261.0 28.1 %all_to_all.13 = bf16[256,4,1024]{2,0,1:T(8,128)(2,1)} all-to-all(bf16[256,4,1024]{2,0,1:T(8,128)(2,1)S(1)} %bitcast.131), channel_id=1, replica_groups=mesh['ctx'=64,'row'=4,'col'=4] {'row'}, dimensions={1} | all-to-all | bytes 4194304 | tf_op jit(solution)/shard_map/all_to_all | solution.py:187
  289.1 2.9 reduce_sum.22
  292.1 82.7 %reduce-scatter.5.cloned.1.call-done = bf16[256,256]{1,0:T(8,128)(2,1)} async-done(((bf16[256,1024]{1,0:T(8,128)(2,1)}), bf16[256,256]{1,0:T(8,128)(2,1)}) %reduce-scatter.5.cloned.1.call-update) | async-done | bytes 131088 | tf_op jit(solution)/shard_map/reduce_scatter | solution.py:193
  374.8 1.6 convert_element_type.113
  (149 shorter events, 10.6 us)
Async XLA Ops:
  6.5 252.9 %copy-start = (bf16[5,64,4096]{2,1,0:T(8,128)(2,1)S(1)}, bf16[5,64,4096]{2,1,0:T(8,128)(2,1)}, u32[]{:S(2)}) copy-start(bf16[5,64,4096]{2,1,0:T(8,128)(2,1)} %param.25) | copy-start | bytes 7864324
  6.5 8.1 %copy-start.2 = (bf16[256,1024]{1,0:T(8,128)(2,1)S(1)}, bf16[256,1024]{1,0:T(8,128)(2,1)}, u32[]{:S(2)}) copy-start(bf16[256,1024]{1,0:T(8,128)(2,1)} %param.13) | copy-start | bytes 1572868
  6.5 168.8 %reduce-scatter.3.cloned.1.call-start = ((), (), s32[]{:S(2)}) async-start(), calls=%async_computation.3 | async-start | bytes 2027520 | tf_op jit(solution)/shard_map/reduce_scatter | solution.py:119
  14.6 5.2 %copy-start.15 = (bf16[1024,2,256]{2,1,0:T(2,128)(2,1)S(1)}, bf16[1024,2,256]{2,1,0:T(2,128)(2,1)}, u32[]{:S(2)}) copy-start(bf16[1024,2,256]{2,1,0:T(2,128)(2,1)} %param.16) | copy-start | bytes 3145732
  22.6 2.8 copy-start.16
  22.6 5.4 %copy-start.5 = (f32[4,5,64]{2,0,1:T(4,128)S(1)}, f32[4,5,64]{2,0,1:T(4,128)}, u32[]{:S(2)}) copy-start(f32[4,5,64]{2,0,1:T(4,128)} %param.17) | copy-start | bytes 15364
  22.6 166.1 %copy-start.14 = (f32[5]{0:T(128)S(1)}, f32[5]{0:T(128)}, u32[]{:S(2)}) copy-start(f32[5]{0:T(128)} %param.21) | copy-start | bytes 64
  25.3 349.5 %reduce-scatter.5.cloned.1.call-start = ((), (), s32[]{:S(2)}) async-start(), calls=%async_computation.4 | async-start | bytes 655360 | tf_op jit(solution)/shard_map/reduce_scatter | solution.py:193
  176.9 16.6 %collective-permute-start = (bf16[256,128]{1,0:T(8,128)(2,1)S(1)}, bf16[256,128]{1,0:T(8,128)(2,1)S(1)}, u32[]{:S(2)}, u32[]{:S(2)}) collective-permute-start(bf16[256,128]{1,0:T(8,128)(2,1)S(1)} %slice.293), channel_id=1, source_target_pairs={{0,1},{1,0},{2,3},{3,2},{4,5},{5,4},{6,7},{7,6},{8,9},{9,8},{10,11... | collective-permute-start | bytes 196616 | tf_op jit(solution)/shard_map/ppermute | solution.py:126
  193.3 5.8 %copy-start.9 = (f32[1,1,256]{2,1,0:T(1,128)S(1)}, f32[1,1,256]{2,1,0:T(1,128)}, u32[]{:S(2)}) copy-start(f32[1,1,256]{2,1,0:T(1,128)} %get-tuple-element.21) | copy-start | bytes 3076
  193.3 5.8 %copy-start.10 = (f32[1,1,256]{2,1,0:T(1,128)S(1)}, f32[1,1,256]{2,1,0:T(1,128)}, u32[]{:S(2)}) copy-start(f32[1,1,256]{2,1,0:T(1,128)} %get-tuple-element.22) | copy-start | bytes 3076
  193.3 5.8 %copy-start.11 = (f32[1,1,256]{2,1,0:T(1,128)S(1)}, f32[1,1,256]{2,1,0:T(1,128)}, u32[]{:S(2)}) copy-start(f32[1,1,256]{2,1,0:T(1,128)} %get-tuple-element.23) | copy-start | bytes 3076
  193.3 5.8 %copy-start.12 = (f32[1,1,256]{2,1,0:T(1,128)S(1)}, f32[1,1,256]{2,1,0:T(1,128)}, u32[]{:S(2)}) copy-start(f32[1,1,256]{2,1,0:T(1,128)} %get-tuple-element.24) | copy-start | bytes 3076
  193.3 5.8 %copy-start.13 = (f32[1,256]{1,0:T(1,128)S(1)}, f32[1,256]{1,0:T(1,128)}, u32[]{:S(2)}) copy-start(f32[1,256]{1,0:T(1,128)} %constant_dynamic-slice_fusion.4) | copy-start | bytes 3076
  193.3 6.0 %copy-start.8 = (f32[5,64]{1,0:T(8,128)S(1)}, f32[5,64]{1,0:T(8,128)}, u32[]{:S(2)}) copy-start(f32[5,64]{1,0:T(8,128)} %param.18) | copy-start | bytes 3844
  193.7 4.9 %collective-permute-start.1 = (bf16[3,576]{1,0:T(4,128)(2,1)S(1)}, bf16[3,576]{1,0:T(4,128)(2,1)S(1)}, u32[]{:S(2)}, u32[]{:S(2)}) collective-permute-start(bf16[3,576]{1,0:T(4,128)(2,1)S(1)} %pad_maximum_fusion.3), channel_id=1, source_target_pairs={{0,16},{16,32},{32,48},{48,64},{64,80},{80,96},{96,112},{112,128},... | collective-permute-start | bytes 10376 | tf_op jit(solution)/shard_map/ppermute | solution.py:12
  199.1 17.4 %copy-start.1 = (f32[5,65,128]{2,1,0:T(8,128)S(1)}, f32[5,65,128]{2,1,0:T(8,128)}, u32[]{:S(2)}) copy-start(f32[5,65,128]{2,1,0:T(8,128)} %constant.85.clone.1) | copy-start | bytes 499204
  200.2 16.1 %collective-permute-start.5 = (bf16[5,65,128]{2,1,0:T(8,128)(2,1)S(1)}, bf16[5,65,128]{2,1,0:T(8,128)(2,1)S(1)}, u32[]{:S(2)}, u32[]{:S(2)}) collective-permute-start(bf16[5,65,128]{2,1,0:T(8,128)(2,1)S(1)} %pad_maximum_fusion.2), channel_id=1, source_target_pairs={{0,64},{16,80},{32,96},{48,112},{64,128},{80,144},{96,160},{112,17... | collective-permute-start | bytes 249608 | tf_op jit(solution)/shard_map/ppermute | solution.py:12
  208.4 8.0 %collective-permute-start.4 = (bf16[5,65,128]{2,1,0:T(8,128)(2,1)S(1)}, bf16[5,65,128]{2,1,0:T(8,128)(2,1)S(1)}, u32[]{:S(2)}, u32[]{:S(2)}) collective-permute-start(bf16[5,65,128]{2,1,0:T(8,128)(2,1)S(1)} %pad_maximum_fusion.2), channel_id=1, source_target_pairs={{0,48},{16,64},{32,80},{48,96},{64,112},{80,128},{96,144},{112,160... | collective-permute-start | bytes 249608 | tf_op jit(solution)/shard_map/ppermute | solution.py:12
  210.7 6.6 %collective-permute-start.3 = (bf16[5,65,128]{2,1,0:T(8,128)(2,1)S(1)}, bf16[5,65,128]{2,1,0:T(8,128)(2,1)S(1)}, u32[]{:S(2)}, u32[]{:S(2)}) collective-permute-start(bf16[5,65,128]{2,1,0:T(8,128)(2,1)S(1)} %pad_maximum_fusion.2), channel_id=1, source_target_pairs={{0,32},{16,48},{32,64},{48,80},{64,96},{80,112},{96,128},{112,144}... | collective-permute-start | bytes 249608 | tf_op jit(solution)/shard_map/ppermute | solution.py:12
  214.1 5.9 %collective-permute-start.2 = (bf16[5,65,128]{2,1,0:T(8,128)(2,1)S(1)}, bf16[5,65,128]{2,1,0:T(8,128)(2,1)S(1)}, u32[]{:S(2)}, u32[]{:S(2)}) collective-permute-start(bf16[5,65,128]{2,1,0:T(8,128)(2,1)S(1)} %pad_maximum_fusion.2), channel_id=1, source_target_pairs={{0,16},{16,32},{32,48},{48,64},{64,80},{80,96},{96,112},{112,128},... | collective-permute-start | bytes 249608 | tf_op jit(solution)/shard_map/ppermute | solution.py:12
  220.1 8.9 %collective-permute-start.6 = (bf16[5,65,128]{2,1,0:T(8,128)(2,1)S(1)}, bf16[5,65,128]{2,1,0:T(8,128)(2,1)S(1)}, u32[]{:S(2)}, u32[]{:S(2)}) collective-permute-start(bf16[5,65,128]{2,1,0:T(8,128)(2,1)S(1)} %get-tuple-element.7), channel_id=1, source_target_pairs={{0,64},{16,80},{32,96},{48,112},{64,128},{80,144},{96,160},{112,17... | collective-permute-start | bytes 249608 | tf_op jit(solution)/shard_map/ppermute | solution.py:12
  222.4 12.7 %copy-start.7 = (f32[5,256]{1,0:T(8,128)S(1)}, f32[5,256]{1,0:T(8,128)}, u32[]{:S(2)}) copy-start(f32[5,256]{1,0:T(8,128)} %get-tuple-element.26) | copy-start | bytes 15364
  222.4 6.6 %collective-permute-start.7 = (bf16[5,65,128]{2,1,0:T(8,128)(2,1)S(1)}, bf16[5,65,128]{2,1,0:T(8,128)(2,1)S(1)}, u32[]{:S(2)}, u32[]{:S(2)}) collective-permute-start(bf16[5,65,128]{2,1,0:T(8,128)(2,1)S(1)} %get-tuple-element.7), channel_id=1, source_target_pairs={{0,128},{16,144},{32,160},{48,176},{64,192},{80,208},{96,224},{112... | collective-permute-start | bytes 249608 | tf_op jit(solution)/shard_map/ppermute | solution.py:12
  225.2 5.8 %collective-permute-start.8 = (bf16[5,65,128]{2,1,0:T(8,128)(2,1)S(1)}, bf16[5,65,128]{2,1,0:T(8,128)(2,1)S(1)}, u32[]{:S(2)}, u32[]{:S(2)}) collective-permute-start(bf16[5,65,128]{2,1,0:T(8,128)(2,1)S(1)} %get-tuple-element.7), channel_id=1, source_target_pairs={{0,192},{16,208},{32,224},{48,240},{64,256},{80,272},{96,288},{112... | collective-permute-start | bytes 249608 | tf_op jit(solution)/shard_map/ppermute | solution.py:12
  231.2 11.5 %collective-permute-start.9 = (bf16[5,65,128]{2,1,0:T(8,128)(2,1)S(1)}, bf16[5,65,128]{2,1,0:T(8,128)(2,1)S(1)}, u32[]{:S(2)}, u32[]{:S(2)}) collective-permute-start(bf16[5,65,128]{2,1,0:T(8,128)(2,1)S(1)} %get-tuple-element.5), channel_id=1, source_target_pairs={{0,256},{16,272},{32,288},{48,304},{64,320},{80,336},{96,352},{112... | collective-permute-start | bytes 249608 | tf_op jit(solution)/shard_map/ppermute | solution.py:12
  235.7 9.1 %copy-start.6 = (f32[256,5]{0,1:T(8,128)S(1)}, f32[256,5]{0,1:T(8,128)}, u32[]{:S(2)}) copy-start(f32[256,5]{0,1:T(8,128)} %get-tuple-element.31) | copy-start | bytes 15364
  235.7 9.1 %copy-start.17 = (f32[5]{0:T(128)S(1)}, f32[5]{0:T(128)}, u32[]{:S(2)}) copy-start(f32[5]{0:T(128)} %param.23) | copy-start | bytes 64
  235.7 7.7 %collective-permute-start.10 = (bf16[5,65,128]{2,1,0:T(8,128)(2,1)S(1)}, bf16[5,65,128]{2,1,0:T(8,128)(2,1)S(1)}, u32[]{:S(2)}, u32[]{:S(2)}) collective-permute-start(bf16[5,65,128]{2,1,0:T(8,128)(2,1)S(1)} %get-tuple-element.5), channel_id=1, source_target_pairs={{0,512},{16,528},{32,544},{48,560},{64,576},{80,592},{96,608},{112... | collective-permute-start | bytes 249608 | tf_op jit(solution)/shard_map/ppermute | solution.py:12
  241.3 3.4 collective-permute-start.11
  243.5 15.9 %copy-start.4 = (f32[5,64]{1,0:T(8,128)S(1)}, f32[5,64]{1,0:T(8,128)}, u32[]{:S(2)}) copy-start(f32[5,64]{1,0:T(8,128)} %param.24) | copy-start | bytes 3844
  245.2 14.2 %collective-permute-start.12 = (f32[256]{0:T(256)S(1)}, f32[256]{0:T(256)S(1)}, u32[]{:S(2)}, u32[]{:S(2)}) collective-permute-start(f32[256]{0:T(256)S(1)} %get-tuple-element.35), channel_id=1, source_target_pairs={{0,1},{1,0},{2,3},{3,2},{4,5},{5,4},{6,7},{7,6},{8,9},{9,8},{10,11... | collective-permute-start | bytes 3080 | tf_op jit(solution)/shard_map/ppermute | solution.py:179
  (1 other events, 2.4 us)
Sparse Core Ops, SparseCore 0:
  25.4 149.9 reduce-scatter.2
  292.2 82.5 reduce-scatter.4

commit v8 on v7

--- a/solution.py
+++ b/solution.py
@@ -190,8 +190,8 @@
     by_row = jnp.sum(
         swapped.reshape(row_count, tok_rows, -1).astype(jnp.float32), axis=0
     ).astype(jnp.bfloat16)
-    mixed = lax.psum_scatter(by_row, "col", scatter_dimension=1, tiled=True)
-    return mixed.astype(jnp.float32)
+    crossed = lax.all_to_all(by_row, "col", split_axis=1, concat_axis=0, tiled=True)
+    return jnp.sum(crossed.reshape(col_count, tok_rows, -1).astype(jnp.float32), axis=0)
 
 
 def solution(mesh):

time: 385 us -> 379 us (0.984)
  the two profiles are of different devices: /device:TPU:24 before, /device:TPU:121 now
where the time goes in v8:
time: 379 us; the launch traced here: 378 us
  waiting for transfers between devices  159 us (42%)
  blocking collectives  116 us (31%)
  starting transfers between devices  49.7 us (13%)
  local copies, waits for them, and re-layouts  18.3 us (5%)
  between operations  14.3 us (4%)
  other arithmetic  11.1 us (3%)
  matrix products  9.41 us (2%)
    reduce_scatter x1, waiting for transfers between devices, body(): lax.psum_scatter(packed.astype(jnp.bfloat16), 'col', scatter_dimension=1,...  148 us
    all_to_all x1, blocking collectives, body(): lax.all_to_all(by_row, 'col', split_axis=1, concat_axis=0, tiled=True)  96.7 us
    ppermute x11, starting transfers between devices, shifted(): return lax.ppermute(block, axis, route)  29.9 us
    all_to_all x1, blocking collectives, body(): lax.all_to_all(partial_out.astype(jnp.bfloat16), 'row', split_axis=1, con...  19.7 us
    ppermute x1, starting transfers between devices, body(): group_sum = squares + lax.ppermute(squares, 'col', partner)  11.7 us
    ppermute x11, waiting for transfers between devices, shifted(): return lax.ppermute(block, axis, route)  9.45 us
    unnamed x50, local copies, waits for them, and re-layouts  8.23 us
    ppermute x1, starting transfers between devices, body(): other = lax.ppermute(bc_pre, 'col', partner)  8.09 us
  transfers between devices with their start and end apart: 14, of which 8 were waited for; matrix products, arithmetic and copies ran while one was open for 2% of the time, Pallas kernels for 0%

profile of v8, /device:TPU:121, one launch (start us, length us, event | category | flops | bytes accessed | tf_op | source)
XLA Modules:
  0.0 378.4 jit_solution(14709985060951823872)
XLA Ops:
  6.5 8.1 %copy.120 = bf16[1024,20,128]{0,2,1:T(8,128)(2,1)} copy(bf16[1024,20,128]{2,0,1:T(8,128)(2,1)} %param.14) | data formatting | bytes 10485760 | tf_op args[1]
  14.6 5.2 %convolution_convert_fusion = bf16[256,4,640]{2,0,1:T(8,128)(2,1)} fusion(bf16[4,640,1024]{2,1,0:T(8,128)(2,1)} %bitcast.133, bf16[256,1024]{1,0:T(8,128)(2,1)S(1)} %copy-done.2), kind=kOutput, calls=%fused_computation.4 | convolution fusion | flops 1342832640 | bytes 7077888 | tf_op jit(solution)/shard_map/dot_general | solution.py:94
  19.9 1.3 convolution_convert_fusion.1
  21.1 1.1 copy.122
  22.6 2.7 pad_maximum_fusion
  25.4 1.3 constant_dynamic-slice_fusion.4
  26.7 1.3 constant_dynamic-slice_fusion.2
  28.1 147.7 %reduce-scatter.2.cloned.1.call-done = bf16[264,1,768]{2,0,1:T(8,128)(2,1)} async-done(((bf16[264,4,768]{2,0,1:T(8,128)(2,1)}), bf16[264,1,768]{2,0,1:T(8,128)(2,1)}) %reduce-scatter.2.cloned.1.call-update) | async-done | bytes 405520 | tf_op jit(solution)/shard_map/reduce_scatter | solution.py:119
  177.3 8.1 %collective-permute-start = (bf16[256,128]{1,0:T(8,128)(2,1)S(1)}, bf16[256,128]{1,0:T(8,128)(2,1)S(1)}, u32[]{:S(2)}, u32[]{:S(2)}) collective-permute-start(bf16[256,128]{1,0:T(8,128)(2,1)S(1)} %slice.293), channel_id=1, source_target_pairs={{0,1},{1,0},{2,3},{3,2},{4,5},{5,4},{6,7},{7,6},{8,9},{9,8},{10,11... | collective-permute-start | bytes 196616 | tf_op jit(solution)/shard_map/ppermute | solution.py:126
  186.1 1.5 reduce-window.6
  188.8 1.0 slice.291
  191.1 1.9 collective-permute-start.1
  193.1 3.9 %collective-permute-done.1 = bf16[3,576]{1,0:T(4,128)(2,1)S(1)} collective-permute-done((bf16[3,576]{1,0:T(4,128)(2,1)S(1)}, bf16[3,576]{1,0:T(4,128)(2,1)S(1)}, u32[]{:S(2)}, u32[]{:S(2)}) %collective-permute-start.1) | collective-permute-done | bytes 3488 | tf_op jit(solution)/shard_map/ppermute | solution.py:12
  198.5 1.9 collective-permute-start.5
  200.5 1.9 collective-permute-start.4
  202.4 1.9 collective-permute-start.3
  204.4 4.3 %collective-permute-start.2 = (bf16[5,65,128]{2,1,0:T(8,128)(2,1)S(1)}, bf16[5,65,128]{2,1,0:T(8,128)(2,1)S(1)}, u32[]{:S(2)}, u32[]{:S(2)}) collective-permute-start(bf16[5,65,128]{2,1,0:T(8,128)(2,1)S(1)} %pad_maximum_fusion.2), channel_id=1, source_target_pairs={{0,16},{16,32},{32,48},{48,64},{64,80},{80,96},{96,112},{112,128},... | collective-permute-start | bytes 249608 | tf_op jit(solution)/shard_map/ppermute | solution.py:12
  209.8 1.5 collective-permute-done.3
  211.7 1.9 collective-permute-start.6
  213.8 3.9 %collective-permute-start.7 = (bf16[5,65,128]{2,1,0:T(8,128)(2,1)S(1)}, bf16[5,65,128]{2,1,0:T(8,128)(2,1)S(1)}, u32[]{:S(2)}, u32[]{:S(2)}) collective-permute-start(bf16[5,65,128]{2,1,0:T(8,128)(2,1)S(1)} %get-tuple-element.7), channel_id=1, source_target_pairs={{0,128},{16,144},{32,160},{48,176},{64,192},{80,208},{96,224},{112... | collective-permute-start | bytes 249608 | tf_op jit(solution)/shard_map/ppermute | solution.py:12
  217.7 6.2 %collective-permute-start.8 = (bf16[5,65,128]{2,1,0:T(8,128)(2,1)S(1)}, bf16[5,65,128]{2,1,0:T(8,128)(2,1)S(1)}, u32[]{:S(2)}, u32[]{:S(2)}) collective-permute-start(bf16[5,65,128]{2,1,0:T(8,128)(2,1)S(1)} %get-tuple-element.7), channel_id=1, source_target_pairs={{0,192},{16,208},{32,224},{48,240},{64,256},{80,272},{96,288},{112... | collective-permute-start | bytes 249608 | tf_op jit(solution)/shard_map/ppermute | solution.py:12
  224.1 2.2 collective-permute-done.8
  226.5 3.8 %collective-permute-start.9 = (bf16[5,65,128]{2,1,0:T(8,128)(2,1)S(1)}, bf16[5,65,128]{2,1,0:T(8,128)(2,1)S(1)}, u32[]{:S(2)}, u32[]{:S(2)}) collective-permute-start(bf16[5,65,128]{2,1,0:T(8,128)(2,1)S(1)} %get-tuple-element.5), channel_id=1, source_target_pairs={{0,256},{16,272},{32,288},{48,304},{64,320},{80,336},{96,352},{112... | collective-permute-start | bytes 249608 | tf_op jit(solution)/shard_map/ppermute | solution.py:12
  230.9 1.4 collective-permute-start.10
  234.5 11.7 %collective-permute-start.12 = (f32[256]{0:T(256)S(1)}, f32[256]{0:T(256)S(1)}, u32[]{:S(2)}, u32[]{:S(2)}) collective-permute-start(f32[256]{0:T(256)S(1)} %get-tuple-element.35), channel_id=1, source_target_pairs={{0,1},{1,0},{2,3},{3,2},{4,5},{5,4},{6,7},{7,6},{8,9},{9,8},{10,11... | collective-permute-start | bytes 3080 | tf_op jit(solution)/shard_map/ppermute | solution.py:179
  246.3 1.3 collective-permute-done.12
  247.6 1.4 fusion
  249.2 19.7 %all_to_all.26 = bf16[256,4,1024]{2,0,1:T(8,128)(2,1)} all-to-all(bf16[256,4,1024]{2,0,1:T(8,128)(2,1)S(1)} %bitcast.132), channel_id=1, replica_groups=mesh['ctx'=64,'row'=4,'col'=4] {'row'}, dimensions={1} | all-to-all | bytes 4194304 | tf_op jit(solution)/shard_map/all_to_all | solution.py:187
  268.9 2.9 reduce_sum.31
  271.8 1.2 copy.132
  273.0 1.0 copy.133
  274.1 96.7 %all_to_all.27 = bf16[256,4,256]{2,0,1:T(8,128)(2,1)S(1)} all-to-all(bf16[256,4,256]{2,0,1:T(8,128)(2,1)} %copy.133), channel_id=1, replica_groups=mesh['ctx'=64,'row'=4,'col'=4] {'col'}, dimensions={1} | all-to-all | bytes 1048576 | tf_op jit(solution)/shard_map/all_to_all | solution.py:193
  (149 shorter events, 12.0 us)
Async XLA Ops:
  6.5 241.0 %copy-start = (bf16[5,64,4096]{2,1,0:T(8,128)(2,1)S(1)}, bf16[5,64,4096]{2,1,0:T(8,128)(2,1)}, u32[]{:S(2)}) copy-start(bf16[5,64,4096]{2,1,0:T(8,128)(2,1)} %param.25) | copy-start | bytes 7864324
  6.5 8.1 %copy-start.2 = (bf16[256,1024]{1,0:T(8,128)(2,1)S(1)}, bf16[256,1024]{1,0:T(8,128)(2,1)}, u32[]{:S(2)}) copy-start(bf16[256,1024]{1,0:T(8,128)(2,1)} %param.13) | copy-start | bytes 1572868
  6.5 169.2 %reduce-scatter.2.cloned.1.call-start = ((), (), s32[]{:S(2)}) async-start(), calls=%async_computation.3 | async-start | bytes 2027520 | tf_op jit(solution)/shard_map/reduce_scatter | solution.py:119
  14.6 5.2 %copy-start.15 = (bf16[1024,2,256]{2,1,0:T(2,128)(2,1)S(1)}, bf16[1024,2,256]{2,1,0:T(2,128)(2,1)}, u32[]{:S(2)}) copy-start(bf16[1024,2,256]{2,1,0:T(2,128)(2,1)} %param.16) | copy-start | bytes 3145732
  19.9 2.4 copy-start.3
  22.6 2.8 copy-start.16
  22.6 5.4 %copy-start.5 = (f32[4,5,64]{2,0,1:T(4,128)S(1)}, f32[4,5,64]{2,0,1:T(4,128)}, u32[]{:S(2)}) copy-start(f32[4,5,64]{2,0,1:T(4,128)} %param.17) | copy-start | bytes 15364
  22.6 162.8 %copy-start.14 = (f32[5]{0:T(128)S(1)}, f32[5]{0:T(128)}, u32[]{:S(2)}) copy-start(f32[5]{0:T(128)} %param.21) | copy-start | bytes 64
  177.3 13.7 %collective-permute-start = (bf16[256,128]{1,0:T(8,128)(2,1)S(1)}, bf16[256,128]{1,0:T(8,128)(2,1)S(1)}, u32[]{:S(2)}, u32[]{:S(2)}) collective-permute-start(bf16[256,128]{1,0:T(8,128)(2,1)S(1)} %slice.293), channel_id=1, source_target_pairs={{0,1},{1,0},{2,3},{3,2},{4,5},{5,4},{6,7},{7,6},{8,9},{9,8},{10,11... | collective-permute-start | bytes 196616 | tf_op jit(solution)/shard_map/ppermute | solution.py:126
  190.0 7.4 %copy-start.9 = (f32[1,1,256]{2,1,0:T(1,128)S(1)}, f32[1,1,256]{2,1,0:T(1,128)}, u32[]{:S(2)}) copy-start(f32[1,1,256]{2,1,0:T(1,128)} %get-tuple-element.21) | copy-start | bytes 3076
  190.0 7.4 %copy-start.10 = (f32[1,1,256]{2,1,0:T(1,128)S(1)}, f32[1,1,256]{2,1,0:T(1,128)}, u32[]{:S(2)}) copy-start(f32[1,1,256]{2,1,0:T(1,128)} %get-tuple-element.22) | copy-start | bytes 3076
  190.0 7.4 %copy-start.11 = (f32[1,1,256]{2,1,0:T(1,128)S(1)}, f32[1,1,256]{2,1,0:T(1,128)}, u32[]{:S(2)}) copy-start(f32[1,1,256]{2,1,0:T(1,128)} %get-tuple-element.23) | copy-start | bytes 3076
  190.0 7.4 %copy-start.12 = (f32[1,1,256]{2,1,0:T(1,128)S(1)}, f32[1,1,256]{2,1,0:T(1,128)}, u32[]{:S(2)}) copy-start(f32[1,1,256]{2,1,0:T(1,128)} %get-tuple-element.24) | copy-start | bytes 3076
  190.0 7.4 %copy-start.13 = (f32[1,256]{1,0:T(1,128)S(1)}, f32[1,256]{1,0:T(1,128)}, u32[]{:S(2)}) copy-start(f32[1,256]{1,0:T(1,128)} %constant_dynamic-slice_fusion.4) | copy-start | bytes 3076
  190.0 7.6 %copy-start.8 = (f32[5,64]{1,0:T(8,128)S(1)}, f32[5,64]{1,0:T(8,128)}, u32[]{:S(2)}) copy-start(f32[5,64]{1,0:T(8,128)} %param.18) | copy-start | bytes 3844
  191.1 5.9 %collective-permute-start.1 = (bf16[3,576]{1,0:T(4,128)(2,1)S(1)}, bf16[3,576]{1,0:T(4,128)(2,1)S(1)}, u32[]{:S(2)}, u32[]{:S(2)}) collective-permute-start(bf16[3,576]{1,0:T(4,128)(2,1)S(1)} %pad_maximum_fusion.3), channel_id=1, source_target_pairs={{0,16},{16,32},{32,48},{48,64},{64,80},{80,96},{96,112},{112,128},... | collective-permute-start | bytes 10376 | tf_op jit(solution)/shard_map/ppermute | solution.py:12
  197.4 12.3 %copy-start.1 = (f32[5,65,128]{2,1,0:T(8,128)S(1)}, f32[5,65,128]{2,1,0:T(8,128)}, u32[]{:S(2)}) copy-start(f32[5,65,128]{2,1,0:T(8,128)} %constant.85.clone.1) | copy-start | bytes 499204
  198.5 10.1 %collective-permute-start.5 = (bf16[5,65,128]{2,1,0:T(8,128)(2,1)S(1)}, bf16[5,65,128]{2,1,0:T(8,128)(2,1)S(1)}, u32[]{:S(2)}, u32[]{:S(2)}) collective-permute-start(bf16[5,65,128]{2,1,0:T(8,128)(2,1)S(1)} %pad_maximum_fusion.2), channel_id=1, source_target_pairs={{0,64},{16,80},{32,96},{48,112},{64,128},{80,144},{96,160},{112,17... | collective-permute-start | bytes 249608 | tf_op jit(solution)/shard_map/ppermute | solution.py:12
  200.5 9.2 %collective-permute-start.4 = (bf16[5,65,128]{2,1,0:T(8,128)(2,1)S(1)}, bf16[5,65,128]{2,1,0:T(8,128)(2,1)S(1)}, u32[]{:S(2)}, u32[]{:S(2)}) collective-permute-start(bf16[5,65,128]{2,1,0:T(8,128)(2,1)S(1)} %pad_maximum_fusion.2), channel_id=1, source_target_pairs={{0,48},{16,64},{32,80},{48,96},{64,112},{80,128},{96,144},{112,160... | collective-permute-start | bytes 249608 | tf_op jit(solution)/shard_map/ppermute | solution.py:12
  202.4 8.9 %collective-permute-start.3 = (bf16[5,65,128]{2,1,0:T(8,128)(2,1)S(1)}, bf16[5,65,128]{2,1,0:T(8,128)(2,1)S(1)}, u32[]{:S(2)}, u32[]{:S(2)}) collective-permute-start(bf16[5,65,128]{2,1,0:T(8,128)(2,1)S(1)} %pad_maximum_fusion.2), channel_id=1, source_target_pairs={{0,32},{16,48},{32,64},{48,80},{64,96},{80,112},{96,128},{112,144}... | collective-permute-start | bytes 249608 | tf_op jit(solution)/shard_map/ppermute | solution.py:12
  204.4 7.1 %collective-permute-start.2 = (bf16[5,65,128]{2,1,0:T(8,128)(2,1)S(1)}, bf16[5,65,128]{2,1,0:T(8,128)(2,1)S(1)}, u32[]{:S(2)}, u32[]{:S(2)}) collective-permute-start(bf16[5,65,128]{2,1,0:T(8,128)(2,1)S(1)} %pad_maximum_fusion.2), channel_id=1, source_target_pairs={{0,16},{16,32},{32,48},{48,64},{64,80},{80,96},{96,112},{112,128},... | collective-permute-start | bytes 249608 | tf_op jit(solution)/shard_map/ppermute | solution.py:12
  211.7 12.2 %collective-permute-start.6 = (bf16[5,65,128]{2,1,0:T(8,128)(2,1)S(1)}, bf16[5,65,128]{2,1,0:T(8,128)(2,1)S(1)}, u32[]{:S(2)}, u32[]{:S(2)}) collective-permute-start(bf16[5,65,128]{2,1,0:T(8,128)(2,1)S(1)} %get-tuple-element.7), channel_id=1, source_target_pairs={{0,64},{16,80},{32,96},{48,112},{64,128},{80,144},{96,160},{112,17... | collective-permute-start | bytes 249608 | tf_op jit(solution)/shard_map/ppermute | solution.py:12
  213.8 16.5 %copy-start.7 = (f32[5,256]{1,0:T(8,128)S(1)}, f32[5,256]{1,0:T(8,128)}, u32[]{:S(2)}) copy-start(f32[5,256]{1,0:T(8,128)} %get-tuple-element.26) | copy-start | bytes 15364
  213.8 10.2 %collective-permute-start.7 = (bf16[5,65,128]{2,1,0:T(8,128)(2,1)S(1)}, bf16[5,65,128]{2,1,0:T(8,128)(2,1)S(1)}, u32[]{:S(2)}, u32[]{:S(2)}) collective-permute-start(bf16[5,65,128]{2,1,0:T(8,128)(2,1)S(1)} %get-tuple-element.7), channel_id=1, source_target_pairs={{0,128},{16,144},{32,160},{48,176},{64,192},{80,208},{96,224},{112... | collective-permute-start | bytes 249608 | tf_op jit(solution)/shard_map/ppermute | solution.py:12
  217.7 8.7 %collective-permute-start.8 = (bf16[5,65,128]{2,1,0:T(8,128)(2,1)S(1)}, bf16[5,65,128]{2,1,0:T(8,128)(2,1)S(1)}, u32[]{:S(2)}, u32[]{:S(2)}) collective-permute-start(bf16[5,65,128]{2,1,0:T(8,128)(2,1)S(1)} %get-tuple-element.7), channel_id=1, source_target_pairs={{0,192},{16,208},{32,224},{48,240},{64,256},{80,272},{96,288},{112... | collective-permute-start | bytes 249608 | tf_op jit(solution)/shard_map/ppermute | solution.py:12
  226.5 7.3 %collective-permute-start.9 = (bf16[5,65,128]{2,1,0:T(8,128)(2,1)S(1)}, bf16[5,65,128]{2,1,0:T(8,128)(2,1)S(1)}, u32[]{:S(2)}, u32[]{:S(2)}) collective-permute-start(bf16[5,65,128]{2,1,0:T(8,128)(2,1)S(1)} %get-tuple-element.5), channel_id=1, source_target_pairs={{0,256},{16,272},{32,288},{48,304},{64,320},{80,336},{96,352},{112... | collective-permute-start | bytes 249608 | tf_op jit(solution)/shard_map/ppermute | solution.py:12
  230.9 3.2 copy-start.6
  230.9 3.2 copy-start.17
  230.9 3.0 collective-permute-start.10
  232.4 1.7 collective-permute-start.11
  234.0 13.6 %copy-start.4 = (f32[5,64]{1,0:T(8,128)S(1)}, f32[5,64]{1,0:T(8,128)}, u32[]{:S(2)}) copy-start(f32[5,64]{1,0:T(8,128)} %param.24) | copy-start | bytes 3844
  234.5 13.0 %collective-permute-start.12 = (f32[256]{0:T(256)S(1)}, f32[256]{0:T(256)S(1)}, u32[]{:S(2)}, u32[]{:S(2)}) collective-permute-start(f32[256]{0:T(256)S(1)} %get-tuple-element.35), channel_id=1, source_target_pairs={{0,1},{1,0},{2,3},{3,2},{4,5},{5,4},{6,7},{7,6},{8,9},{9,8},{10,11... | collective-permute-start | bytes 3080 | tf_op jit(solution)/shard_map/ppermute | solution.py:179
Sparse Core Ops, SparseCore 0:
  25.4 150.2 reduce-scatter.1

commit v9 on v8

--- a/solution.py
+++ b/solution.py
@@ -115,9 +115,11 @@
     dt_flat = jnp.pad(dt_flat, ((0, 0), (0, dt_rows * feat - dt_flat.shape[1])))
     dt_block = dt_flat.reshape(col_count, dt_rows, feat).transpose(1, 0, 2)
     packed = jnp.concatenate([main, dt_block], axis=0)
-    summed = lax.optimization_barrier(
-        lax.psum_scatter(packed.astype(jnp.bfloat16), "col", scatter_dimension=1, tiled=True)
-    )[:, 0]
+    crossed = lax.all_to_all(
+        packed.astype(jnp.bfloat16), "col", split_axis=1, concat_axis=1, tiled=True
+    )
+    summed_wide = jnp.sum(crossed.astype(jnp.float32), axis=1)
+    summed = summed_wide.astype(jnp.bfloat16)
     xz_width = heads_dev * 2 * head_width
     xz_sum = summed[:tok_rows, :xz_width].reshape(tok_rows, heads_dev, 2 * head_width)
     bc_pre = summed[:tok_rows, xz_width:]
@@ -130,9 +132,9 @@
             jnp.concatenate([other, bc_pre], axis=1),
         )
     dt_raw = (
-        summed[tok_rows:].reshape(-1)[: heads_dev * tok_rows]
+        summed_wide[tok_rows:].reshape(-1)[: heads_dev * tok_rows]
         .reshape(heads_dev, tok_rows)
-        .T.astype(jnp.float32)
+        .T
     )
     x_pre = xz_sum[:, :, :head_width]
     gate_z = xz_sum[:, :, head_width:]

time: 379 us -> 393 us (1.037)
  the two profiles are of different devices: /device:TPU:121 before, /device:TPU:104 now
where the time goes in v9:
time: 393 us; the launch traced here: 392 us
  waiting for transfers between devices  200 us (51%)
  blocking collectives  90.9 us (23%)
  starting transfers between devices  63.7 us (16%)
  local copies, waits for them, and re-layouts  15 us (4%)
  other arithmetic  12.4 us (3%)
  matrix products  9.44 us (2%)
    all_to_all x1, waiting for transfers between devices, body(): lax.all_to_all(packed.astype(jnp.bfloat16), 'col', split_axis=1, concat_a...  156 us
    all_to_all x1, blocking collectives, body(): lax.all_to_all(by_row, 'col', split_axis=1, concat_axis=0, tiled=True)  68.9 us
    ppermute x11, starting transfers between devices, shifted(): return lax.ppermute(block, axis, route)  32.5 us
    all_to_all x1, starting transfers between devices, body(): lax.all_to_all(packed.astype(jnp.bfloat16), 'col', split_axis=1, concat_a...  25.8 us
    ppermute x11, waiting for transfers between devices, shifted(): return lax.ppermute(block, axis, route)  23.6 us
    all_to_all x1, blocking collectives, body(): lax.all_to_all(partial_out.astype(jnp.bfloat16), 'row', split_axis=1, con...  22 us
    ppermute x1, waiting for transfers between devices, body(): group_sum = squares + lax.ppermute(squares, 'col', partner)  10.6 us
    ppermute x1, waiting for transfers between devices, body(): other = lax.ppermute(bc_pre, 'col', partner)  9.68 us
  transfers between devices with their start and end apart: 14, of which 11 were waited for; matrix products, arithmetic and copies ran while one was open for 2% of the time, Pallas kernels for 0%

profile of v9, /device:TPU:104, one launch (start us, length us, event | category | flops | bytes accessed | tf_op | source)
XLA Modules:
  0.0 392.2 jit_solution(4892110523650470017)
XLA Ops:
  0.0 8.1 %copy.120 = bf16[1024,20,128]{0,2,1:T(8,128)(2,1)} copy(bf16[1024,20,128]{2,0,1:T(8,128)(2,1)} %param.14) | data formatting | bytes 10485760 | tf_op args[1]
  8.1 5.2 %convolution_convert_fusion = bf16[256,4,640]{2,0,1:T(8,128)(2,1)} fusion(bf16[4,640,1024]{2,1,0:T(8,128)(2,1)} %bitcast.130, bf16[256,1024]{1,0:T(8,128)(2,1)S(1)} %copy-done.4), kind=kOutput, calls=%fused_computation.5 | convolution fusion | flops 1342832640 | bytes 7077888 | tf_op jit(solution)/shard_map/dot_general | solution.py:94
  13.3 1.3 convolution_convert_fusion.1
  16.0 2.6 pad_maximum_fusion
  18.7 25.8 %all-to-all-start = ((bf16[264,4,768]{2,0,1:T(8,128)(2,1)}), bf16[264,4,768]{2,0,1:T(8,128)(2,1)}, u32[]{:S(2)}, u32[]{:S(2)}) async-start(bf16[264,4,768]{2,0,1:T(8,128)(2,1)} %pad_maximum_fusion), calls=%async_computation | async-start | bytes 3244032 | tf_op jit(solution)/shard_map/all_to_all | solution.py:118
  46.0 156.0 %all-to-all-done = bf16[264,4,768]{2,0,1:T(8,128)(2,1)} async-done(((bf16[264,4,768]{2,0,1:T(8,128)(2,1)}), bf16[264,4,768]{2,0,1:T(8,128)(2,1)}, u32[]{:S(2)}, u32[]{:S(2)}) %all-to-all-start) | async-done | bytes 1622048 | tf_op jit(solution)/shard_map/all_to_all | solution.py:118
  202.0 1.8 convert_reduce_fusion
  203.9 1.9 collective-permute-start
  205.9 1.5 reduce-window.6
  209.1 9.7 %collective-permute-done = bf16[256,128]{1,0:T(8,128)(2,1)S(1)} collective-permute-done((bf16[256,128]{1,0:T(8,128)(2,1)S(1)}, bf16[256,128]{1,0:T(8,128)(2,1)S(1)}, u32[]{:S(2)}, u32[]{:S(2)}) %collective-permute-start) | collective-permute-done | bytes 65568 | tf_op jit(solution)/shard_map/ppermute | solution.py:128
  218.9 1.9 collective-permute-start.1
  221.5 2.3 collective-permute-done.1
  225.3 3.8 collective-permute-start.5
  229.1 5.2 %collective-permute-start.4 = (bf16[5,65,128]{2,1,0:T(8,128)(2,1)S(1)}, bf16[5,65,128]{2,1,0:T(8,128)(2,1)S(1)}, u32[]{:S(2)}, u32[]{:S(2)}) collective-permute-start(bf16[5,65,128]{2,1,0:T(8,128)(2,1)S(1)} %pad_maximum_fusion.2), channel_id=1, source_target_pairs={{0,48},{16,64},{32,80},{48,96},{64,112},{80,128},{96,144},{112,160... | collective-permute-start | bytes 249608 | tf_op jit(solution)/shard_map/ppermute | solution.py:12
  234.3 5.8 %collective-permute-start.3 = (bf16[5,65,128]{2,1,0:T(8,128)(2,1)S(1)}, bf16[5,65,128]{2,1,0:T(8,128)(2,1)S(1)}, u32[]{:S(2)}, u32[]{:S(2)}) collective-permute-start(bf16[5,65,128]{2,1,0:T(8,128)(2,1)S(1)} %pad_maximum_fusion.2), channel_id=1, source_target_pairs={{0,32},{16,48},{32,64},{48,80},{64,96},{80,112},{96,128},{112,144}... | collective-permute-start | bytes 249608 | tf_op jit(solution)/shard_map/ppermute | solution.py:12
  240.2 1.9 collective-permute-start.2
  243.4 2.7 collective-permute-done.2
  246.2 2.5 collective-permute-start.6
  248.9 1.9 collective-permute-start.7
  250.8 4.1 %collective-permute-start.8 = (bf16[5,65,128]{2,1,0:T(8,128)(2,1)S(1)}, bf16[5,65,128]{2,1,0:T(8,128)(2,1)S(1)}, u32[]{:S(2)}, u32[]{:S(2)}) collective-permute-start(bf16[5,65,128]{2,1,0:T(8,128)(2,1)S(1)} %get-tuple-element.7), channel_id=1, source_target_pairs={{0,192},{16,208},{32,224},{48,240},{64,256},{80,272},{96,288},{112... | collective-permute-start | bytes 249608 | tf_op jit(solution)/shard_map/ppermute | solution.py:12
  255.9 6.7 %collective-permute-done.8 = bf16[5,65,128]{2,1,0:T(8,128)(2,1)S(1)} collective-permute-done((bf16[5,65,128]{2,1,0:T(8,128)(2,1)S(1)}, bf16[5,65,128]{2,1,0:T(8,128)(2,1)S(1)}, u32[]{:S(2)}, u32[]{:S(2)}) %collective-permute-start.8) | collective-permute-done | bytes 83232 | tf_op jit(solution)/shard_map/ppermute | solution.py:12
  262.6 3.4 collective-permute-start.9
  266.6 1.3 collective-permute-start.10
  268.6 7.1 %collective-permute-done.9 = bf16[5,65,128]{2,1,0:T(8,128)(2,1)S(1)} collective-permute-done((bf16[5,65,128]{2,1,0:T(8,128)(2,1)S(1)}, bf16[5,65,128]{2,1,0:T(8,128)(2,1)S(1)}, u32[]{:S(2)}, u32[]{:S(2)}) %collective-permute-start.9) | collective-permute-done | bytes 83232 | tf_op jit(solution)/shard_map/ppermute | solution.py:12
  275.8 3.2 collective-permute-done.10
  279.6 3.5 collective-permute-start.12
  283.1 10.6 %collective-permute-done.12 = f32[256]{0:T(256)S(1)} collective-permute-done((f32[256]{0:T(256)S(1)}, f32[256]{0:T(256)S(1)}, u32[]{:S(2)}, u32[]{:S(2)}) %collective-permute-start.12) | collective-permute-done | bytes 1056 | tf_op jit(solution)/shard_map/ppermute | solution.py:181
  293.8 1.4 fusion
  295.4 22.0 %all_to_all.31 = bf16[256,4,1024]{2,0,1:T(8,128)(2,1)} all-to-all(bf16[256,4,1024]{2,0,1:T(8,128)(2,1)S(1)} %bitcast.129), channel_id=1, replica_groups=mesh['ctx'=64,'row'=4,'col'=4] {'row'}, dimensions={1} | all-to-all | bytes 4194304 | tf_op jit(solution)/shard_map/all_to_all | solution.py:189
  317.3 2.9 reduce_sum.41
  320.2 1.2 copy.132
  322.5 68.9 %all_to_all.32 = bf16[256,4,256]{2,0,1:T(8,128)(2,1)S(1)} all-to-all(bf16[256,4,256]{2,0,1:T(8,128)(2,1)} %copy.133), channel_id=1, replica_groups=mesh['ctx'=64,'row'=4,'col'=4] {'col'}, dimensions={1} | all-to-all | bytes 1048576 | tf_op jit(solution)/shard_map/all_to_all | solution.py:195
  (142 shorter events, 13.2 us)
Async XLA Ops:
  0.0 293.8 %copy-start = (bf16[5,64,4096]{2,1,0:T(8,128)(2,1)S(1)}, bf16[5,64,4096]{2,1,0:T(8,128)(2,1)}, u32[]{:S(2)}) copy-start(bf16[5,64,4096]{2,1,0:T(8,128)(2,1)} %param.25) | copy-start | bytes 7864324
  0.0 8.1 %copy-start.4 = (bf16[256,1024]{1,0:T(8,128)(2,1)S(1)}, bf16[256,1024]{1,0:T(8,128)(2,1)}, u32[]{:S(2)}) copy-start(bf16[256,1024]{1,0:T(8,128)(2,1)} %param.13) | copy-start | bytes 1572868
  8.1 5.2 %copy-start.11 = (bf16[1024,2,256]{2,1,0:T(2,128)(2,1)S(1)}, bf16[1024,2,256]{2,1,0:T(2,128)(2,1)}, u32[]{:S(2)}) copy-start(bf16[1024,2,256]{2,1,0:T(2,128)(2,1)} %param.16) | copy-start | bytes 3145732
  13.3 2.4 copy-start.5
  18.7 25.8 %copy-start.12 = (f32[5]{0:T(128)S(1)}, f32[5]{0:T(128)}, u32[]{:S(2)}) copy-start(f32[5]{0:T(128)} %param.22) | copy-start | bytes 64
  18.7 27.3 %copy-start.7 = (f32[4,5,64]{2,0,1:T(4,128)S(1)}, f32[4,5,64]{2,0,1:T(4,128)}, u32[]{:S(2)}) copy-start(f32[4,5,64]{2,0,1:T(4,128)} %param.17) | copy-start | bytes 15364
  18.7 183.3 %all-to-all-start = ((bf16[264,4,768]{2,0,1:T(8,128)(2,1)}), bf16[264,4,768]{2,0,1:T(8,128)(2,1)}, u32[]{:S(2)}, u32[]{:S(2)}) async-start(bf16[264,4,768]{2,0,1:T(8,128)(2,1)} %pad_maximum_fusion), calls=%async_computation | async-start | bytes 3244032 | tf_op jit(solution)/shard_map/all_to_all | solution.py:118
  46.0 159.8 %copy-start.9 = (f32[5]{0:T(128)S(1)}, f32[5]{0:T(128)}, u32[]{:S(2)}) copy-start(f32[5]{0:T(128)} %param.21) | copy-start | bytes 64
  203.9 14.9 %collective-permute-start = (bf16[256,128]{1,0:T(8,128)(2,1)S(1)}, bf16[256,128]{1,0:T(8,128)(2,1)S(1)}, u32[]{:S(2)}, u32[]{:S(2)}) collective-permute-start(bf16[256,128]{1,0:T(8,128)(2,1)S(1)} %slice.292), channel_id=1, source_target_pairs={{0,1},{1,0},{2,3},{3,2},{4,5},{5,4},{6,7},{7,6},{8,9},{9,8},{10,11... | collective-permute-start | bytes 196616 | tf_op jit(solution)/shard_map/ppermute | solution.py:128
  208.0 0.5 copy-start.10
  208.9 14.9 %copy-start.1 = (bf16[256,640]{0,1:T(8,128)(2,1)}, bf16[256,640]{0,1:T(8,128)(2,1)S(1)}, u32[]{:S(2)}) copy-start(bf16[256,640]{0,1:T(8,128)(2,1)S(1)} %copy.123) | copy-start | bytes 983044
  208.9 15.6 %copy-start.8 = (f32[5,64]{1,0:T(8,128)S(1)}, f32[5,64]{1,0:T(8,128)}, u32[]{:S(2)}) copy-start(f32[5,64]{1,0:T(8,128)} %param.18) | copy-start | bytes 3844
  218.9 4.9 %collective-permute-start.1 = (bf16[3,576]{1,0:T(4,128)(2,1)S(1)}, bf16[3,576]{1,0:T(4,128)(2,1)S(1)}, u32[]{:S(2)}, u32[]{:S(2)}) collective-permute-start(bf16[3,576]{1,0:T(4,128)(2,1)S(1)} %pad_maximum_fusion.3), channel_id=1, source_target_pairs={{0,16},{16,32},{32,48},{48,64},{64,80},{80,96},{96,112},{112,128},... | collective-permute-start | bytes 10376 | tf_op jit(solution)/shard_map/ppermute | solution.py:12
  224.4 17.8 %copy-start.3 = (f32[5,65,128]{2,1,0:T(8,128)S(1)}, f32[5,65,128]{2,1,0:T(8,128)}, u32[]{:S(2)}) copy-start(f32[5,65,128]{2,1,0:T(8,128)} %constant.85.clone.1) | copy-start | bytes 499204
  225.3 16.8 %collective-permute-start.5 = (bf16[5,65,128]{2,1,0:T(8,128)(2,1)S(1)}, bf16[5,65,128]{2,1,0:T(8,128)(2,1)S(1)}, u32[]{:S(2)}, u32[]{:S(2)}) collective-permute-start(bf16[5,65,128]{2,1,0:T(8,128)(2,1)S(1)} %pad_maximum_fusion.2), channel_id=1, source_target_pairs={{0,64},{16,80},{32,96},{48,112},{64,128},{80,144},{96,160},{112,17... | collective-permute-start | bytes 249608 | tf_op jit(solution)/shard_map/ppermute | solution.py:12
  229.1 13.0 %collective-permute-start.4 = (bf16[5,65,128]{2,1,0:T(8,128)(2,1)S(1)}, bf16[5,65,128]{2,1,0:T(8,128)(2,1)S(1)}, u32[]{:S(2)}, u32[]{:S(2)}) collective-permute-start(bf16[5,65,128]{2,1,0:T(8,128)(2,1)S(1)} %pad_maximum_fusion.2), channel_id=1, source_target_pairs={{0,48},{16,64},{32,80},{48,96},{64,112},{80,128},{96,144},{112,160... | collective-permute-start | bytes 249608 | tf_op jit(solution)/shard_map/ppermute | solution.py:12
  234.3 8.9 %collective-permute-start.3 = (bf16[5,65,128]{2,1,0:T(8,128)(2,1)S(1)}, bf16[5,65,128]{2,1,0:T(8,128)(2,1)S(1)}, u32[]{:S(2)}, u32[]{:S(2)}) collective-permute-start(bf16[5,65,128]{2,1,0:T(8,128)(2,1)S(1)} %pad_maximum_fusion.2), channel_id=1, source_target_pairs={{0,32},{16,48},{32,64},{48,80},{64,96},{80,112},{96,128},{112,144}... | collective-permute-start | bytes 249608 | tf_op jit(solution)/shard_map/ppermute | solution.py:12
  240.2 5.9 %collective-permute-start.2 = (bf16[5,65,128]{2,1,0:T(8,128)(2,1)S(1)}, bf16[5,65,128]{2,1,0:T(8,128)(2,1)S(1)}, u32[]{:S(2)}, u32[]{:S(2)}) collective-permute-start(bf16[5,65,128]{2,1,0:T(8,128)(2,1)S(1)} %pad_maximum_fusion.2), channel_id=1, source_target_pairs={{0,16},{16,32},{32,48},{48,64},{64,80},{80,96},{96,112},{112,128},... | collective-permute-start | bytes 249608 | tf_op jit(solution)/shard_map/ppermute | solution.py:12
  246.2 9.3 %collective-permute-start.6 = (bf16[5,65,128]{2,1,0:T(8,128)(2,1)S(1)}, bf16[5,65,128]{2,1,0:T(8,128)(2,1)S(1)}, u32[]{:S(2)}, u32[]{:S(2)}) collective-permute-start(bf16[5,65,128]{2,1,0:T(8,128)(2,1)S(1)} %get-tuple-element.7), channel_id=1, source_target_pairs={{0,64},{16,80},{32,96},{48,112},{64,128},{80,144},{96,160},{112,17... | collective-permute-start | bytes 249608 | tf_op jit(solution)/shard_map/ppermute | solution.py:12
  248.9 6.9 %collective-permute-start.7 = (bf16[5,65,128]{2,1,0:T(8,128)(2,1)S(1)}, bf16[5,65,128]{2,1,0:T(8,128)(2,1)S(1)}, u32[]{:S(2)}, u32[]{:S(2)}) collective-permute-start(bf16[5,65,128]{2,1,0:T(8,128)(2,1)S(1)} %get-tuple-element.7), channel_id=1, source_target_pairs={{0,128},{16,144},{32,160},{48,176},{64,192},{80,208},{96,224},{112... | collective-permute-start | bytes 249608 | tf_op jit(solution)/shard_map/ppermute | solution.py:12
  250.8 11.7 %collective-permute-start.8 = (bf16[5,65,128]{2,1,0:T(8,128)(2,1)S(1)}, bf16[5,65,128]{2,1,0:T(8,128)(2,1)S(1)}, u32[]{:S(2)}, u32[]{:S(2)}) collective-permute-start(bf16[5,65,128]{2,1,0:T(8,128)(2,1)S(1)} %get-tuple-element.7), channel_id=1, source_target_pairs={{0,192},{16,208},{32,224},{48,240},{64,256},{80,272},{96,288},{112... | collective-permute-start | bytes 249608 | tf_op jit(solution)/shard_map/ppermute | solution.py:12
  262.6 13.0 %collective-permute-start.9 = (bf16[5,65,128]{2,1,0:T(8,128)(2,1)S(1)}, bf16[5,65,128]{2,1,0:T(8,128)(2,1)S(1)}, u32[]{:S(2)}, u32[]{:S(2)}) collective-permute-start(bf16[5,65,128]{2,1,0:T(8,128)(2,1)S(1)} %get-tuple-element.5), channel_id=1, source_target_pairs={{0,256},{16,272},{32,288},{48,304},{64,320},{80,336},{96,352},{112... | collective-permute-start | bytes 249608 | tf_op jit(solution)/shard_map/ppermute | solution.py:12
  266.6 12.4 %collective-permute-start.10 = (bf16[5,65,128]{2,1,0:T(8,128)(2,1)S(1)}, bf16[5,65,128]{2,1,0:T(8,128)(2,1)S(1)}, u32[]{:S(2)}, u32[]{:S(2)}) collective-permute-start(bf16[5,65,128]{2,1,0:T(8,128)(2,1)S(1)} %get-tuple-element.5), channel_id=1, source_target_pairs={{0,512},{16,528},{32,544},{48,560},{64,576},{80,592},{96,608},{112... | collective-permute-start | bytes 249608 | tf_op jit(solution)/shard_map/ppermute | solution.py:12
  267.9 11.2 %collective-permute-start.11 = (bf16[5,65,128]{2,1,0:T(8,128)(2,1)S(1)}, bf16[5,65,128]{2,1,0:T(8,128)(2,1)S(1)}, u32[]{:S(2)}, u32[]{:S(2)}) collective-permute-start(bf16[5,65,128]{2,1,0:T(8,128)(2,1)S(1)} %get-tuple-element.5), channel_id=1, source_target_pairs={{0,768},{16,784},{32,800},{48,816},{64,832},{80,848},{96,864},{112... | collective-permute-start | bytes 249608 | tf_op jit(solution)/shard_map/ppermute | solution.py:12
  275.7 3.5 copy-start.2
  275.7 3.5 copy-start.13
  279.1 14.7 %copy-start.6 = (f32[5,64]{1,0:T(8,128)S(1)}, f32[5,64]{1,0:T(8,128)}, u32[]{:S(2)}) copy-start(f32[5,64]{1,0:T(8,128)} %param.24) | copy-start | bytes 3844
  279.6 14.2 %collective-permute-start.12 = (f32[256]{0:T(256)S(1)}, f32[256]{0:T(256)S(1)}, u32[]{:S(2)}, u32[]{:S(2)}) collective-permute-start(f32[256]{0:T(256)S(1)} %get-tuple-element.35), channel_id=1, source_target_pairs={{0,1},{1,0},{2,3},{3,2},{4,5},{5,4},{6,7},{7,6},{8,9},{9,8},{10,11... | collective-permute-start | bytes 3080 | tf_op jit(solution)/shard_map/ppermute | solution.py:181

commit v10 on v8

--- a/solution.py
+++ b/solution.py
@@ -91,9 +91,9 @@
     row_first = lax.axis_index("row") * col_count * heads_dev
     group_start = row_first // group_heads
     own_group = (row_first + col_index * heads_dev) // group_heads
-    xz_term = jnp.dot(
-        tokens, w_xz.reshape(w_xz.shape[0], -1), preferred_element_type=jnp.float32
-    ).reshape(tok_rows, heads_row, w_xz.shape[2])
+    xz_term = jnp.einsum(
+        "hdk,ld->lhk", jnp.transpose(w_xz, (1, 0, 2)), tokens, preferred_element_type=jnp.float32
+    )
     dt_term = jnp.dot(tokens, w_dt, preferred_element_type=jnp.float32)
     bc_part = jnp.einsum("ld,dgn->lgn", tokens, w_bc, preferred_element_type=jnp.float32)
     slot_group = (

time: 379 us -> 381 us (level)
  blocking collectives: 116 us -> 112 us
  starting transfers between devices: 49.7 us -> 53.7 us
    unnamed x50 -> x47, local copies, waits for them, and re-layouts: 8.23 us -> 0.14 us
    transpose x0 -> x1, local copies, waits for them, and re-layouts: none -> 8.08 us  [body(): jnp.transpose(w_xz, (1, 0, 2))]
    dot_general x1 -> x0, matrix products: 5.22 us -> none  [body(): jnp.dot(tokens, w_xz.reshape(w_xz.shape[0], -1), preferred_element_type=j...]
    unnamed x0 -> x1, matrix products: none -> 4.14 us
where the time goes in v10:
time: 381 us; the launch traced here: 380 us
  waiting for transfers between devices  158 us (41%)
  blocking collectives  112 us (29%)
  starting transfers between devices  53.7 us (14%)
  local copies, waits for them, and re-layouts  20.7 us (5%)
  between operations  14.3 us (4%)
  other arithmetic  12.4 us (3%)
  matrix products  9.55 us (3%)
    reduce_scatter x1, waiting for transfers between devices, body(): lax.psum_scatter(packed.astype(jnp.bfloat16), 'col', scatter_dimension=1,...  145 us
    all_to_all x1, blocking collectives, body(): lax.all_to_all(by_row, 'col', split_axis=1, concat_axis=0, tiled=True)  93.2 us
    ppermute x11, starting transfers between devices, shifted(): return lax.ppermute(block, axis, route)  31.5 us
    all_to_all x1, blocking collectives, body(): lax.all_to_all(partial_out.astype(jnp.bfloat16), 'row', split_axis=1, con...  18.6 us
    ppermute x1, starting transfers between devices, body(): group_sum = squares + lax.ppermute(squares, 'col', partner)  13.3 us
    ppermute x11, waiting for transfers between devices, shifted(): return lax.ppermute(block, axis, route)  11.5 us
    ppermute x1, starting transfers between devices, body(): other = lax.ppermute(bc_pre, 'col', partner)  8.87 us
    transpose x1, local copies, waits for them, and re-layouts, body(): jnp.transpose(w_xz, (1, 0, 2))  8.08 us
  transfers between devices with their start and end apart: 14, of which 8 were waited for; matrix products, arithmetic and copies ran while one was open for 2% of the time, Pallas kernels for 0%

profile of v10, /device:TPU:121, one launch (start us, length us, event | category | flops | bytes accessed | tf_op | source)
XLA Modules:
  0.0 380.3 jit_solution(10040011670153781035)
XLA Ops:
  6.5 8.1 %copy.128 = bf16[20,1024,128]{1,2,0:T(8,128)(2,1)} copy(bf16[20,1024,128]{2,1,0:T(8,128)(2,1)} %bitcast.133) | data formatting | bytes 10485760 | tf_op jit(solution)/shard_map/transpose | solution.py:95
  14.6 4.1 %fusion.58 = f32[256,2560]{0,1:S(1)} fusion(bf16[256,1024]{1,0:T(8,128)(2,1)S(1)} %copy-done.2, bf16[1024,2560]{0,1:T(8,128)(2,1)} %bitcast.134), kind=kOutput, calls=%fused_computation.158 | convolution fusion | flops 1342177280 | bytes 8388608
  18.8 1.2 convert.27
  20.0 2.4 copy.130
  22.4 2.5 convolution_convert_fusion
  24.9 1.1 copy.131
  26.4 2.7 pad_maximum_fusion
  29.2 1.3 constant_dynamic-slice_fusion.4
  30.5 1.4 constant_dynamic-slice_fusion.2
  31.9 145.4 %reduce-scatter.2.cloned.1.call-done = bf16[264,1,768]{2,0,1:T(8,128)(2,1)} async-done(((bf16[264,4,768]{2,0,1:T(8,128)(2,1)}), bf16[264,1,768]{2,0,1:T(8,128)(2,1)}) %reduce-scatter.2.cloned.1.call-update) | async-done | bytes 405520 | tf_op jit(solution)/shard_map/reduce_scatter | solution.py:119
  178.8 8.9 %collective-permute-start = (bf16[256,128]{1,0:T(8,128)(2,1)S(1)}, bf16[256,128]{1,0:T(8,128)(2,1)S(1)}, u32[]{:S(2)}, u32[]{:S(2)}) collective-permute-start(bf16[256,128]{1,0:T(8,128)(2,1)S(1)} %slice.293), channel_id=1, source_target_pairs={{0,1},{1,0},{2,3},{3,2},{4,5},{5,4},{6,7},{7,6},{8,9},{9,8},{10,11... | collective-permute-start | bytes 196616 | tf_op jit(solution)/shard_map/ppermute | solution.py:126
  188.4 1.5 reduce-window.6
  192.7 3.4 collective-permute-start.1
  196.1 4.6 %collective-permute-done.1 = bf16[3,576]{1,0:T(4,128)(2,1)S(1)} collective-permute-done((bf16[3,576]{1,0:T(4,128)(2,1)S(1)}, bf16[3,576]{1,0:T(4,128)(2,1)S(1)}, u32[]{:S(2)}, u32[]{:S(2)}) %collective-permute-start.1) | collective-permute-done | bytes 3488 | tf_op jit(solution)/shard_map/ppermute | solution.py:12
  202.3 1.9 collective-permute-start.5
  204.2 1.9 collective-permute-start.4
  206.2 1.9 collective-permute-start.3
  208.1 3.6 collective-permute-start.2
  212.3 1.1 collective-permute-done.3
  213.7 1.9 collective-permute-start.6
  215.8 6.5 %collective-permute-start.7 = (bf16[5,65,128]{2,1,0:T(8,128)(2,1)S(1)}, bf16[5,65,128]{2,1,0:T(8,128)(2,1)S(1)}, u32[]{:S(2)}, u32[]{:S(2)}) collective-permute-start(bf16[5,65,128]{2,1,0:T(8,128)(2,1)S(1)} %get-tuple-element.7), channel_id=1, source_target_pairs={{0,128},{16,144},{32,160},{48,176},{64,192},{80,208},{96,224},{112... | collective-permute-start | bytes 249608 | tf_op jit(solution)/shard_map/ppermute | solution.py:12
  222.3 4.8 %collective-permute-start.8 = (bf16[5,65,128]{2,1,0:T(8,128)(2,1)S(1)}, bf16[5,65,128]{2,1,0:T(8,128)(2,1)S(1)}, u32[]{:S(2)}, u32[]{:S(2)}) collective-permute-start(bf16[5,65,128]{2,1,0:T(8,128)(2,1)S(1)} %get-tuple-element.7), channel_id=1, source_target_pairs={{0,192},{16,208},{32,224},{48,240},{64,256},{80,272},{96,288},{112... | collective-permute-start | bytes 249608 | tf_op jit(solution)/shard_map/ppermute | solution.py:12
  227.4 3.4 collective-permute-done.8
  230.9 3.4 collective-permute-start.9
  234.9 1.4 collective-permute-start.10
  237.1 1.0 collective-permute-done.9
  239.8 13.3 %collective-permute-start.12 = (f32[256]{0:T(256)S(1)}, f32[256]{0:T(256)S(1)}, u32[]{:S(2)}, u32[]{:S(2)}) collective-permute-start(f32[256]{0:T(256)S(1)} %get-tuple-element.35), channel_id=1, source_target_pairs={{0,1},{1,0},{2,3},{3,2},{4,5},{5,4},{6,7},{7,6},{8,9},{9,8},{10,11... | collective-permute-start | bytes 3080 | tf_op jit(solution)/shard_map/ppermute | solution.py:179
  254.1 1.4 fusion
  255.7 18.6 %all_to_all.26 = bf16[256,4,1024]{2,0,1:T(8,128)(2,1)} all-to-all(bf16[256,4,1024]{2,0,1:T(8,128)(2,1)S(1)} %bitcast.132), channel_id=1, replica_groups=mesh['ctx'=64,'row'=4,'col'=4] {'row'}, dimensions={1} | all-to-all | bytes 4194304 | tf_op jit(solution)/shard_map/all_to_all | solution.py:187
  274.3 2.9 reduce_sum.31
  277.2 1.2 copy.141
  279.5 93.2 %all_to_all.27 = bf16[256,4,256]{2,0,1:T(8,128)(2,1)S(1)} all-to-all(bf16[256,4,256]{2,0,1:T(8,128)(2,1)} %copy.142), channel_id=1, replica_groups=mesh['ctx'=64,'row'=4,'col'=4] {'col'}, dimensions={1} | all-to-all | bytes 1048576 | tf_op jit(solution)/shard_map/all_to_all | solution.py:193
  (149 shorter events, 13.8 us)
Async XLA Ops:
  6.5 247.5 %copy-start = (bf16[5,64,4096]{2,1,0:T(8,128)(2,1)S(1)}, bf16[5,64,4096]{2,1,0:T(8,128)(2,1)}, u32[]{:S(2)}) copy-start(bf16[5,64,4096]{2,1,0:T(8,128)(2,1)} %param.25) | copy-start | bytes 7864324
  6.5 170.7 %reduce-scatter.2.cloned.1.call-start = ((), (), s32[]{:S(2)}) async-start(), calls=%async_computation.3 | async-start | bytes 2027520 | tf_op jit(solution)/shard_map/reduce_scatter | solution.py:119
  6.5 8.1 %copy-start.2 = (bf16[256,1024]{1,0:T(8,128)(2,1)S(1)}, bf16[256,1024]{1,0:T(8,128)(2,1)}, u32[]{:S(2)}) copy-start(bf16[256,1024]{1,0:T(8,128)(2,1)} %param.13) | copy-start | bytes 1572868
  20.0 6.0 %copy-start.3 = (bf16[1024,20]{0,1:T(8,128)(2,1)S(1)}, bf16[1024,20]{0,1:T(8,128)(2,1)}, u32[]{:S(2)}) copy-start(bf16[1024,20]{0,1:T(8,128)(2,1)} %param.15) | copy-start | bytes 122884
  26.4 2.8 copy-start.15
  26.4 5.4 %copy-start.5 = (f32[4,5,64]{2,0,1:T(4,128)S(1)}, f32[4,5,64]{2,0,1:T(4,128)}, u32[]{:S(2)}) copy-start(f32[4,5,64]{2,0,1:T(4,128)} %param.17) | copy-start | bytes 15364
  26.4 161.3 %copy-start.14 = (f32[5]{0:T(128)S(1)}, f32[5]{0:T(128)}, u32[]{:S(2)}) copy-start(f32[5]{0:T(128)} %param.21) | copy-start | bytes 64
  178.8 13.8 %collective-permute-start = (bf16[256,128]{1,0:T(8,128)(2,1)S(1)}, bf16[256,128]{1,0:T(8,128)(2,1)S(1)}, u32[]{:S(2)}, u32[]{:S(2)}) collective-permute-start(bf16[256,128]{1,0:T(8,128)(2,1)S(1)} %slice.293), channel_id=1, source_target_pairs={{0,1},{1,0},{2,3},{3,2},{4,5},{5,4},{6,7},{7,6},{8,9},{9,8},{10,11... | collective-permute-start | bytes 196616 | tf_op jit(solution)/shard_map/ppermute | solution.py:126
  192.3 8.9 %copy-start.9 = (f32[1,1,256]{2,1,0:T(1,128)S(1)}, f32[1,1,256]{2,1,0:T(1,128)}, u32[]{:S(2)}) copy-start(f32[1,1,256]{2,1,0:T(1,128)} %get-tuple-element.21) | copy-start | bytes 3076
  192.3 8.9 %copy-start.10 = (f32[1,1,256]{2,1,0:T(1,128)S(1)}, f32[1,1,256]{2,1,0:T(1,128)}, u32[]{:S(2)}) copy-start(f32[1,1,256]{2,1,0:T(1,128)} %get-tuple-element.22) | copy-start | bytes 3076
  192.3 8.9 %copy-start.11 = (f32[1,1,256]{2,1,0:T(1,128)S(1)}, f32[1,1,256]{2,1,0:T(1,128)}, u32[]{:S(2)}) copy-start(f32[1,1,256]{2,1,0:T(1,128)} %get-tuple-element.23) | copy-start | bytes 3076
  192.3 8.9 %copy-start.12 = (f32[1,1,256]{2,1,0:T(1,128)S(1)}, f32[1,1,256]{2,1,0:T(1,128)}, u32[]{:S(2)}) copy-start(f32[1,1,256]{2,1,0:T(1,128)} %get-tuple-element.24) | copy-start | bytes 3076
  192.3 8.9 %copy-start.13 = (f32[1,256]{1,0:T(1,128)S(1)}, f32[1,256]{1,0:T(1,128)}, u32[]{:S(2)}) copy-start(f32[1,256]{1,0:T(1,128)} %constant_dynamic-slice_fusion.4) | copy-start | bytes 3076
  192.3 9.1 %copy-start.8 = (f32[5,64]{1,0:T(8,128)S(1)}, f32[5,64]{1,0:T(8,128)}, u32[]{:S(2)}) copy-start(f32[5,64]{1,0:T(8,128)} %param.18) | copy-start | bytes 3844
  192.7 8.0 %collective-permute-start.1 = (bf16[3,576]{1,0:T(4,128)(2,1)S(1)}, bf16[3,576]{1,0:T(4,128)(2,1)S(1)}, u32[]{:S(2)}, u32[]{:S(2)}) collective-permute-start(bf16[3,576]{1,0:T(4,128)(2,1)S(1)} %pad_maximum_fusion.3), channel_id=1, source_target_pairs={{0,16},{16,32},{32,48},{48,64},{64,80},{80,96},{96,112},{112,128},... | collective-permute-start | bytes 10376 | tf_op jit(solution)/shard_map/ppermute | solution.py:12
  201.1 11.1 %copy-start.1 = (f32[5,65,128]{2,1,0:T(8,128)S(1)}, f32[5,65,128]{2,1,0:T(8,128)}, u32[]{:S(2)}) copy-start(f32[5,65,128]{2,1,0:T(8,128)} %constant.85.clone.1) | copy-start | bytes 499204
  202.3 9.5 %collective-permute-start.5 = (bf16[5,65,128]{2,1,0:T(8,128)(2,1)S(1)}, bf16[5,65,128]{2,1,0:T(8,128)(2,1)S(1)}, u32[]{:S(2)}, u32[]{:S(2)}) collective-permute-start(bf16[5,65,128]{2,1,0:T(8,128)(2,1)S(1)} %pad_maximum_fusion.2), channel_id=1, source_target_pairs={{0,64},{16,80},{32,96},{48,112},{64,128},{80,144},{96,160},{112,17... | collective-permute-start | bytes 249608 | tf_op jit(solution)/shard_map/ppermute | solution.py:12
  204.2 8.0 %collective-permute-start.4 = (bf16[5,65,128]{2,1,0:T(8,128)(2,1)S(1)}, bf16[5,65,128]{2,1,0:T(8,128)(2,1)S(1)}, u32[]{:S(2)}, u32[]{:S(2)}) collective-permute-start(bf16[5,65,128]{2,1,0:T(8,128)(2,1)S(1)} %pad_maximum_fusion.2), channel_id=1, source_target_pairs={{0,48},{16,64},{32,80},{48,96},{64,112},{80,128},{96,144},{112,160... | collective-permute-start | bytes 249608 | tf_op jit(solution)/shard_map/ppermute | solution.py:12
  206.2 7.2 %collective-permute-start.3 = (bf16[5,65,128]{2,1,0:T(8,128)(2,1)S(1)}, bf16[5,65,128]{2,1,0:T(8,128)(2,1)S(1)}, u32[]{:S(2)}, u32[]{:S(2)}) collective-permute-start(bf16[5,65,128]{2,1,0:T(8,128)(2,1)S(1)} %pad_maximum_fusion.2), channel_id=1, source_target_pairs={{0,32},{16,48},{32,64},{48,80},{64,96},{80,112},{96,128},{112,144}... | collective-permute-start | bytes 249608 | tf_op jit(solution)/shard_map/ppermute | solution.py:12
  208.1 5.4 %collective-permute-start.2 = (bf16[5,65,128]{2,1,0:T(8,128)(2,1)S(1)}, bf16[5,65,128]{2,1,0:T(8,128)(2,1)S(1)}, u32[]{:S(2)}, u32[]{:S(2)}) collective-permute-start(bf16[5,65,128]{2,1,0:T(8,128)(2,1)S(1)} %pad_maximum_fusion.2), channel_id=1, source_target_pairs={{0,16},{16,32},{32,48},{48,64},{64,80},{80,96},{96,112},{112,128},... | collective-permute-start | bytes 249608 | tf_op jit(solution)/shard_map/ppermute | solution.py:12
  213.7 13.4 %collective-permute-start.6 = (bf16[5,65,128]{2,1,0:T(8,128)(2,1)S(1)}, bf16[5,65,128]{2,1,0:T(8,128)(2,1)S(1)}, u32[]{:S(2)}, u32[]{:S(2)}) collective-permute-start(bf16[5,65,128]{2,1,0:T(8,128)(2,1)S(1)} %get-tuple-element.7), channel_id=1, source_target_pairs={{0,64},{16,80},{32,96},{48,112},{64,128},{80,144},{96,160},{112,17... | collective-permute-start | bytes 249608 | tf_op jit(solution)/shard_map/ppermute | solution.py:12
  215.8 18.5 %copy-start.7 = (f32[5,256]{1,0:T(8,128)S(1)}, f32[5,256]{1,0:T(8,128)}, u32[]{:S(2)}) copy-start(f32[5,256]{1,0:T(8,128)} %get-tuple-element.26) | copy-start | bytes 15364
  215.8 11.4 %collective-permute-start.7 = (bf16[5,65,128]{2,1,0:T(8,128)(2,1)S(1)}, bf16[5,65,128]{2,1,0:T(8,128)(2,1)S(1)}, u32[]{:S(2)}, u32[]{:S(2)}) collective-permute-start(bf16[5,65,128]{2,1,0:T(8,128)(2,1)S(1)} %get-tuple-element.7), channel_id=1, source_target_pairs={{0,128},{16,144},{32,160},{48,176},{64,192},{80,208},{96,224},{112... | collective-permute-start | bytes 249608 | tf_op jit(solution)/shard_map/ppermute | solution.py:12
  222.3 8.5 %collective-permute-start.8 = (bf16[5,65,128]{2,1,0:T(8,128)(2,1)S(1)}, bf16[5,65,128]{2,1,0:T(8,128)(2,1)S(1)}, u32[]{:S(2)}, u32[]{:S(2)}) collective-permute-start(bf16[5,65,128]{2,1,0:T(8,128)(2,1)S(1)} %get-tuple-element.7), channel_id=1, source_target_pairs={{0,192},{16,208},{32,224},{48,240},{64,256},{80,272},{96,288},{112... | collective-permute-start | bytes 249608 | tf_op jit(solution)/shard_map/ppermute | solution.py:12
  230.9 7.2 %collective-permute-start.9 = (bf16[5,65,128]{2,1,0:T(8,128)(2,1)S(1)}, bf16[5,65,128]{2,1,0:T(8,128)(2,1)S(1)}, u32[]{:S(2)}, u32[]{:S(2)}) collective-permute-start(bf16[5,65,128]{2,1,0:T(8,128)(2,1)S(1)} %get-tuple-element.5), channel_id=1, source_target_pairs={{0,256},{16,272},{32,288},{48,304},{64,320},{80,336},{96,352},{112... | collective-permute-start | bytes 249608 | tf_op jit(solution)/shard_map/ppermute | solution.py:12
  234.9 4.4 %copy-start.6 = (f32[256,5]{0,1:T(8,128)S(1)}, f32[256,5]{0,1:T(8,128)}, u32[]{:S(2)}) copy-start(f32[256,5]{0,1:T(8,128)} %get-tuple-element.31) | copy-start | bytes 15364
  234.9 4.4 %copy-start.16 = (f32[5]{0:T(128)S(1)}, f32[5]{0:T(128)}, u32[]{:S(2)}) copy-start(f32[5]{0:T(128)} %param.23) | copy-start | bytes 64
  234.9 4.2 %collective-permute-start.10 = (bf16[5,65,128]{2,1,0:T(8,128)(2,1)S(1)}, bf16[5,65,128]{2,1,0:T(8,128)(2,1)S(1)}, u32[]{:S(2)}, u32[]{:S(2)}) collective-permute-start(bf16[5,65,128]{2,1,0:T(8,128)(2,1)S(1)} %get-tuple-element.5), channel_id=1, source_target_pairs={{0,512},{16,528},{32,544},{48,560},{64,576},{80,592},{96,608},{112... | collective-permute-start | bytes 249608 | tf_op jit(solution)/shard_map/ppermute | solution.py:12
  236.4 2.9 collective-permute-start.11
  239.2 14.9 %copy-start.4 = (f32[5,64]{1,0:T(8,128)S(1)}, f32[5,64]{1,0:T(8,128)}, u32[]{:S(2)}) copy-start(f32[5,64]{1,0:T(8,128)} %param.24) | copy-start | bytes 3844
  239.8 14.3 %collective-permute-start.12 = (f32[256]{0:T(256)S(1)}, f32[256]{0:T(256)S(1)}, u32[]{:S(2)}, u32[]{:S(2)}) collective-permute-start(f32[256]{0:T(256)S(1)} %get-tuple-element.35), channel_id=1, source_target_pairs={{0,1},{1,0},{2,3},{3,2},{4,5},{5,4},{6,7},{7,6},{8,9},{9,8},{10,11... | collective-permute-start | bytes 3080 | tf_op jit(solution)/shard_map/ppermute | solution.py:179
Sparse Core Ops, SparseCore 0:
  29.2 147.9 reduce-scatter.1

commit v11 on v8

--- a/solution.py
+++ b/solution.py
@@ -111,7 +111,7 @@
     main = jnp.concatenate([xz_slots, bc_slots], axis=2)
     feat = main.shape[2]
     dt_flat = dt_term.reshape(tok_rows, col_count, heads_dev).transpose(1, 2, 0).reshape(col_count, -1)
-    dt_rows = -(-dt_flat.shape[1] // (8 * feat)) * 8
+    dt_rows = -(-dt_flat.shape[1] // feat)
     dt_flat = jnp.pad(dt_flat, ((0, 0), (0, dt_rows * feat - dt_flat.shape[1])))
     dt_block = dt_flat.reshape(col_count, dt_rows, feat).transpose(1, 0, 2)
     packed = jnp.concatenate([main, dt_block], axis=0)

time: 379 us -> 379 us (level)
    unnamed x50 -> x49, local copies, waits for them, and re-layouts: 8.23 us -> 8.22 us
where the time goes in v11:
time: 379 us; the launch traced here: 378 us
  waiting for transfers between devices  159 us (42%)
  blocking collectives  116 us (31%)
  starting transfers between devices  49.7 us (13%)
  local copies, waits for them, and re-layouts  18.3 us (5%)
  between operations  14.3 us (4%)
  other arithmetic  11.1 us (3%)
  matrix products  9.42 us (2%)
    reduce_scatter x1, waiting for transfers between devices, body(): lax.psum_scatter(packed.astype(jnp.bfloat16), 'col', scatter_dimension=1,...  148 us
    all_to_all x1, blocking collectives, body(): lax.all_to_all(by_row, 'col', split_axis=1, concat_axis=0, tiled=True)  96.7 us
    ppermute x11, starting transfers between devices, shifted(): return lax.ppermute(block, axis, route)  29.9 us
    all_to_all x1, blocking collectives, body(): lax.all_to_all(partial_out.astype(jnp.bfloat16), 'row', split_axis=1, con...  19.7 us
    ppermute x1, starting transfers between devices, body(): group_sum = squares + lax.ppermute(squares, 'col', partner)  11.7 us
    ppermute x11, waiting for transfers between devices, shifted(): return lax.ppermute(block, axis, route)  9.45 us
    unnamed x49, local copies, waits for them, and re-layouts  8.22 us
    ppermute x1, starting transfers between devices, body(): other = lax.ppermute(bc_pre, 'col', partner)  8.09 us
  transfers between devices with their start and end apart: 14, of which 8 were waited for; matrix products, arithmetic and copies ran while one was open for 2% of the time, Pallas kernels for 0%

profile of v11, /device:TPU:121, one launch (start us, length us, event | category | flops | bytes accessed | tf_op | source)
XLA Modules:
  0.0 378.4 jit_solution(7556584425993202377)
XLA Ops:
  6.5 8.1 %copy.120 = bf16[1024,20,128]{0,2,1:T(8,128)(2,1)} copy(bf16[1024,20,128]{2,0,1:T(8,128)(2,1)} %param.14) | data formatting | bytes 10485760 | tf_op args[1]
  14.6 5.2 %convolution_convert_fusion = bf16[256,4,640]{2,0,1:T(8,128)(2,1)} fusion(bf16[4,640,1024]{2,1,0:T(8,128)(2,1)} %bitcast.127, bf16[256,1024]{1,0:T(8,128)(2,1)S(1)} %copy-done.2), kind=kOutput, calls=%fused_computation.4 | convolution fusion | flops 1342832640 | bytes 7077888 | tf_op jit(solution)/shard_map/dot_general | solution.py:94
  19.9 1.3 convolution_convert_fusion.1
  21.1 1.1 copy.122
  22.6 2.7 pad_maximum_fusion
  25.4 1.3 constant_dynamic-slice_fusion.4
  26.7 1.3 constant_dynamic-slice_fusion.2
  28.1 147.7 %reduce-scatter.2.cloned.1.call-done = bf16[258,1,768]{2,0,1:T(8,128)(2,1)} async-done(((bf16[258,4,768]{2,0,1:T(8,128)(2,1)}), bf16[258,1,768]{2,0,1:T(8,128)(2,1)}) %reduce-scatter.2.cloned.1.call-update) | async-done | bytes 396304 | tf_op jit(solution)/shard_map/reduce_scatter | solution.py:119
  177.3 8.1 %collective-permute-start = (bf16[256,128]{1,0:T(8,128)(2,1)S(1)}, bf16[256,128]{1,0:T(8,128)(2,1)S(1)}, u32[]{:S(2)}, u32[]{:S(2)}) collective-permute-start(bf16[256,128]{1,0:T(8,128)(2,1)S(1)} %slice.293), channel_id=1, source_target_pairs={{0,1},{1,0},{2,3},{3,2},{4,5},{5,4},{6,7},{7,6},{8,9},{9,8},{10,11... | collective-permute-start | bytes 196616 | tf_op jit(solution)/shard_map/ppermute | solution.py:126
  186.1 1.5 reduce-window.6
  188.8 1.0 slice.291
  191.1 1.9 collective-permute-start.1
  193.1 3.9 %collective-permute-done.1 = bf16[3,576]{1,0:T(4,128)(2,1)S(1)} collective-permute-done((bf16[3,576]{1,0:T(4,128)(2,1)S(1)}, bf16[3,576]{1,0:T(4,128)(2,1)S(1)}, u32[]{:S(2)}, u32[]{:S(2)}) %collective-permute-start.1) | collective-permute-done | bytes 3488 | tf_op jit(solution)/shard_map/ppermute | solution.py:12
  198.5 1.9 collective-permute-start.5
  200.5 1.9 collective-permute-start.4
  202.4 1.9 collective-permute-start.3
  204.4 4.3 %collective-permute-start.2 = (bf16[5,65,128]{2,1,0:T(8,128)(2,1)S(1)}, bf16[5,65,128]{2,1,0:T(8,128)(2,1)S(1)}, u32[]{:S(2)}, u32[]{:S(2)}) collective-permute-start(bf16[5,65,128]{2,1,0:T(8,128)(2,1)S(1)} %pad_maximum_fusion.2), channel_id=1, source_target_pairs={{0,16},{16,32},{32,48},{48,64},{64,80},{80,96},{96,112},{112,128},... | collective-permute-start | bytes 249608 | tf_op jit(solution)/shard_map/ppermute | solution.py:12
  209.9 1.5 collective-permute-done.3
  211.7 1.9 collective-permute-start.6
  213.8 3.8 %collective-permute-start.7 = (bf16[5,65,128]{2,1,0:T(8,128)(2,1)S(1)}, bf16[5,65,128]{2,1,0:T(8,128)(2,1)S(1)}, u32[]{:S(2)}, u32[]{:S(2)}) collective-permute-start(bf16[5,65,128]{2,1,0:T(8,128)(2,1)S(1)} %get-tuple-element.7), channel_id=1, source_target_pairs={{0,128},{16,144},{32,160},{48,176},{64,192},{80,208},{96,224},{112... | collective-permute-start | bytes 249608 | tf_op jit(solution)/shard_map/ppermute | solution.py:12
  217.7 6.2 %collective-permute-start.8 = (bf16[5,65,128]{2,1,0:T(8,128)(2,1)S(1)}, bf16[5,65,128]{2,1,0:T(8,128)(2,1)S(1)}, u32[]{:S(2)}, u32[]{:S(2)}) collective-permute-start(bf16[5,65,128]{2,1,0:T(8,128)(2,1)S(1)} %get-tuple-element.7), channel_id=1, source_target_pairs={{0,192},{16,208},{32,224},{48,240},{64,256},{80,272},{96,288},{112... | collective-permute-start | bytes 249608 | tf_op jit(solution)/shard_map/ppermute | solution.py:12
  224.1 2.2 collective-permute-done.8
  226.5 3.8 %collective-permute-start.9 = (bf16[5,65,128]{2,1,0:T(8,128)(2,1)S(1)}, bf16[5,65,128]{2,1,0:T(8,128)(2,1)S(1)}, u32[]{:S(2)}, u32[]{:S(2)}) collective-permute-start(bf16[5,65,128]{2,1,0:T(8,128)(2,1)S(1)} %get-tuple-element.5), channel_id=1, source_target_pairs={{0,256},{16,272},{32,288},{48,304},{64,320},{80,336},{96,352},{112... | collective-permute-start | bytes 249608 | tf_op jit(solution)/shard_map/ppermute | solution.py:12
  230.9 1.4 collective-permute-start.10
  234.5 11.7 %collective-permute-start.12 = (f32[256]{0:T(256)S(1)}, f32[256]{0:T(256)S(1)}, u32[]{:S(2)}, u32[]{:S(2)}) collective-permute-start(f32[256]{0:T(256)S(1)} %get-tuple-element.35), channel_id=1, source_target_pairs={{0,1},{1,0},{2,3},{3,2},{4,5},{5,4},{6,7},{7,6},{8,9},{9,8},{10,11... | collective-permute-start | bytes 3080 | tf_op jit(solution)/shard_map/ppermute | solution.py:179
  246.3 1.3 collective-permute-done.12
  247.6 1.4 fusion
  249.2 19.7 %all_to_all.26 = bf16[256,4,1024]{2,0,1:T(8,128)(2,1)} all-to-all(bf16[256,4,1024]{2,0,1:T(8,128)(2,1)S(1)} %bitcast.126), channel_id=1, replica_groups=mesh['ctx'=64,'row'=4,'col'=4] {'row'}, dimensions={1} | all-to-all | bytes 4194304 | tf_op jit(solution)/shard_map/all_to_all | solution.py:187
  268.8 2.9 reduce_sum.31
  271.8 1.2 copy.132
  273.0 1.0 copy.133
  274.0 96.7 %all_to_all.27 = bf16[256,4,256]{2,0,1:T(8,128)(2,1)S(1)} all-to-all(bf16[256,4,256]{2,0,1:T(8,128)(2,1)} %copy.133), channel_id=1, replica_groups=mesh['ctx'=64,'row'=4,'col'=4] {'col'}, dimensions={1} | all-to-all | bytes 1048576 | tf_op jit(solution)/shard_map/all_to_all | solution.py:193
  (149 shorter events, 12.0 us)
Async XLA Ops:
  6.5 241.0 %copy-start = (bf16[5,64,4096]{2,1,0:T(8,128)(2,1)S(1)}, bf16[5,64,4096]{2,1,0:T(8,128)(2,1)}, u32[]{:S(2)}) copy-start(bf16[5,64,4096]{2,1,0:T(8,128)(2,1)} %param.25) | copy-start | bytes 7864324
  6.5 8.1 %copy-start.2 = (bf16[256,1024]{1,0:T(8,128)(2,1)S(1)}, bf16[256,1024]{1,0:T(8,128)(2,1)}, u32[]{:S(2)}) copy-start(bf16[256,1024]{1,0:T(8,128)(2,1)} %param.13) | copy-start | bytes 1572868
  6.5 169.2 %reduce-scatter.2.cloned.1.call-start = ((), (), s32[]{:S(2)}) async-start(), calls=%async_computation.3 | async-start | bytes 2027520 | tf_op jit(solution)/shard_map/reduce_scatter | solution.py:119
  14.6 5.2 %copy-start.15 = (bf16[1024,2,256]{2,1,0:T(2,128)(2,1)S(1)}, bf16[1024,2,256]{2,1,0:T(2,128)(2,1)}, u32[]{:S(2)}) copy-start(bf16[1024,2,256]{2,1,0:T(2,128)(2,1)} %param.16) | copy-start | bytes 3145732
  19.9 2.4 copy-start.3
  22.6 2.8 copy-start.16
  22.6 5.4 %copy-start.5 = (f32[4,5,64]{2,0,1:T(4,128)S(1)}, f32[4,5,64]{2,0,1:T(4,128)}, u32[]{:S(2)}) copy-start(f32[4,5,64]{2,0,1:T(4,128)} %param.17) | copy-start | bytes 15364
  22.6 162.8 %copy-start.14 = (f32[5]{0:T(128)S(1)}, f32[5]{0:T(128)}, u32[]{:S(2)}) copy-start(f32[5]{0:T(128)} %param.21) | copy-start | bytes 64
  177.3 13.7 %collective-permute-start = (bf16[256,128]{1,0:T(8,128)(2,1)S(1)}, bf16[256,128]{1,0:T(8,128)(2,1)S(1)}, u32[]{:S(2)}, u32[]{:S(2)}) collective-permute-start(bf16[256,128]{1,0:T(8,128)(2,1)S(1)} %slice.293), channel_id=1, source_target_pairs={{0,1},{1,0},{2,3},{3,2},{4,5},{5,4},{6,7},{7,6},{8,9},{9,8},{10,11... | collective-permute-start | bytes 196616 | tf_op jit(solution)/shard_map/ppermute | solution.py:126
  190.0 7.4 %copy-start.9 = (f32[1,1,256]{2,1,0:T(1,128)S(1)}, f32[1,1,256]{2,1,0:T(1,128)}, u32[]{:S(2)}) copy-start(f32[1,1,256]{2,1,0:T(1,128)} %get-tuple-element.21) | copy-start | bytes 3076
  190.0 7.4 %copy-start.10 = (f32[1,1,256]{2,1,0:T(1,128)S(1)}, f32[1,1,256]{2,1,0:T(1,128)}, u32[]{:S(2)}) copy-start(f32[1,1,256]{2,1,0:T(1,128)} %get-tuple-element.22) | copy-start | bytes 3076
  190.0 7.4 %copy-start.11 = (f32[1,1,256]{2,1,0:T(1,128)S(1)}, f32[1,1,256]{2,1,0:T(1,128)}, u32[]{:S(2)}) copy-start(f32[1,1,256]{2,1,0:T(1,128)} %get-tuple-element.23) | copy-start | bytes 3076
  190.0 7.4 %copy-start.12 = (f32[1,1,256]{2,1,0:T(1,128)S(1)}, f32[1,1,256]{2,1,0:T(1,128)}, u32[]{:S(2)}) copy-start(f32[1,1,256]{2,1,0:T(1,128)} %get-tuple-element.24) | copy-start | bytes 3076
  190.0 7.4 %copy-start.13 = (f32[1,256]{1,0:T(1,128)S(1)}, f32[1,256]{1,0:T(1,128)}, u32[]{:S(2)}) copy-start(f32[1,256]{1,0:T(1,128)} %constant_dynamic-slice_fusion.4) | copy-start | bytes 3076
  190.0 7.6 %copy-start.8 = (f32[5,64]{1,0:T(8,128)S(1)}, f32[5,64]{1,0:T(8,128)}, u32[]{:S(2)}) copy-start(f32[5,64]{1,0:T(8,128)} %param.18) | copy-start | bytes 3844
  191.1 5.9 %collective-permute-start.1 = (bf16[3,576]{1,0:T(4,128)(2,1)S(1)}, bf16[3,576]{1,0:T(4,128)(2,1)S(1)}, u32[]{:S(2)}, u32[]{:S(2)}) collective-permute-start(bf16[3,576]{1,0:T(4,128)(2,1)S(1)} %pad_maximum_fusion.3), channel_id=1, source_target_pairs={{0,16},{16,32},{32,48},{48,64},{64,80},{80,96},{96,112},{112,128},... | collective-permute-start | bytes 10376 | tf_op jit(solution)/shard_map/ppermute | solution.py:12
  197.4 12.3 %copy-start.1 = (f32[5,65,128]{2,1,0:T(8,128)S(1)}, f32[5,65,128]{2,1,0:T(8,128)}, u32[]{:S(2)}) copy-start(f32[5,65,128]{2,1,0:T(8,128)} %constant.85.clone.1) | copy-start | bytes 499204
  198.5 10.1 %collective-permute-start.5 = (bf16[5,65,128]{2,1,0:T(8,128)(2,1)S(1)}, bf16[5,65,128]{2,1,0:T(8,128)(2,1)S(1)}, u32[]{:S(2)}, u32[]{:S(2)}) collective-permute-start(bf16[5,65,128]{2,1,0:T(8,128)(2,1)S(1)} %pad_maximum_fusion.2), channel_id=1, source_target_pairs={{0,64},{16,80},{32,96},{48,112},{64,128},{80,144},{96,160},{112,17... | collective-permute-start | bytes 249608 | tf_op jit(solution)/shard_map/ppermute | solution.py:12
  200.5 9.2 %collective-permute-start.4 = (bf16[5,65,128]{2,1,0:T(8,128)(2,1)S(1)}, bf16[5,65,128]{2,1,0:T(8,128)(2,1)S(1)}, u32[]{:S(2)}, u32[]{:S(2)}) collective-permute-start(bf16[5,65,128]{2,1,0:T(8,128)(2,1)S(1)} %pad_maximum_fusion.2), channel_id=1, source_target_pairs={{0,48},{16,64},{32,80},{48,96},{64,112},{80,128},{96,144},{112,160... | collective-permute-start | bytes 249608 | tf_op jit(solution)/shard_map/ppermute | solution.py:12
  202.4 8.9 %collective-permute-start.3 = (bf16[5,65,128]{2,1,0:T(8,128)(2,1)S(1)}, bf16[5,65,128]{2,1,0:T(8,128)(2,1)S(1)}, u32[]{:S(2)}, u32[]{:S(2)}) collective-permute-start(bf16[5,65,128]{2,1,0:T(8,128)(2,1)S(1)} %pad_maximum_fusion.2), channel_id=1, source_target_pairs={{0,32},{16,48},{32,64},{48,80},{64,96},{80,112},{96,128},{112,144}... | collective-permute-start | bytes 249608 | tf_op jit(solution)/shard_map/ppermute | solution.py:12
  204.4 7.1 %collective-permute-start.2 = (bf16[5,65,128]{2,1,0:T(8,128)(2,1)S(1)}, bf16[5,65,128]{2,1,0:T(8,128)(2,1)S(1)}, u32[]{:S(2)}, u32[]{:S(2)}) collective-permute-start(bf16[5,65,128]{2,1,0:T(8,128)(2,1)S(1)} %pad_maximum_fusion.2), channel_id=1, source_target_pairs={{0,16},{16,32},{32,48},{48,64},{64,80},{80,96},{96,112},{112,128},... | collective-permute-start | bytes 249608 | tf_op jit(solution)/shard_map/ppermute | solution.py:12
  211.7 12.2 %collective-permute-start.6 = (bf16[5,65,128]{2,1,0:T(8,128)(2,1)S(1)}, bf16[5,65,128]{2,1,0:T(8,128)(2,1)S(1)}, u32[]{:S(2)}, u32[]{:S(2)}) collective-permute-start(bf16[5,65,128]{2,1,0:T(8,128)(2,1)S(1)} %get-tuple-element.7), channel_id=1, source_target_pairs={{0,64},{16,80},{32,96},{48,112},{64,128},{80,144},{96,160},{112,17... | collective-permute-start | bytes 249608 | tf_op jit(solution)/shard_map/ppermute | solution.py:12
  213.8 16.5 %copy-start.7 = (f32[5,256]{1,0:T(8,128)S(1)}, f32[5,256]{1,0:T(8,128)}, u32[]{:S(2)}) copy-start(f32[5,256]{1,0:T(8,128)} %get-tuple-element.34) | copy-start | bytes 15364
  213.8 10.2 %collective-permute-start.7 = (bf16[5,65,128]{2,1,0:T(8,128)(2,1)S(1)}, bf16[5,65,128]{2,1,0:T(8,128)(2,1)S(1)}, u32[]{:S(2)}, u32[]{:S(2)}) collective-permute-start(bf16[5,65,128]{2,1,0:T(8,128)(2,1)S(1)} %get-tuple-element.7), channel_id=1, source_target_pairs={{0,128},{16,144},{32,160},{48,176},{64,192},{80,208},{96,224},{112... | collective-permute-start | bytes 249608 | tf_op jit(solution)/shard_map/ppermute | solution.py:12
  217.7 8.7 %collective-permute-start.8 = (bf16[5,65,128]{2,1,0:T(8,128)(2,1)S(1)}, bf16[5,65,128]{2,1,0:T(8,128)(2,1)S(1)}, u32[]{:S(2)}, u32[]{:S(2)}) collective-permute-start(bf16[5,65,128]{2,1,0:T(8,128)(2,1)S(1)} %get-tuple-element.7), channel_id=1, source_target_pairs={{0,192},{16,208},{32,224},{48,240},{64,256},{80,272},{96,288},{112... | collective-permute-start | bytes 249608 | tf_op jit(solution)/shard_map/ppermute | solution.py:12
  226.5 7.3 %collective-permute-start.9 = (bf16[5,65,128]{2,1,0:T(8,128)(2,1)S(1)}, bf16[5,65,128]{2,1,0:T(8,128)(2,1)S(1)}, u32[]{:S(2)}, u32[]{:S(2)}) collective-permute-start(bf16[5,65,128]{2,1,0:T(8,128)(2,1)S(1)} %get-tuple-element.5), channel_id=1, source_target_pairs={{0,256},{16,272},{32,288},{48,304},{64,320},{80,336},{96,352},{112... | collective-permute-start | bytes 249608 | tf_op jit(solution)/shard_map/ppermute | solution.py:12
  230.9 3.2 copy-start.6
  230.9 3.2 copy-start.17
  230.9 3.0 collective-permute-start.10
  232.4 1.7 collective-permute-start.11
  234.0 13.6 %copy-start.4 = (f32[5,64]{1,0:T(8,128)S(1)}, f32[5,64]{1,0:T(8,128)}, u32[]{:S(2)}) copy-start(f32[5,64]{1,0:T(8,128)} %param.24) | copy-start | bytes 3844
  234.5 13.0 %collective-permute-start.12 = (f32[256]{0:T(256)S(1)}, f32[256]{0:T(256)S(1)}, u32[]{:S(2)}, u32[]{:S(2)}) collective-permute-start(f32[256]{0:T(256)S(1)} %get-tuple-element.35), channel_id=1, source_target_pairs={{0,1},{1,0},{2,3},{3,2},{4,5},{5,4},{6,7},{7,6},{8,9},{9,8},{10,11... | collective-permute-start | bytes 3080 | tf_op jit(solution)/shard_map/ppermute | solution.py:179
Sparse Core Ops, SparseCore 0:
  25.4 150.2 reduce-scatter.1
